TPU v7x, 512 devices: a whole 4x8x8 slice. The times are simulated.
512 devices in a mesh: cache: 32 (over x_hi, z, core), dp: 16 (over y, x_lo).
Axes of the slice: x: 4 (x_hi: 2, x_lo: 2; x = x_hi * 2 + x_lo), y: 8, z: 8, core: 2. Of those that a mesh axis runs over, the one named last changes fastest.
Arguments:
- tokens: bfloat16 [4096, 2048], P('dp', 'cache'), may hold values from -6 to 6
- gate_values: bfloat16 [4096, 2048], P('dp', 'cache'), may hold values from -6 to 6
- output_grad: bfloat16 [4096, 2048], P('dp', 'cache'), may hold values from -12 to 12
- query_weight: bfloat16 [2048, 2048], P(None, 'cache'), may hold values from -6 to 6
- master: float32 [2048, 2048], P('dp', 'cache'), may hold values from -6 to 6
- moment: float32 [2048, 2048], P('dp', 'cache'), may hold values from -6 to 6
- second: float32 [2048, 2048], P('dp', 'cache'), may hold values from 0.5 to 2
- key_codes: bfloat16 [32, 8192, 2048], P('dp', 'cache'), may hold values from -30 to 30
- value_codes: bfloat16 [32, 8192, 2048], P('dp', 'cache'), may hold values from -6 to 6
- key_scales: float32 [32, 256, 16], P('dp', 'cache'), may hold values from 0.25 to 2
- value_scales: float32 [32, 256, 16], P('dp', 'cache'), may hold values from 0.25 to 2
- span_keys: bfloat16 [4096, 2048], P(('dp', 'cache')), may hold values from -6 to 6
- span_values: bfloat16 [4096, 2048], P(('dp', 'cache')), may hold values from -6 to 6
- lengths: int32 [32], P('dp'), may hold values from 1 to 8192, 131072 in all
- segments: int32 [16, 256], P('dp'), may hold values from 0 to 1, never falling along the last dimension, each value on 1 to 192 neighbouring positions
Outputs:
- layer_output: bfloat16 [4096, 2048], P('dp', 'cache')
- new_weight: bfloat16 [2048, 2048], P(None, 'cache')
- new_master: float32 [2048, 2048], P('dp', 'cache')
- new_moment: float32 [2048, 2048], P('dp', 'cache')
- new_second: float32 [2048, 2048], P('dp', 'cache')
Inputs may be any that keep to these rules, and one draw needn't show every extreme that they name: `segments`: in every row the ids never fall, every one of the 2 ids appears, each on at most three quarters of the 256 events. The lengths sum to 32 * 4096 and the largest is exactly 8192.
All inputs are finite; a program needn't handle non-finite values. No bound on the sum of `lengths` on one device may be relied on, other than what follows from the above.
Results may differ from a plain program's by a relative error of at most 0.0058.
The roundings to bfloat16 on the way count: a program that leaves them out, or rounds other values in their place, can miss the bound.
Values may be sent and summed in bfloat16 or wider, within the bound.
No kernel may reach another device: no remote copies, remote signals or barrier semaphores. Data moves between devices by JAX's collectives and lax.ppermute only.
A program may use at most 128 MiB of HBM per device.

v0:
```python
import math

import jax
import jax.numpy as jnp
from jax import lax
from jax.sharding import Mesh
from jax.sharding import PartitionSpec as P

HEADS = 16
STEP = 20
CACHE = ("cache_0", "cache_1", "cache_2")
DP = ("dp_0", "dp_1")
CACHE_DP = ("cache_0", "cache_1", "cache_2", "dp_0", "dp_1")
DP_CACHE = ("dp_0", "dp_1", "cache_0", "cache_1", "cache_2")


def split_up(array, dim, peers):
    dims = array.shape
    tiles = array.reshape(*dims[:dim], peers, dims[dim] // peers, *dims[dim + 1 :])
    return jnp.moveaxis(tiles, dim, 0)


def summed_on_arrival(array, axis, dim):
    tiles = split_up(array, dim, lax.axis_size(axis))
    arrived = lax.all_to_all(tiles, axis, split_axis=0, concat_axis=0, tiled=True)
    return arrived.sum(axis=0)


def sent_to_all(array, axis):
    copies = jnp.broadcast_to(array, (lax.axis_size(axis), *array.shape))
    return lax.all_to_all(copies, axis, split_axis=0, concat_axis=0, tiled=True)


def of_everyone(array, axis):
    everything = sent_to_all(array, axis)
    return jnp.sum(everything, axis=0)


def packed_total(arrays, axis):
    flat, at, outs = (jnp.concatenate([a.reshape(-1) for a in arrays]), 0, [])
    subtotal = of_everyone(flat, axis)
    for a in arrays:
        outs.append(subtotal[at : at + a.size].reshape(a.shape))
        at += a.size
    return tuple(outs)


def in_order(tiles, dim):
    dims = list(tiles.shape[1:])
    dims[dim] *= tiles.shape[0]
    return jnp.moveaxis(tiles, 0, dim).reshape(dims)


def collect(array, axis, dim):
    tiles = sent_to_all(array, axis)
    return in_order(tiles, dim)


def sent_and_summed(array, axis, dim):
    peers = lax.axis_size(axis)
    tiles = lax.all_to_all(split_up(array, dim, peers), axis, 0, 0, tiled=True)
    return jnp.sum(tiles.astype(jnp.float32), axis=0)


def by_axis(array, axes):
    for axis in axes:
        array = lax.psum(array, axis)
    return array


def silu_slope(values):
    sigmoid_value = jax.nn.sigmoid(values)
    return sigmoid_value * (1.0 + values * (1.0 - sigmoid_value))


def product(form, left, right):
    return jnp.einsum(form, left, right, preferred_element_type=jnp.float32)


def dequantize(stored, scales):
    user_count, row_count, model_width = stored.shape
    block_count, head_count = (scales.shape[1], scales.shape[2])
    shaped = stored.astype(jnp.float32).reshape(
        user_count, block_count, row_count // block_count, head_count, model_width // head_count
    )
    scaled = shaped * scales[:, :, None, :, None]
    return scaled.astype(jnp.bfloat16).reshape(user_count * row_count, model_width)


def key_mask(user_ids, lengths, shard_index, hist_rows, span_rows):
    query_count = user_ids.shape[0]
    user_count = lengths.shape[0]
    key_index = jnp.arange(user_count * hist_rows, dtype=jnp.int32)
    key_user = key_index // hist_rows
    key_row = shard_index * hist_rows + key_index % hist_rows
    user_range = jnp.arange(user_count, dtype=jnp.int32)
    key_limit = jnp.sum(
        jnp.where(key_user[:, None] == user_range[None, :], lengths[None, :], 0), axis=1
    )
    history_mask = (user_ids[:, None] == key_user[None, :]) & (key_row < key_limit)[None, :]
    span_start = shard_index * span_rows
    span_pos = span_start + jnp.arange(span_rows, dtype=jnp.int32)
    span_users = lax.dynamic_slice_in_dim(user_ids, span_start, span_rows, 0)
    query_pos = jnp.arange(query_count, dtype=jnp.int32)
    span_mask = (user_ids[:, None] == span_users[None, :]) & (
        span_pos[None, :] <= query_pos[:, None]
    )
    return jnp.concatenate([history_mask, span_mask], axis=1)


def split_heads(matrix, head_count):
    return matrix.reshape(matrix.shape[0], head_count, matrix.shape[1] // head_count)


def forward_part(queries, keys, values_all, mask, head_count):
    head_size = queries.shape[1] // head_count
    scores = product(
        "qhd,khd->hqk", split_heads(queries, head_count), split_heads(keys, head_count)
    ) / math.sqrt(head_size)
    attn = jnp.where(mask[None], jax.nn.silu(scores), 0.0).astype(jnp.bfloat16)
    mixed = product("hqk,khd->qhd", attn, split_heads(values_all, head_count))
    weighted_slope = jnp.where(mask[None], silu_slope(scores), 0.0) / math.sqrt(head_size)
    return (mixed.reshape(queries.shape[0], queries.shape[1]), weighted_slope)


def backward_part(keys, values_all, weighted_slope, mixed_grad, head_count):
    attn_grad = product(
        "qhd,khd->hqk", split_heads(mixed_grad, head_count), split_heads(values_all, head_count)
    )
    score_grad = (attn_grad * weighted_slope).astype(jnp.bfloat16)
    query_grad = product("hqk,khd->qhd", score_grad, split_heads(keys, head_count))
    return query_grad.reshape(mixed_grad.shape[0], mixed_grad.shape[1])


def shards(
    tokens,
    gate_values,
    output_grad,
    query_weight,
    master,
    moment,
    second,
    key_codes,
    value_codes,
    key_scales,
    value_scales,
    span_keys,
    span_values,
    lengths,
    segments,
):
    model_width = query_weight.shape[0]
    shard_index = lax.axis_index(CACHE)
    features = lax.all_gather(tokens, CACHE, axis=1, tiled=True)
    query_pre = jnp.dot(features, query_weight, preferred_element_type=jnp.float32) / math.sqrt(
        model_width
    )
    query_block = jax.nn.silu(query_pre).astype(jnp.bfloat16)
    queries = lax.all_gather(query_block, CACHE, axis=1, tiled=True)
    user_ids = segments[0]
    hist_rows = key_codes.shape[1]
    span_rows = span_keys.shape[0]
    keys = jnp.concatenate([dequantize(key_codes, key_scales), span_keys], axis=0)
    values_all = jnp.concatenate([dequantize(value_codes, value_scales), span_values], axis=0)
    mask = key_mask(user_ids, lengths, shard_index, hist_rows, span_rows)
    mixed_part, weighted_slope = forward_part(queries, keys, values_all, mask, HEADS)
    gate_float = gate_values.astype(jnp.float32)
    mixed_block = summed_on_arrival(mixed_part, CACHE, 1)
    row_sum, row_square = packed_total(
        (jnp.sum(mixed_block, axis=1), jnp.sum(mixed_block * mixed_block, axis=1)), CACHE
    )
    row_mean = (row_sum / model_width)[:, None]
    row_var = (row_square / model_width)[:, None] - row_mean * row_mean
    inverse = 1.0 / jnp.sqrt(row_var + 1e-05)
    normed = (mixed_block - row_mean) * inverse
    layer_block = (gate_float * normed).astype(jnp.bfloat16)
    back = output_grad.astype(jnp.float32) * gate_float
    back_sum, back_cross = packed_total(
        (jnp.sum(back, axis=1), jnp.sum(back * normed, axis=1)), CACHE
    )
    grad_block = inverse * (
        back - (back_sum / model_width)[:, None] - normed * (back_cross / model_width)[:, None]
    )
    mixed_grad = collect(grad_block.astype(jnp.bfloat16), CACHE, 1)
    query_part = backward_part(keys, values_all, weighted_slope, mixed_grad, HEADS)
    query_grad = sent_and_summed(query_part.astype(jnp.bfloat16), CACHE, 1)
    pre_grad = (query_grad * silu_slope(query_pre)).astype(jnp.bfloat16)
    weight_part = lax.dot_general(
        features, pre_grad, (((0,), (0,)), ((), ())), preferred_element_type=jnp.float32
    ) / math.sqrt(model_width)
    grad_owned = sent_and_summed(weight_part.astype(jnp.bfloat16), DP, 0)
    square_total = by_axis(jnp.sum(grad_owned * grad_owned), CACHE_DP)
    grad_level = jnp.sqrt(square_total / (model_width * model_width))
    clip_factor = jnp.minimum(1.0, 0.5 / (grad_level + 1e-06))
    clipped = clip_factor * grad_owned
    new_moment = 0.9 * moment + 0.1 * clipped
    new_second = 0.95 * second + 0.05 * clipped * clipped
    first_fix = new_moment / (1.0 - 0.9**STEP)
    second_fix = new_second / (1.0 - 0.95**STEP)
    new_master = master - 0.01 * (first_fix / (jnp.sqrt(second_fix) + 1e-08) + 0.1 * master)
    new_weight = lax.all_gather(new_master.astype(jnp.bfloat16), DP, axis=0, tiled=True)
    return (layer_block, new_weight, new_master, new_moment, new_second)


def solution(mesh):
    torus = Mesh(
        mesh.devices.reshape(2, 8, 2, 8, 2), ("cache_0", "cache_1", "cache_2", "dp_0", "dp_1")
    )
    placed = (
        P(DP, CACHE),
        P(DP, CACHE),
        P(DP, CACHE),
        P(None, CACHE),
        P(DP, CACHE),
        P(DP, CACHE),
        P(DP, CACHE),
        P(DP, CACHE, None),
        P(DP, CACHE, None),
        P(DP, CACHE, None),
        P(DP, CACHE, None),
        P(DP_CACHE, None),
        P(DP_CACHE, None),
        P(DP),
        P(DP, None),
    )
    return jax.shard_map(
        shards,
        mesh=torus,
        in_specs=placed,
        out_specs=(P(DP, CACHE), P(None, CACHE), P(DP, CACHE), P(DP, CACHE), P(DP, CACHE)),
        check_vma=False,
    )
```

profile of v0, /device:TPU:2, one launch (start us, length us, event | category | flops | bytes accessed | tf_op | source)
XLA Modules:
  0.0 461.2 jit_solution(14215436737967602290)
XLA Ops:
  8.0 90.7 %all-gather.3.cloned.1.call-done = bf16[256,2048]{0,1:T(8,128)(2,1)} async-done(((bf16[256,64]{0,1:T(8,128)(2,1)}), bf16[256,2048]{0,1:T(8,128)(2,1)}) %all-gather.3.cloned.1.call-update) | async-done | bytes 1048592 | tf_op jit(solution)/shard_map/all_gather | solution.py:154
  98.6 2.2 multiply_convert_fusion.6
  100.8 0.8 copy.45
  101.6 0.8 copy.43
  102.8 4.1 copy.62
  106.9 2.6 copy.61
  110.0 8.2 %fusion.2 = (bf16[512,16,128]{2,0,1:T(8,128)(2,1)S(1)}, bf16[512,16,128]{2,0,1:T(8,128)(2,1)}) fusion(f32[512,16,128]{2,1,0:T(8,128)} %bitcast.46, f32[512,16]{0,1:T(8,128)S(1)} %mul.156, f32[512,16]{0,1:T(8,128)S(1)} %mul.147, f32[512,16,128]{2,1,0:T(8,128)} %bitcast.47), kind=kLoop, calls=%fused_computation.6 | loop fusion | flops 4194304 | bytes 12648448 | tf_op jit(solution)/shard_map/convert_element_type | solution.py:87
  118.2 64.5 %all-gather.5.cloned.1.call-done = bf16[256,2048]{0,1:T(8,128)(2,1)} async-done(((bf16[256,64]{0,1:T(8,128)(2,1)}), bf16[256,2048]{0,1:T(8,128)(2,1)}) %all-gather.5.cloned.1.call-update) | async-done | bytes 1048592 | tf_op jit(solution)/shard_map/all_gather | solution.py:159
  182.8 2.6 fusion.8
  185.4 3.2 fusion
  188.7 57.7 %all_to_all.32 = f32[32,256,64]{1,2,0:T(8,128)S(1)} all-to-all(f32[32,256,64]{1,2,0:T(8,128)S(1)} %bitcast.50), channel_id=1, replica_groups=mesh['cache_0'=2,'cache_1'=8,'cache_2'=2,'dp_0'=8,'dp_1'=2] {'cache_0','..., dimensions={0} | all-to-all | bytes 4194304 | tf_op jit(solution)/shard_map/all_to_all | solution.py:25
  246.8 14.5 %all_to_all.33 = f32[32,1,512]{2,1,0:T(1,128)S(1)} all-to-all(f32[32,1,512]{2,1,0:T(1,128)S(1)} %broadcast_in_dim.57), channel_id=1, replica_groups=mesh['cache_0'=2,'cache_1'=8,'cache_2'=2,'dp_0'=8,'dp_1'=2] {'cache_0','..., dimensions={0} | all-to-all | bytes 131072 | tf_op jit(solution)/shard_map/all_to_all | solution.py:31
  261.5 13.5 %all_to_all.34 = f32[32,1,512]{2,1,0:T(1,128)S(1)} all-to-all(f32[32,1,512]{2,1,0:T(1,128)S(1)} %broadcast_in_dim.58), channel_id=1, replica_groups=mesh['cache_0'=2,'cache_1'=8,'cache_2'=2,'dp_0'=8,'dp_1'=2] {'cache_0','..., dimensions={0} | all-to-all | bytes 131072 | tf_op jit(solution)/shard_map/all_to_all | solution.py:31
  275.8 33.5 %all_to_all.35 = bf16[32,256,64]{1,2,0:T(8,128)(2,1)} all-to-all(bf16[32,256,64]{1,2,0:T(8,128)(2,1)S(1)} %broadcast_in_dim.59), channel_id=1, replica_groups=mesh['cache_0'=2,'cache_1'=8,'cache_2'=2,'dp_0'=8,'dp_1'=2] {'cache_0','..., dimensions={0} | all-to-all | bytes 2097152 | tf_op jit(solution)/shard_map/all_to_all | solution.py:31
  309.4 8.9 %fusion.7 = bf16[16,128,256]{2,1,0:T(8,128)(2,1)} fusion(f32[16,256,520]{1,2,0:T(8,128)} %copy-done.1, pred[256,520]{0,1:T(8,128)(4,1)} %copy-done.5, bf16[256,16,128]{0,2,1:T(8,128)(2,1)} %bitcast.52, bf16[8,16,128]{2,0,1:T(8,128)(2,1)S(1)} %bitcast.56, bf16[512,16,128]{2,0,1:T(8,128)(2,1)S(1)} %get-tuple-element.21, bf16[8,16,128]{2,0,1:T(8,128)(2,1)S(1)} %bitcast.60, ...), kind=kOutput, calls=%fused_computation.15 | convolution fusion | flops 1125122048 | bytes 15009792 | tf_op jit(solution)/shard_map/hqk,khd->qhd/dot_general | solution.py:77
  318.3 34.1 %all_to_all.36 = bf16[32,256,64]{1,2,0:T(8,128)(2,1)S(1)} all-to-all(bf16[32,256,64]{1,2,0:T(8,128)(2,1)} %bitcast.53), channel_id=1, replica_groups=mesh['cache_0'=2,'cache_1'=8,'cache_2'=2,'dp_0'=8,'dp_1'=2] {'cache_0','..., dimensions={0} | all-to-all | bytes 2097152 | tf_op jit(solution)/shard_map/all_to_all | solution.py:61
  353.1 17.4 %all_to_all.37 = bf16[16,128,64]{1,2,0:T(8,128)(2,1)S(1)} all-to-all(bf16[16,128,64]{1,2,0:T(8,128)(2,1)S(1)} %bitcast.54), channel_id=1, replica_groups=mesh['cache_0'=2,'cache_1'=8,'cache_2'=2,'dp_0'=8,'dp_1'=2] {'dp_0','dp_1'}, dimensions={0} | all-to-all | bytes 524288 | tf_op jit(solution)/shard_map/all_to_all | solution.py:61
  371.1 7.1 %psum.35 = f32[]{:T(128)} all-reduce(f32[]{:T(128)} %multiply_reduce_fusion.2), channel_id=1, replica_groups=mesh['cache_0'=2,'cache_1'=8,'cache_2'=2,'dp_0'=8,'dp_1'=2] {'cache_0'}, use_global_device_ids=true, to_apply=%region_11.12 | all-reduce | flops 1 | bytes 8 | tf_op jit(solution)/shard_map/psum | solution.py:67
  378.2 17.8 %psum.36 = f32[]{:T(128)} all-reduce(f32[]{:T(128)} %psum.35), channel_id=1, replica_groups=mesh['cache_0'=2,'cache_1'=8,'cache_2'=2,'dp_0'=8,'dp_1'=2] {'cache_1'}, use_global_device_ids=true, to_apply=%region_12.13 | all-reduce | flops 1 | bytes 8 | tf_op jit(solution)/shard_map/psum | solution.py:67
  395.9 3.1 psum.37
  399.0 15.2 %psum.38 = f32[]{:T(128)} all-reduce(f32[]{:T(128)} %psum.37), channel_id=1, replica_groups=mesh['cache_0'=2,'cache_1'=8,'cache_2'=2,'dp_0'=8,'dp_1'=2] {'dp_0'}, use_global_device_ids=true, to_apply=%region_14.15 | all-reduce | flops 1 | bytes 8 | tf_op jit(solution)/shard_map/psum | solution.py:67
  414.2 5.6 %psum.39 = f32[]{:T(128)} all-reduce(f32[]{:T(128)} %psum.38), channel_id=1, replica_groups=mesh['cache_0'=2,'cache_1'=8,'cache_2'=2,'dp_0'=8,'dp_1'=2] {'dp_1'}, use_global_device_ids=true, to_apply=%region_15.16 | all-reduce | flops 1 | bytes 8 | tf_op jit(solution)/shard_map/psum | solution.py:67
  421.1 32.5 %all_gather.11 = bf16[2048,64]{0,1:T(8,128)(2,1)S(1)} all-gather(bf16[128,64]{0,1:T(8,128)(2,1)S(1)} %get-tuple-element.9), channel_id=1, replica_groups=mesh['cache_0'=2,'cache_1'=8,'cache_2'=2,'dp_0'=8,'dp_1'=2] {'dp_0','dp_1'}, dimensions={0}, use_global_device_ids=true | all-gather | bytes 278528 | tf_op jit(solution)/shard_map/all_gather | solution.py:201
  453.7 0.7 copy.72
  (65 shorter events, 5.0 us)
Async XLA Ops:
  7.2 91.5 %copy-start = (bf16[2048,64]{0,1:T(8,128)(2,1)S(1)}, bf16[2048,64]{0,1:T(8,128)(2,1)}, u32[]{:S(2)}) copy-start(bf16[2048,64]{0,1:T(8,128)(2,1)} %param.18) | copy-start | bytes 786436
  7.2 91.5 %all-gather.3.cloned.1.call-start = ((), (), s32[]{:S(2)}) async-start(), calls=%async_computation.6 | async-start | bytes 1081344 | tf_op jit(solution)/shard_map/all_gather | solution.py:154
  7.9 99.0 %copy-start.3 = (bf16[2,256,2048]{2,1,0:T(8,128)(2,1)S(1)}, bf16[2,256,2048]{2,1,0:T(8,128)(2,1)}, u32[]{:S(2)}) copy-start(bf16[2,256,2048]{2,1,0:T(8,128)(2,1)} %param.23) | copy-start | bytes 6291460
  7.9 174.8 %all-gather.5.cloned.1.call-start = ((), (), s32[]{:S(2)}) async-start(), calls=%async_computation.7 | async-start | bytes 1081344 | tf_op jit(solution)/shard_map/all_gather | solution.py:159
  106.9 2.6 copy-start.12
  106.9 2.6 copy-start.13
  110.0 75.4 %copy-start.5 = (pred[256,520]{0,1:T(8,128)(4,1)}, pred[256,520]{0,1:T(8,128)(4,1)S(1)}, u32[]{:S(2)}) copy-start(pred[256,520]{0,1:T(8,128)(4,1)S(1)} %pad_add_fusion) | copy-start | bytes 399364
  110.0 72.8 %copy-start.8 = (bf16[8,2048]{1,0:T(8,128)(2,1)S(1)}, bf16[8,2048]{1,0:T(8,128)(2,1)}, u32[]{:S(2)}) copy-start(bf16[8,2048]{1,0:T(8,128)(2,1)} %param.26) | copy-start | bytes 98308
  182.8 2.7 copy-start.4
  182.8 2.7 copy-start.14
  185.4 3.3 copy-start.1
  188.7 72.7 %copy-start.6 = (bf16[256,64]{0,1:T(8,128)(2,1)S(1)}, bf16[256,64]{0,1:T(8,128)(2,1)}, u32[]{:S(2)}) copy-start(bf16[256,64]{0,1:T(8,128)(2,1)} %param.16) | copy-start | bytes 98308
  188.7 72.7 %copy-start.7 = (bf16[256,64]{0,1:T(8,128)(2,1)S(1)}, bf16[256,64]{0,1:T(8,128)(2,1)}, u32[]{:S(2)}) copy-start(bf16[256,64]{0,1:T(8,128)(2,1)} %param.17) | copy-start | bytes 98308
  309.4 43.2 %copy-start.2 = (bf16[256,2048]{0,1:T(8,128)(2,1)S(1)}, bf16[256,2048]{0,1:T(8,128)(2,1)}, u32[]{:S(2)}) copy-start(bf16[256,2048]{0,1:T(8,128)(2,1)} %all-gather.3.cloned.1.call-done) | copy-start | bytes 3145732
  318.3 102.2 %copy-start.9 = (f32[128,64]{0,1:T(8,128)S(1)}, f32[128,64]{0,1:T(8,128)}, u32[]{:S(2)}) copy-start(f32[128,64]{0,1:T(8,128)} %param.19) | copy-start | bytes 98308
  318.3 102.2 %copy-start.10 = (f32[128,64]{0,1:T(8,128)S(1)}, f32[128,64]{0,1:T(8,128)}, u32[]{:S(2)}) copy-start(f32[128,64]{0,1:T(8,128)} %param.20) | copy-start | bytes 98308
  318.3 102.2 %copy-start.11 = (f32[128,64]{0,1:T(8,128)S(1)}, f32[128,64]{0,1:T(8,128)}, u32[]{:S(2)}) copy-start(f32[128,64]{0,1:T(8,128)} %param.21) | copy-start | bytes 98308
Sparse Core Ops, SparseCore 0:
  11.4 87.2 all-gather.2
  102.6 80.1 all-gather.4
where the time goes:
time: 462 us; the launch traced here: 461 us
  blocking collectives  252 us (55%)
  waiting for transfers between devices  156 us (34%)
  matrix products  17.4 us (4%)
  between operations  15 us (3%)
  other arithmetic  11.3 us (2%)
  local copies, waits for them, and re-layouts  9.72 us (2%)
    all_gather x1, waiting for transfers between devices, shards(): features = lax.all_gather(tokens, CACHE, axis=1, tiled=True)  90.7 us
    all_gather x1, waiting for transfers between devices, shards(): queries = lax.all_gather(query_block, CACHE, axis=1, tiled=True)  64.5 us
    all_to_all x3, blocking collectives, sent_to_all(): return lax.all_to_all(copies, axis, split_axis=0, concat_axis=0, tiled=True)  61.5 us
    all_to_all x1, blocking collectives, summed_on_arrival(): lax.all_to_all(tiles, axis, split_axis=0, concat_axis=0, tiled=True)  57.7 us
    all_to_all x2, blocking collectives, sent_and_summed(): tiles = lax.all_to_all(split_up(array, dim, peers), axis, 0, 0, tiled=True)  51.5 us
    psum x5, blocking collectives, by_axis(): array = lax.psum(array, axis)  48.6 us
    all_gather x1, blocking collectives, shards(): lax.all_gather(new_master.astype(jnp.bfloat16), DP, axis=0, tiled=True)  32.5 us
    dot_general x3, matrix products, product(): return jnp.einsum(form, left, right, preferred_element_type=jnp.float32)  14.8 us
  transfers between devices with their start and end apart: 2, of which 2 were waited for; matrix products, arithmetic and copies ran while one was open for 4% of the time, Pallas kernels for 0%

commit v1 on v0

--- a/solution.py
+++ b/solution.py
@@ -151,12 +151,12 @@
 ):
     model_width = query_weight.shape[0]
     shard_index = lax.axis_index(CACHE)
-    features = lax.all_gather(tokens, CACHE, axis=1, tiled=True)
+    features = collect(tokens, CACHE, 1)
     query_pre = jnp.dot(features, query_weight, preferred_element_type=jnp.float32) / math.sqrt(
         model_width
     )
     query_block = jax.nn.silu(query_pre).astype(jnp.bfloat16)
-    queries = lax.all_gather(query_block, CACHE, axis=1, tiled=True)
+    queries = collect(query_block, CACHE, 1)
     user_ids = segments[0]
     hist_rows = key_codes.shape[1]
     span_rows = span_keys.shape[0]
@@ -166,18 +166,22 @@
     mixed_part, weighted_slope = forward_part(queries, keys, values_all, mask, HEADS)
     gate_float = gate_values.astype(jnp.float32)
     mixed_block = summed_on_arrival(mixed_part, CACHE, 1)
-    row_sum, row_square = packed_total(
-        (jnp.sum(mixed_block, axis=1), jnp.sum(mixed_block * mixed_block, axis=1)), CACHE
+    back = output_grad.astype(jnp.float32) * gate_float
+    row_sum, row_square, back_sum, back_mixed = packed_total(
+        (
+            jnp.sum(mixed_block, axis=1),
+            jnp.sum(mixed_block * mixed_block, axis=1),
+            jnp.sum(back, axis=1),
+            jnp.sum(back * mixed_block, axis=1),
+        ),
+        CACHE,
     )
     row_mean = (row_sum / model_width)[:, None]
     row_var = (row_square / model_width)[:, None] - row_mean * row_mean
     inverse = 1.0 / jnp.sqrt(row_var + 1e-05)
     normed = (mixed_block - row_mean) * inverse
     layer_block = (gate_float * normed).astype(jnp.bfloat16)
-    back = output_grad.astype(jnp.float32) * gate_float
-    back_sum, back_cross = packed_total(
-        (jnp.sum(back, axis=1), jnp.sum(back * normed, axis=1)), CACHE
-    )
+    back_cross = inverse[:, 0] * (back_mixed - row_mean[:, 0] * back_sum)
     grad_block = inverse * (
         back - (back_sum / model_width)[:, None] - normed * (back_cross / model_width)[:, None]
     )
@@ -189,7 +193,7 @@
         features, pre_grad, (((0,), (0,)), ((), ())), preferred_element_type=jnp.float32
     ) / math.sqrt(model_width)
     grad_owned = sent_and_summed(weight_part.astype(jnp.bfloat16), DP, 0)
-    square_total = by_axis(jnp.sum(grad_owned * grad_owned), CACHE_DP)
+    square_total = of_everyone(jnp.sum(grad_owned * grad_owned).reshape(1), CACHE_DP)[0]
     grad_level = jnp.sqrt(square_total / (model_width * model_width))
     clip_factor = jnp.minimum(1.0, 0.5 / (grad_level + 1e-06))
     clipped = clip_factor * grad_owned
@@ -198,7 +202,7 @@
     first_fix = new_moment / (1.0 - 0.9**STEP)
     second_fix = new_second / (1.0 - 0.95**STEP)
     new_master = master - 0.01 * (first_fix / (jnp.sqrt(second_fix) + 1e-08) + 0.1 * master)
-    new_weight = lax.all_gather(new_master.astype(jnp.bfloat16), DP, axis=0, tiled=True)
+    new_weight = collect(new_master.astype(jnp.bfloat16), DP, 0)
     return (layer_block, new_weight, new_master, new_moment, new_second)
 
 

time: 462 us -> 304 us (0.66)
  the two profiles are of different devices: /device:TPU:2 before, /device:TPU:1 now
where the time goes in v1:
time: 304 us; the launch traced here: 302 us
  blocking collectives  240 us (79%)
  matrix products  17.8 us (6%)
  other arithmetic  13.3 us (4%)
  local copies, waits for them, and re-layouts  12.3 us (4%)
  waiting for transfers between devices  10.9 us (4%)
  starting transfers between devices  6.61 us (2%)
    all_to_all x5, blocking collectives, sent_to_all(): return lax.all_to_all(copies, axis, split_axis=0, concat_axis=0, tiled=True)  133 us
    all_to_all x1, blocking collectives, summed_on_arrival(): lax.all_to_all(tiles, axis, split_axis=0, concat_axis=0, tiled=True)  56.2 us
    all_to_all x2, blocking collectives, sent_and_summed(): tiles = lax.all_to_all(split_up(array, dim, peers), axis, 0, 0, tiled=True)  50.4 us
    dot_general x3, matrix products, product(): return jnp.einsum(form, left, right, preferred_element_type=jnp.float32)  16.4 us
    all_to_all x1, waiting for transfers between devices, sent_to_all(): return lax.all_to_all(copies, axis, split_axis=0, concat_axis=0, tiled=True)  10.9 us
    convert_element_type x1, other arithmetic, dequantize(): scaled.astype(jnp.bfloat16).reshape(user_count * row_count, model_width)  8.3 us
    all_to_all x1, starting transfers between devices, sent_to_all(): return lax.all_to_all(copies, axis, split_axis=0, concat_axis=0, tiled=True)  6.61 us
  transfers between devices with their start and end apart: 1, of which 1 were waited for; matrix products, arithmetic and copies ran while one was open for 6% of the time, Pallas kernels for 0%

profile of v1, /device:TPU:1, one launch (start us, length us, event | category | flops | bytes accessed | tf_op | source)
XLA Modules:
  0.0 302.1 jit_solution(8849943152026773080)
XLA Ops:
  0.7 1.0 broadcast_in_dim.65
  1.7 42.0 %all_to_all.47 = bf16[32,256,64]{1,2,0:T(8,128)(2,1)S(1)} all-to-all(bf16[32,256,64]{1,2,0:T(8,128)(2,1)S(1)} %broadcast_in_dim.65), channel_id=1, replica_groups=mesh['cache_0'=2,'cache_1'=8,'cache_2'=2,'dp_0'=8,'dp_1'=2] {'cache_0','..., dimensions={0} | all-to-all | bytes 2097152 | tf_op jit(solution)/shard_map/all_to_all | solution.py:31
  43.7 0.9 multiply_convert_fusion.6
  44.6 1.1 broadcast_in_dim.66
  45.7 6.6 %all-to-all-start.1 = ((bf16[32,256,64]{1,2,0:T(8,128)(2,1)}), bf16[32,256,64]{1,2,0:T(8,128)(2,1)}, u32[]{:S(2)}, u32[]{:S(2)}) async-start(bf16[32,256,64]{1,2,0:T(8,128)(2,1)} %broadcast_in_dim.66), calls=%async_computation.1 | async-start | bytes 2097152 | tf_op jit(solution)/shard_map/all_to_all | solution.py:31
  53.1 0.8 mul.152
  55.5 2.5 copy.74
  58.0 2.6 copy.73
  61.1 8.3 %fusion.2 = (bf16[512,16,128]{2,0,1:T(8,128)(2,1)S(1)}, bf16[512,16,128]{2,0,1:T(8,128)(2,1)}) fusion(f32[512,16,128]{2,1,0:T(8,128)} %bitcast.56, f32[512,16]{0,1:T(8,128)} %mul.162, f32[512,16]{0,1:T(8,128)} %mul.153, f32[512,16,128]{2,1,0:T(8,128)} %bitcast.57), kind=kLoop, calls=%fused_computation.6 | loop fusion | flops 4194304 | bytes 12648448 | tf_op jit(solution)/shard_map/convert_element_type | solution.py:87
  69.4 10.9 %all-to-all-done.1 = bf16[32,256,64]{1,2,0:T(8,128)(2,1)} async-done(((bf16[32,256,64]{1,2,0:T(8,128)(2,1)}), bf16[32,256,64]{1,2,0:T(8,128)(2,1)}, u32[]{:S(2)}, u32[]{:S(2)}) %all-to-all-start.1) | async-done | bytes 1048608 | tf_op jit(solution)/shard_map/all_to_all | solution.py:31
  80.3 2.6 fusion.8
  82.9 3.2 %fusion = f32[16,128,256]{2,1,0:T(8,128)S(1)} fusion(f32[16,256,520]{1,2,0:T(8,128)S(1)} %fusion.8, pred[256,520]{0,1:T(8,128)(4,1)S(1)} %pad_add_fusion, bf16[8,16,128]{2,0,1:T(8,128)(2,1)S(1)} %bitcast.71, bf16[512,16,128]{2,0,1:T(8,128)(2,1)S(1)} %copy-done.4), kind=kOutput, calls=%fused_computation.3 | convolution fusion | flops 564428800 | bytes 12879872 | tf_op jit(solution)/shard_map/hqk,khd->qhd/dot_general | solution.py:77
  86.2 56.2 %all_to_all.48 = f32[32,256,64]{1,2,0:T(8,128)S(1)} all-to-all(f32[32,256,64]{1,2,0:T(8,128)S(1)} %bitcast.62), channel_id=1, replica_groups=mesh['cache_0'=2,'cache_1'=8,'cache_2'=2,'dp_0'=8,'dp_1'=2] {'cache_0','..., dimensions={0} | all-to-all | bytes 4194304 | tf_op jit(solution)/shard_map/all_to_all | solution.py:25
  142.9 16.7 %all_to_all.49 = f32[32,1,1024]{2,1,0:T(1,128)} all-to-all(f32[32,1,1024]{2,1,0:T(1,128)S(1)} %broadcast_in_dim.68), channel_id=1, replica_groups=mesh['cache_0'=2,'cache_1'=8,'cache_2'=2,'dp_0'=8,'dp_1'=2] {'cache_0','..., dimensions={0} | all-to-all | bytes 262144 | tf_op jit(solution)/shard_map/all_to_all | solution.py:31
  159.6 1.0 reduce_sum.105
  161.3 32.8 %all_to_all.50 = bf16[32,256,64]{1,2,0:T(8,128)(2,1)} all-to-all(bf16[32,256,64]{1,2,0:T(8,128)(2,1)S(1)} %broadcast_in_dim.69), channel_id=1, replica_groups=mesh['cache_0'=2,'cache_1'=8,'cache_2'=2,'dp_0'=8,'dp_1'=2] {'cache_0','..., dimensions={0} | all-to-all | bytes 2097152 | tf_op jit(solution)/shard_map/all_to_all | solution.py:31
  194.2 10.5 %fusion.7 = bf16[16,128,256]{2,1,0:T(8,128)(2,1)} fusion(f32[16,256,520]{1,2,0:T(8,128)} %copy-done.1, pred[256,520]{0,1:T(8,128)(4,1)} %copy-done.6, bf16[256,16,128]{0,2,1:T(8,128)(2,1)} %bitcast.63, bf16[8,16,128]{2,0,1:T(8,128)(2,1)} %bitcast.67, bf16[512,16,128]{2,0,1:T(8,128)(2,1)S(1)} %get-tuple-element.22, bf16[8,16,128]{2,0,1:T(8,128)(2,1)} %bitcast.70, ...), kind=kOutput, calls=%fused_computation.15 | convolution fusion | flops 1125122048 | bytes 15009792 | tf_op jit(solution)/shard_map/hqk,khd->qhd/dot_general | solution.py:77
  204.7 34.1 %all_to_all.51 = bf16[32,256,64]{1,2,0:T(8,128)(2,1)S(1)} all-to-all(bf16[32,256,64]{1,2,0:T(8,128)(2,1)} %bitcast.64), channel_id=1, replica_groups=mesh['cache_0'=2,'cache_1'=8,'cache_2'=2,'dp_0'=8,'dp_1'=2] {'cache_0','..., dimensions={0} | all-to-all | bytes 2097152 | tf_op jit(solution)/shard_map/all_to_all | solution.py:61
  239.4 16.4 %all_to_all.52 = bf16[16,128,64]{1,2,0:T(8,128)(2,1)S(1)} all-to-all(bf16[16,128,64]{1,2,0:T(8,128)(2,1)S(1)} %bitcast.65), channel_id=1, replica_groups=mesh['cache_0'=2,'cache_1'=8,'cache_2'=2,'dp_0'=8,'dp_1'=2] {'dp_0','dp_1'}, dimensions={0} | all-to-all | bytes 524288 | tf_op jit(solution)/shard_map/all_to_all | solution.py:61
  256.5 0.8 broadcast_in_dim.70
  257.3 29.0 %all_to_all.53 = f32[512,1,1]{2,1,0:T(1,128)S(1)} all-to-all(f32[512,1,1]{2,1,0:T(1,128)S(1)} %broadcast_in_dim.70), channel_id=1, replica_groups=mesh['cache_0'=2,'cache_1'=8,'cache_2'=2,'dp_0'=8,'dp_1'=2] {'cache_0','..., dimensions={0} | all-to-all | bytes 4096 | tf_op jit(solution)/shard_map/all_to_all | solution.py:31
  286.3 1.1 reduce_sum.109
  288.9 12.4 %all_to_all.54 = bf16[16,128,64]{1,2,0:T(8,128)(2,1)S(1)} all-to-all(bf16[16,128,64]{1,2,0:T(8,128)(2,1)S(1)} %broadcast_in_dim.71), channel_id=1, replica_groups=mesh['cache_0'=2,'cache_1'=8,'cache_2'=2,'dp_0'=8,'dp_1'=2] {'dp_0','dp_1'}, dimensions={0} | all-to-all | bytes 524288 | tf_op jit(solution)/shard_map/all_to_all | solution.py:31
  301.3 0.7 copy_bitcast_fusion
  (61 shorter events, 6.0 us)
Async XLA Ops:
  0.6 43.0 %copy-start = (bf16[2048,64]{0,1:T(8,128)(2,1)S(1)}, bf16[2048,64]{0,1:T(8,128)(2,1)}, u32[]{:S(2)}) copy-start(bf16[2048,64]{0,1:T(8,128)(2,1)} %param.18) | copy-start | bytes 786436
  0.6 51.7 %copy-start.12 = (f32[2,8,16]{2,1,0:T(8,128)S(1)}, f32[2,8,16]{2,1,0:T(8,128)}, u32[]{:S(2)}) copy-start(f32[2,8,16]{2,1,0:T(8,128)} %param.24) | copy-start | bytes 3076
  0.7 51.8 %copy-start.13 = (f32[2,8,16]{2,1,0:T(8,128)S(1)}, f32[2,8,16]{2,1,0:T(8,128)}, u32[]{:S(2)}) copy-start(f32[2,8,16]{2,1,0:T(8,128)} %param.25) | copy-start | bytes 3076
  0.7 54.8 %copy-start.2 = (bf16[2,256,2048]{2,1,0:T(8,128)(2,1)S(1)}, bf16[2,256,2048]{2,1,0:T(8,128)(2,1)}, u32[]{:S(2)}) copy-start(bf16[2,256,2048]{2,1,0:T(8,128)(2,1)} %param.22) | copy-start | bytes 6291460
  45.7 34.6 %all-to-all-start.1 = ((bf16[32,256,64]{1,2,0:T(8,128)(2,1)}), bf16[32,256,64]{1,2,0:T(8,128)(2,1)}, u32[]{:S(2)}, u32[]{:S(2)}) async-start(bf16[32,256,64]{1,2,0:T(8,128)(2,1)} %broadcast_in_dim.66), calls=%async_computation.1 | async-start | bytes 2097152 | tf_op jit(solution)/shard_map/all_to_all | solution.py:31
  55.5 2.5 copy-start.3
  58.0 2.6 copy-start.14
  58.0 2.7 copy-start.15
  61.1 21.8 %copy-start.6 = (pred[256,520]{0,1:T(8,128)(4,1)}, pred[256,520]{0,1:T(8,128)(4,1)S(1)}, u32[]{:S(2)}) copy-start(pred[256,520]{0,1:T(8,128)(4,1)S(1)} %pad_add_fusion) | copy-start | bytes 399364
  80.3 2.7 copy-start.4
  80.3 2.7 copy-start.16
  82.9 3.3 %copy-start.1 = (f32[16,256,520]{1,2,0:T(8,128)}, f32[16,256,520]{1,2,0:T(8,128)S(1)}, u32[]{:S(2)}) copy-start(f32[16,256,520]{1,2,0:T(8,128)S(1)} %fusion.8) | copy-start | bytes 25559044
  86.2 56.5 %copy-start.7 = (bf16[256,64]{0,1:T(8,128)(2,1)S(1)}, bf16[256,64]{0,1:T(8,128)(2,1)}, u32[]{:S(2)}) copy-start(bf16[256,64]{0,1:T(8,128)(2,1)} %param.16) | copy-start | bytes 98308
  86.2 56.5 %copy-start.8 = (bf16[256,64]{0,1:T(8,128)(2,1)S(1)}, bf16[256,64]{0,1:T(8,128)(2,1)}, u32[]{:S(2)}) copy-start(bf16[256,64]{0,1:T(8,128)(2,1)} %param.17) | copy-start | bytes 98308
  194.2 44.8 %copy-start.5 = (f32[256,64]{0,1:T(8,128)S(1)}, f32[256,64]{0,1:T(8,128)}, u32[]{:S(2)}) copy-start(f32[256,64]{0,1:T(8,128)} %get-tuple-element.21) | copy-start | bytes 196612
  204.7 83.5 %copy-start.9 = (f32[128,64]{0,1:T(8,128)S(1)}, f32[128,64]{0,1:T(8,128)}, u32[]{:S(2)}) copy-start(f32[128,64]{0,1:T(8,128)} %param.19) | copy-start | bytes 98308
  204.7 83.5 %copy-start.10 = (f32[128,64]{0,1:T(8,128)S(1)}, f32[128,64]{0,1:T(8,128)}, u32[]{:S(2)}) copy-start(f32[128,64]{0,1:T(8,128)} %param.20) | copy-start | bytes 98308
  204.7 83.5 %copy-start.11 = (f32[128,64]{0,1:T(8,128)S(1)}, f32[128,64]{0,1:T(8,128)}, u32[]{:S(2)}) copy-start(f32[128,64]{0,1:T(8,128)} %param.21) | copy-start | bytes 98308

commit v2 on v1

--- a/solution.py
+++ b/solution.py
@@ -49,6 +49,31 @@
     dims = list(tiles.shape[1:])
     dims[dim] *= tiles.shape[0]
     return jnp.moveaxis(tiles, 0, dim).reshape(dims)
+
+
+CHIPS = ("cache_0", "cache_1")
+CORE = "cache_2"
+
+
+def collect_cache(array, dim):
+    chips = lax.axis_size(CHIPS)
+    across = lax.all_to_all(
+        jnp.broadcast_to(array, (chips, *array.shape)), CHIPS, 0, 0, tiled=True
+    )
+    cores = lax.axis_size(CORE)
+    pairs = lax.all_to_all(
+        jnp.broadcast_to(across, (cores, *across.shape)), CORE, 0, 0, tiled=True
+    )
+    tiles = jnp.swapaxes(pairs, 0, 1).reshape(chips * cores, *array.shape)
+    return in_order(tiles, dim)
+
+
+def summed_over_cache(array, dim):
+    chips, cores = (lax.axis_size(CHIPS), lax.axis_size(CORE))
+    tiles = split_up(array, dim, chips * cores)
+    tiles = jnp.swapaxes(tiles.reshape(chips, cores, *tiles.shape[1:]), 0, 1)
+    on_chip = lax.all_to_all(tiles, CORE, 0, 0, tiled=True).sum(axis=0)
+    return lax.all_to_all(on_chip, CHIPS, 0, 0, tiled=True).sum(axis=0)
 
 
 def collect(array, axis, dim):
@@ -151,12 +176,12 @@
 ):
     model_width = query_weight.shape[0]
     shard_index = lax.axis_index(CACHE)
-    features = collect(tokens, CACHE, 1)
+    features = collect_cache(tokens, 1)
     query_pre = jnp.dot(features, query_weight, preferred_element_type=jnp.float32) / math.sqrt(
         model_width
     )
     query_block = jax.nn.silu(query_pre).astype(jnp.bfloat16)
-    queries = collect(query_block, CACHE, 1)
+    queries = collect_cache(query_block, 1)
     user_ids = segments[0]
     hist_rows = key_codes.shape[1]
     span_rows = span_keys.shape[0]
@@ -165,7 +190,7 @@
     mask = key_mask(user_ids, lengths, shard_index, hist_rows, span_rows)
     mixed_part, weighted_slope = forward_part(queries, keys, values_all, mask, HEADS)
     gate_float = gate_values.astype(jnp.float32)
-    mixed_block = summed_on_arrival(mixed_part, CACHE, 1)
+    mixed_block = summed_over_cache(mixed_part, 1)
     back = output_grad.astype(jnp.float32) * gate_float
     row_sum, row_square, back_sum, back_mixed = packed_total(
         (
@@ -185,7 +210,7 @@
     grad_block = inverse * (
         back - (back_sum / model_width)[:, None] - normed * (back_cross / model_width)[:, None]
     )
-    mixed_grad = collect(grad_block.astype(jnp.bfloat16), CACHE, 1)
+    mixed_grad = collect_cache(grad_block.astype(jnp.bfloat16), 1)
     query_part = backward_part(keys, values_all, weighted_slope, mixed_grad, HEADS)
     query_grad = sent_and_summed(query_part.astype(jnp.bfloat16), CACHE, 1)
     pre_grad = (query_grad * silu_slope(query_pre)).astype(jnp.bfloat16)

time: 304 us -> 267 us (0.88)
  blocking collectives: 240 us -> 185 us
  starting transfers between devices: 6.61 us -> 17.8 us
  waiting for transfers between devices: 10.9 us -> 16.6 us
  matrix products: 17.8 us -> 14.7 us
    all_to_all x5 -> x3, blocking collectives: 133 us -> 59.9 us  [sent_to_all(): return lax.all_to_all(copies, axis, split_axis=0, concat_axis=0, tiled=True)]
    all_to_all x1 -> x6, blocking collectives: 56.2 us -> 75.5 us  [the longest x1 30.5 us: summed_over_cache(): return lax.all_to_all(on_chip, CHIPS, 0, 0, tiled=True).sum(axis=0)]
    all_to_all x1 -> x2, starting transfers between devices: 6.61 us -> 17.8 us  [collect_cache(): lax.all_to_all(jnp.broadcast_to(array, (chips, *array.shape)), CHIPS, 0,...]
    all_to_all x1 -> x2, waiting for transfers between devices: 10.9 us -> 16.6 us  [collect_cache(): lax.all_to_all(jnp.broadcast_to(array, (chips, *array.shape)), CHIPS, 0,...]
    broadcast_in_dim x0 -> x6, local copies, waits for them, and re-layouts: none -> 3.93 us  [the longest x3 2.54 us: collect_cache(): jnp.broadcast_to(array, (chips, *array.shape))]
    convert_element_type x1 -> x2, other arithmetic: 8.3 us -> 4.73 us  [dequantize(): scaled.astype(jnp.bfloat16).reshape(user_count * row_count, model_width)]
  transfers between devices with their start and end apart: 1 -> 2, of which waited for: 1 -> 2; matrix products, arithmetic and copies ran while one was open for 6% -> 5% of each run, Pallas kernels for 0% -> 0%
where the time goes in v2:
time: 267 us; the launch traced here: 264 us
  blocking collectives  185 us (69%)
  starting transfers between devices  17.8 us (7%)
  waiting for transfers between devices  16.6 us (6%)
  other arithmetic  15 us (6%)
  matrix products  14.7 us (6%)
  local copies, waits for them, and re-layouts  13.4 us (5%)
    all_to_all x3, blocking collectives, sent_to_all(): return lax.all_to_all(copies, axis, split_axis=0, concat_axis=0, tiled=True)  59.9 us
    all_to_all x2, blocking collectives, sent_and_summed(): tiles = lax.all_to_all(split_up(array, dim, peers), axis, 0, 0, tiled=True)  49.8 us
    all_to_all x1, blocking collectives, summed_over_cache(): return lax.all_to_all(on_chip, CHIPS, 0, 0, tiled=True).sum(axis=0)  30.5 us
    all_to_all x3, blocking collectives, collect_cache(): lax.all_to_all(jnp.broadcast_to(across, (cores, *across.shape)), CORE, 0,...  22 us
    all_to_all x2, starting transfers between devices, collect_cache(): lax.all_to_all(jnp.broadcast_to(array, (chips, *array.shape)), CHIPS, 0,...  17.8 us
    all_to_all x1, blocking collectives, collect_cache(): lax.all_to_all(jnp.broadcast_to(array, (chips, *array.shape)), CHIPS, 0,...  16.8 us
    all_to_all x2, waiting for transfers between devices, collect_cache(): lax.all_to_all(jnp.broadcast_to(array, (chips, *array.shape)), CHIPS, 0,...  16.6 us
    dot_general x3, matrix products, product(): return jnp.einsum(form, left, right, preferred_element_type=jnp.float32)  13.4 us
  transfers between devices with their start and end apart: 2, of which 2 were waited for; matrix products, arithmetic and copies ran while one was open for 5% of the time, Pallas kernels for 0%

profile of v2, /device:TPU:1, one launch (start us, length us, event | category | flops | bytes accessed | tf_op | source)
XLA Modules:
  0.0 264.5 jit_solution(1780934455095059002)
XLA Ops:
  0.6 1.6 broadcast_in_dim.74
  2.3 13.4 %all-to-all-start = ((bf16[16,256,64]{1,2,0:T(8,128)(2,1)}), bf16[16,256,64]{1,2,0:T(8,128)(2,1)S(1)}, u32[]{:S(2)}, u32[]{:S(2)}) async-start(bf16[16,256,64]{1,2,0:T(8,128)(2,1)} %broadcast_in_dim.74), calls=%async_computation | async-start | bytes 1048576 | tf_op jit(solution)/shard_map/all_to_all | solution.py:60
  17.2 1.5 compare_and_fusion
  18.8 12.2 %all-to-all-done = bf16[16,256,64]{1,2,0:T(8,128)(2,1)S(1)} async-done(((bf16[16,256,64]{1,2,0:T(8,128)(2,1)}), bf16[16,256,64]{1,2,0:T(8,128)(2,1)S(1)}, u32[]{:S(2)}, u32[]{:S(2)}) %all-to-all-start) | async-done | bytes 524320 | tf_op jit(solution)/shard_map/all_to_all | solution.py:60
  31.1 7.2 %all_to_all.67 = bf16[2,16,256,64]{2,3,1,0:T(8,128)(2,1)S(1)} all-to-all(bf16[2,16,256,64]{2,3,1,0:T(8,128)(2,1)S(1)} %broadcast_in_dim.75), channel_id=1, replica_groups=mesh['cache_0'=2,'cache_1'=8,'cache_2'=2,'dp_0'=8,'dp_1'=2] {'cache_2'}, dimensions={0} | all-to-all | bytes 2097152 | tf_op jit(solution)/shard_map/all_to_all | solution.py:64
  40.2 4.3 %all-to-all-start.2 = ((bf16[16,256,64]{1,2,0:T(8,128)(2,1)}), bf16[16,256,64]{1,2,0:T(8,128)(2,1)}, u32[]{:S(2)}, u32[]{:S(2)}) async-start(bf16[16,256,64]{1,2,0:T(8,128)(2,1)} %broadcast_in_dim.76), calls=%async_computation.2 | async-start | bytes 1048576 | tf_op jit(solution)/shard_map/all_to_all | solution.py:60
  50.6 1.8 fusion.2
  52.4 2.9 %fusion.3 = bf16[512,16,128]{2,0,1:T(8,128)(2,1)} fusion(f32[512,16,128]{2,1,0:T(8,128)S(1)} %bitcast.72, f32[512,16]{0,1:T(8,128)S(1)} %copy-done.8), kind=kLoop, calls=%fused_computation.8 | loop fusion | flops 2097152 | bytes 6324224 | tf_op jit(solution)/shard_map/convert_element_type | solution.py:112
  55.4 4.4 %all-to-all-done.2 = bf16[16,256,64]{1,2,0:T(8,128)(2,1)} async-done(((bf16[16,256,64]{1,2,0:T(8,128)(2,1)}), bf16[16,256,64]{1,2,0:T(8,128)(2,1)}, u32[]{:S(2)}, u32[]{:S(2)}) %all-to-all-start.2) | async-done | bytes 524320 | tf_op jit(solution)/shard_map/all_to_all | solution.py:60
  59.7 1.2 broadcast_in_dim.77
  60.9 7.0 %all_to_all.68 = bf16[2,16,256,64]{2,3,1,0:T(8,128)(2,1)S(1)} all-to-all(bf16[2,16,256,64]{2,3,1,0:T(8,128)(2,1)S(1)} %broadcast_in_dim.77), channel_id=1, replica_groups=mesh['cache_0'=2,'cache_1'=8,'cache_2'=2,'dp_0'=8,'dp_1'=2] {'cache_2'}, dimensions={0} | all-to-all | bytes 2097152 | tf_op jit(solution)/shard_map/all_to_all | solution.py:64
  68.1 1.3 fusion.8
  69.6 3.2 %fusion = f32[16,128,256]{2,1,0:T(8,128)S(1)} fusion(f32[16,256,520]{1,2,0:T(8,128)S(1)} %fusion.8, pred[256,520]{0,1:T(8,128)(4,1)S(1)} %pad_add_fusion, bf16[8,16,128]{2,0,1:T(8,128)(2,1)S(1)} %bitcast.87, bf16[512,16,128]{2,0,1:T(8,128)(2,1)S(1)} %copy-done.4), kind=kOutput, calls=%fused_computation.3 | convolution fusion | flops 564428800 | bytes 12879872 | tf_op jit(solution)/shard_map/hqk,khd->qhd/dot_general | solution.py:102
  73.0 6.3 %all_to_all.69 = f32[2,16,256,64]{2,3,1,0:T(8,128)} all-to-all(f32[2,16,256,64]{2,3,1,0:T(8,128)S(1)} %copy.74), channel_id=1, replica_groups=mesh['cache_0'=2,'cache_1'=8,'cache_2'=2,'dp_0'=8,'dp_1'=2] {'cache_2'}, dimensions={0} | all-to-all | bytes 4194304 | tf_op jit(solution)/shard_map/all_to_all | solution.py:75
  79.3 2.9 %reduce_sum.109 = f32[16,256,64]{1,2,0:T(8,128)} reduce(f32[2,16,256,64]{2,3,1,0:T(8,128)} %all_to_all.69, f32[]{:T(128)} %constant.95.clone.1), dimensions={0}, to_apply=%region_1.2 | reduce | flops 262144 | bytes 3145732 | tf_op jit(solution)/shard_map/reduce_sum | solution.py:75
  82.2 30.5 %all_to_all.70 = f32[16,256,64]{1,2,0:T(8,128)S(1)} all-to-all(f32[16,256,64]{1,2,0:T(8,128)} %reduce_sum.109), channel_id=1, replica_groups=mesh['cache_0'=2,'cache_1'=8,'cache_2'=2,'dp_0'=8,'dp_1'=2] {'cache_0','..., dimensions={0} | all-to-all | bytes 2097152 | tf_op jit(solution)/shard_map/all_to_all | solution.py:76
  113.0 18.5 %all_to_all.71 = f32[32,1,1024]{2,1,0:T(1,128)} all-to-all(f32[32,1,1024]{2,1,0:T(1,128)S(1)} %broadcast_in_dim.79), channel_id=1, replica_groups=mesh['cache_0'=2,'cache_1'=8,'cache_2'=2,'dp_0'=8,'dp_1'=2] {'cache_0','..., dimensions={0} | all-to-all | bytes 262144 | tf_op jit(solution)/shard_map/all_to_all | solution.py:31
  133.2 16.8 %all_to_all.72 = bf16[16,256,64]{1,2,0:T(8,128)(2,1)S(1)} all-to-all(bf16[16,256,64]{1,2,0:T(8,128)(2,1)S(1)} %broadcast_in_dim.80), channel_id=1, replica_groups=mesh['cache_0'=2,'cache_1'=8,'cache_2'=2,'dp_0'=8,'dp_1'=2] {'cache_0','..., dimensions={0} | all-to-all | bytes 1048576 | tf_op jit(solution)/shard_map/all_to_all | solution.py:60
  150.1 7.7 %all_to_all.73 = bf16[2,16,256,64]{2,3,1,0:T(8,128)(2,1)S(1)} all-to-all(bf16[2,16,256,64]{2,3,1,0:T(8,128)(2,1)S(1)} %broadcast_in_dim.81), channel_id=1, replica_groups=mesh['cache_0'=2,'cache_1'=8,'cache_2'=2,'dp_0'=8,'dp_1'=2] {'cache_2'}, dimensions={0} | all-to-all | bytes 2097152 | tf_op jit(solution)/shard_map/all_to_all | solution.py:64
  158.9 8.9 %fusion.7 = bf16[16,128,256]{2,1,0:T(8,128)(2,1)} fusion(f32[16,256,520]{1,2,0:T(8,128)} %copy-done.1, pred[256,520]{0,1:T(8,128)(4,1)} %copy-done.7, bf16[256,16,128]{0,2,1:T(8,128)(2,1)} %bitcast.80, bf16[8,16,128]{2,0,1:T(8,128)(2,1)S(1)} %bitcast.84, bf16[512,16,128]{2,0,1:T(8,128)(2,1)S(1)} %fusion.2, bf16[8,16,128]{2,0,1:T(8,128)(2,1)S(1)} %bitcast.88, ...), kind=kOutput, calls=%fused_computation.15 | convolution fusion | flops 1125122048 | bytes 15009792 | tf_op jit(solution)/shard_map/hqk,khd->qhd/dot_general | solution.py:102
  167.8 33.4 %all_to_all.74 = bf16[32,256,64]{1,2,0:T(8,128)(2,1)S(1)} all-to-all(bf16[32,256,64]{1,2,0:T(8,128)(2,1)} %bitcast.81), channel_id=1, replica_groups=mesh['cache_0'=2,'cache_1'=8,'cache_2'=2,'dp_0'=8,'dp_1'=2] {'cache_0','..., dimensions={0} | all-to-all | bytes 2097152 | tf_op jit(solution)/shard_map/all_to_all | solution.py:86
  201.8 16.4 %all_to_all.75 = bf16[16,128,64]{1,2,0:T(8,128)(2,1)S(1)} all-to-all(bf16[16,128,64]{1,2,0:T(8,128)(2,1)S(1)} %bitcast.82), channel_id=1, replica_groups=mesh['cache_0'=2,'cache_1'=8,'cache_2'=2,'dp_0'=8,'dp_1'=2] {'dp_0','dp_1'}, dimensions={0} | all-to-all | bytes 524288 | tf_op jit(solution)/shard_map/all_to_all | solution.py:86
  219.7 29.0 %all_to_all.76 = f32[512,1,1]{2,1,0:T(1,128)S(1)} all-to-all(f32[512,1,1]{2,1,0:T(1,128)S(1)} %broadcast_in_dim.82), channel_id=1, replica_groups=mesh['cache_0'=2,'cache_1'=8,'cache_2'=2,'dp_0'=8,'dp_1'=2] {'cache_0','..., dimensions={0} | all-to-all | bytes 4096 | tf_op jit(solution)/shard_map/all_to_all | solution.py:31
  251.3 12.4 %all_to_all.77 = bf16[16,128,64]{1,2,0:T(8,128)(2,1)S(1)} all-to-all(bf16[16,128,64]{1,2,0:T(8,128)(2,1)S(1)} %broadcast_in_dim.83), channel_id=1, replica_groups=mesh['cache_0'=2,'cache_1'=8,'cache_2'=2,'dp_0'=8,'dp_1'=2] {'dp_0','dp_1'}, dimensions={0} | all-to-all | bytes 524288 | tf_op jit(solution)/shard_map/all_to_all | solution.py:31
  (87 shorter events, 17.8 us)
Async XLA Ops:
  0.6 37.8 %copy-start = (bf16[2048,64]{0,1:T(8,128)(2,1)S(1)}, bf16[2048,64]{0,1:T(8,128)(2,1)}, u32[]{:S(2)}) copy-start(bf16[2048,64]{0,1:T(8,128)(2,1)} %param.18) | copy-start | bytes 786436
  2.3 28.7 %all-to-all-start = ((bf16[16,256,64]{1,2,0:T(8,128)(2,1)}), bf16[16,256,64]{1,2,0:T(8,128)(2,1)S(1)}, u32[]{:S(2)}, u32[]{:S(2)}) async-start(bf16[16,256,64]{1,2,0:T(8,128)(2,1)} %broadcast_in_dim.74), calls=%async_computation | async-start | bytes 1048576 | tf_op jit(solution)/shard_map/all_to_all | solution.py:60
  18.8 25.8 %copy-start.20 = (s32[1,256]{1,0:T(1,128)S(1)}, s32[1,256]{1,0:T(1,128)}, u32[]{:S(2)}) copy-start(s32[1,256]{1,0:T(1,128)} %param.29) | copy-start | bytes 3076
  18.8 26.5 %copy-start.18 = (f32[2,8,16]{2,1,0:T(8,128)S(1)}, f32[2,8,16]{2,1,0:T(8,128)}, u32[]{:S(2)}) copy-start(f32[2,8,16]{2,1,0:T(8,128)} %param.24) | copy-start | bytes 3076
  18.8 26.5 %copy-start.19 = (f32[2,8,16]{2,1,0:T(8,128)S(1)}, f32[2,8,16]{2,1,0:T(8,128)}, u32[]{:S(2)}) copy-start(f32[2,8,16]{2,1,0:T(8,128)} %param.25) | copy-start | bytes 3076
  31.1 17.3 %copy-start.2 = (bf16[2,256,2048]{2,1,0:T(8,128)(2,1)S(1)}, bf16[2,256,2048]{2,1,0:T(8,128)(2,1)}, u32[]{:S(2)}) copy-start(bf16[2,256,2048]{2,1,0:T(8,128)(2,1)} %param.22) | copy-start | bytes 6291460
  40.2 19.5 %all-to-all-start.2 = ((bf16[16,256,64]{1,2,0:T(8,128)(2,1)}), bf16[16,256,64]{1,2,0:T(8,128)(2,1)}, u32[]{:S(2)}, u32[]{:S(2)}) async-start(bf16[16,256,64]{1,2,0:T(8,128)(2,1)} %broadcast_in_dim.76), calls=%async_computation.2 | async-start | bytes 1048576 | tf_op jit(solution)/shard_map/all_to_all | solution.py:60
  48.4 1.6 copy-start.3
  49.0 1.6 copy-start.5
  49.0 1.6 copy-start.9
  50.6 1.8 copy-start.8
  50.6 18.7 %copy-start.7 = (pred[256,520]{0,1:T(8,128)(4,1)}, pred[256,520]{0,1:T(8,128)(4,1)S(1)}, u32[]{:S(2)}) copy-start(pred[256,520]{0,1:T(8,128)(4,1)S(1)} %pad_add_fusion) | copy-start | bytes 399364
  59.7 8.3 %copy-start.12 = (bf16[8,2048]{1,0:T(8,128)(2,1)S(1)}, bf16[8,2048]{1,0:T(8,128)(2,1)}, u32[]{:S(2)}) copy-start(bf16[8,2048]{1,0:T(8,128)(2,1)} %param.26) | copy-start | bytes 98308
  68.0 1.6 copy-start.4
  68.0 1.6 copy-start.21
  69.3 3.6 %copy-start.1 = (f32[16,256,520]{1,2,0:T(8,128)}, f32[16,256,520]{1,2,0:T(8,128)S(1)}, u32[]{:S(2)}) copy-start(f32[16,256,520]{1,2,0:T(8,128)S(1)} %fusion.8) | copy-start | bytes 25559044
  79.3 33.6 %copy-start.10 = (bf16[256,64]{0,1:T(8,128)(2,1)S(1)}, bf16[256,64]{0,1:T(8,128)(2,1)}, u32[]{:S(2)}) copy-start(bf16[256,64]{0,1:T(8,128)(2,1)} %param.16) | copy-start | bytes 98308
  79.3 33.6 %copy-start.11 = (bf16[256,64]{0,1:T(8,128)(2,1)S(1)}, bf16[256,64]{0,1:T(8,128)(2,1)}, u32[]{:S(2)}) copy-start(bf16[256,64]{0,1:T(8,128)(2,1)} %param.17) | copy-start | bytes 98308
  133.2 25.7 %copy-start.13 = (bf16[8,2048]{1,0:T(8,128)(2,1)S(1)}, bf16[8,2048]{1,0:T(8,128)(2,1)}, u32[]{:S(2)}) copy-start(bf16[8,2048]{1,0:T(8,128)(2,1)} %param.26) | copy-start | bytes 98308
  133.2 25.7 %copy-start.22 = (bf16[8,2048]{1,0:T(8,128)(2,1)S(1)}, bf16[8,2048]{1,0:T(8,128)(2,1)}, u32[]{:S(2)}) copy-start(bf16[8,2048]{1,0:T(8,128)(2,1)} %param.27) | copy-start | bytes 98308
  158.9 42.4 %copy-start.6 = (f32[256,64]{0,1:T(8,128)S(1)}, f32[256,64]{0,1:T(8,128)}, u32[]{:S(2)}) copy-start(f32[256,64]{0,1:T(8,128)} %get-tuple-element.21) | copy-start | bytes 196612
  167.8 82.8 %copy-start.14 = (f32[128,64]{0,1:T(8,128)S(1)}, f32[128,64]{0,1:T(8,128)}, u32[]{:S(2)}) copy-start(f32[128,64]{0,1:T(8,128)} %param.19) | copy-start | bytes 98308
  167.8 82.8 %copy-start.15 = (f32[128,64]{0,1:T(8,128)S(1)}, f32[128,64]{0,1:T(8,128)}, u32[]{:S(2)}) copy-start(f32[128,64]{0,1:T(8,128)} %param.20) | copy-start | bytes 98308
  167.8 82.8 %copy-start.16 = (f32[128,64]{0,1:T(8,128)S(1)}, f32[128,64]{0,1:T(8,128)}, u32[]{:S(2)}) copy-start(f32[128,64]{0,1:T(8,128)} %param.21) | copy-start | bytes 98308
  (1 other events, 1.6 us)

commit v3 on v2

--- a/solution.py
+++ b/solution.py
@@ -74,6 +74,16 @@
     tiles = jnp.swapaxes(tiles.reshape(chips, cores, *tiles.shape[1:]), 0, 1)
     on_chip = lax.all_to_all(tiles, CORE, 0, 0, tiled=True).sum(axis=0)
     return lax.all_to_all(on_chip, CHIPS, 0, 0, tiled=True).sum(axis=0)
+
+
+def rounded_sum_over_cache(array, dim):
+    chips, cores = (lax.axis_size(CHIPS), lax.axis_size(CORE))
+    tiles = split_up(array.astype(jnp.bfloat16), dim, chips * cores)
+    tiles = jnp.swapaxes(tiles.reshape(chips, cores, *tiles.shape[1:]), 0, 1)
+    on_chip = lax.all_to_all(tiles, CORE, 0, 0, tiled=True)
+    pair_sum = jnp.sum(on_chip.astype(jnp.float32), axis=0).astype(jnp.bfloat16)
+    arrived = lax.all_to_all(pair_sum, CHIPS, 0, 0, tiled=True)
+    return jnp.sum(arrived.astype(jnp.float32), axis=0)
 
 
 def collect(array, axis, dim):
@@ -212,7 +222,7 @@
     )
     mixed_grad = collect_cache(grad_block.astype(jnp.bfloat16), 1)
     query_part = backward_part(keys, values_all, weighted_slope, mixed_grad, HEADS)
-    query_grad = sent_and_summed(query_part.astype(jnp.bfloat16), CACHE, 1)
+    query_grad = rounded_sum_over_cache(query_part, 1)
     pre_grad = (query_grad * silu_slope(query_pre)).astype(jnp.bfloat16)
     weight_part = lax.dot_general(
         features, pre_grad, (((0,), (0,)), ((), ())), preferred_element_type=jnp.float32

time: 267 us -> 262 us (0.981)
  blocking collectives: 185 us -> 178 us
    all_to_all x2 -> x1, blocking collectives: 49.8 us -> 16.4 us  [sent_and_summed(): tiles = lax.all_to_all(split_up(array, dim, peers), axis, 0, 0, tiled=True)]
    all_to_all x0 -> x2, blocking collectives: none -> 24.4 us  [the longest x1 19.8 us: rounded_sum_over_cache(): arrived = lax.all_to_all(pair_sum, CHIPS, 0, 0, tiled=True)]
where the time goes in v3:
time: 262 us; the launch traced here: 260 us
  blocking collectives  178 us (68%)
  starting transfers between devices  17.8 us (7%)
  waiting for transfers between devices  16.6 us (6%)
  matrix products  16.4 us (6%)
  other arithmetic  15.3 us (6%)
  local copies, waits for them, and re-layouts  14.7 us (6%)
    all_to_all x3, blocking collectives, sent_to_all(): return lax.all_to_all(copies, axis, split_axis=0, concat_axis=0, tiled=True)  61.2 us
    all_to_all x1, blocking collectives, summed_over_cache(): return lax.all_to_all(on_chip, CHIPS, 0, 0, tiled=True).sum(axis=0)  30.5 us
    all_to_all x3, blocking collectives, collect_cache(): lax.all_to_all(jnp.broadcast_to(across, (cores, *across.shape)), CORE, 0,...  22 us
    all_to_all x1, blocking collectives, rounded_sum_over_cache(): arrived = lax.all_to_all(pair_sum, CHIPS, 0, 0, tiled=True)  19.8 us
    all_to_all x2, starting transfers between devices, collect_cache(): lax.all_to_all(jnp.broadcast_to(array, (chips, *array.shape)), CHIPS, 0,...  17.8 us
    all_to_all x1, blocking collectives, collect_cache(): lax.all_to_all(jnp.broadcast_to(array, (chips, *array.shape)), CHIPS, 0,...  16.8 us
    all_to_all x2, waiting for transfers between devices, collect_cache(): lax.all_to_all(jnp.broadcast_to(array, (chips, *array.shape)), CHIPS, 0,...  16.6 us
    all_to_all x1, blocking collectives, sent_and_summed(): tiles = lax.all_to_all(split_up(array, dim, peers), axis, 0, 0, tiled=True)  16.4 us
  transfers between devices with their start and end apart: 2, of which 2 were waited for; matrix products, arithmetic and copies ran while one was open for 5% of the time, Pallas kernels for 0%

profile of v3, /device:TPU:1, one launch (start us, length us, event | category | flops | bytes accessed | tf_op | source)
XLA Modules:
  0.0 260.0 jit_solution(16119165818520101864)
XLA Ops:
  0.6 1.6 broadcast_in_dim.74
  2.3 13.4 %all-to-all-start = ((bf16[16,256,64]{1,2,0:T(8,128)(2,1)}), bf16[16,256,64]{1,2,0:T(8,128)(2,1)S(1)}, u32[]{:S(2)}, u32[]{:S(2)}) async-start(bf16[16,256,64]{1,2,0:T(8,128)(2,1)} %broadcast_in_dim.74), calls=%async_computation | async-start | bytes 1048576 | tf_op jit(solution)/shard_map/all_to_all | solution.py:60
  17.2 1.5 compare_and_fusion
  18.8 12.2 %all-to-all-done = bf16[16,256,64]{1,2,0:T(8,128)(2,1)S(1)} async-done(((bf16[16,256,64]{1,2,0:T(8,128)(2,1)}), bf16[16,256,64]{1,2,0:T(8,128)(2,1)S(1)}, u32[]{:S(2)}, u32[]{:S(2)}) %all-to-all-start) | async-done | bytes 524320 | tf_op jit(solution)/shard_map/all_to_all | solution.py:60
  31.1 7.2 %all_to_all.72 = bf16[2,16,256,64]{2,3,1,0:T(8,128)(2,1)S(1)} all-to-all(bf16[2,16,256,64]{2,3,1,0:T(8,128)(2,1)S(1)} %broadcast_in_dim.75), channel_id=1, replica_groups=mesh['cache_0'=2,'cache_1'=8,'cache_2'=2,'dp_0'=8,'dp_1'=2] {'cache_2'}, dimensions={0} | all-to-all | bytes 2097152 | tf_op jit(solution)/shard_map/all_to_all | solution.py:64
  40.2 4.3 %all-to-all-start.2 = ((bf16[16,256,64]{1,2,0:T(8,128)(2,1)}), bf16[16,256,64]{1,2,0:T(8,128)(2,1)}, u32[]{:S(2)}, u32[]{:S(2)}) async-start(bf16[16,256,64]{1,2,0:T(8,128)(2,1)} %broadcast_in_dim.76), calls=%async_computation.2 | async-start | bytes 1048576 | tf_op jit(solution)/shard_map/all_to_all | solution.py:60
  50.6 1.8 fusion.2
  52.4 2.9 %fusion.3 = bf16[512,16,128]{2,0,1:T(8,128)(2,1)} fusion(f32[512,16,128]{2,1,0:T(8,128)S(1)} %bitcast.76, f32[512,16]{0,1:T(8,128)S(1)} %copy-done.9), kind=kLoop, calls=%fused_computation.8 | loop fusion | flops 2097152 | bytes 6324224 | tf_op jit(solution)/shard_map/convert_element_type | solution.py:122
  55.4 4.4 %all-to-all-done.2 = bf16[16,256,64]{1,2,0:T(8,128)(2,1)} async-done(((bf16[16,256,64]{1,2,0:T(8,128)(2,1)}), bf16[16,256,64]{1,2,0:T(8,128)(2,1)}, u32[]{:S(2)}, u32[]{:S(2)}) %all-to-all-start.2) | async-done | bytes 524320 | tf_op jit(solution)/shard_map/all_to_all | solution.py:60
  60.9 7.0 %all_to_all.73 = bf16[2,16,256,64]{2,3,1,0:T(8,128)(2,1)S(1)} all-to-all(bf16[2,16,256,64]{2,3,1,0:T(8,128)(2,1)S(1)} %broadcast_in_dim.77), channel_id=1, replica_groups=mesh['cache_0'=2,'cache_1'=8,'cache_2'=2,'dp_0'=8,'dp_1'=2] {'cache_2'}, dimensions={0} | all-to-all | bytes 2097152 | tf_op jit(solution)/shard_map/all_to_all | solution.py:64
  69.6 3.2 %fusion = f32[16,128,256]{2,1,0:T(8,128)S(1)} fusion(f32[16,256,520]{1,2,0:T(8,128)S(1)} %fusion.8, pred[256,520]{0,1:T(8,128)(4,1)S(1)} %pad_add_fusion, bf16[8,16,128]{2,0,1:T(8,128)(2,1)S(1)} %bitcast.92, bf16[512,16,128]{2,0,1:T(8,128)(2,1)S(1)} %copy-done.4), kind=kOutput, calls=%fused_computation.3 | convolution fusion | flops 564428800 | bytes 12879872 | tf_op jit(solution)/shard_map/hqk,khd->qhd/dot_general | solution.py:112
  73.1 6.3 %all_to_all.74 = f32[2,16,256,64]{2,3,1,0:T(8,128)} all-to-all(f32[2,16,256,64]{2,3,1,0:T(8,128)S(1)} %copy.79), channel_id=1, replica_groups=mesh['cache_0'=2,'cache_1'=8,'cache_2'=2,'dp_0'=8,'dp_1'=2] {'cache_2'}, dimensions={0} | all-to-all | bytes 4194304 | tf_op jit(solution)/shard_map/all_to_all | solution.py:75
  79.4 2.9 %reduce_sum.121 = f32[16,256,64]{1,2,0:T(8,128)} reduce(f32[2,16,256,64]{2,3,1,0:T(8,128)} %all_to_all.74, f32[]{:T(128)} %constant.96.clone.1), dimensions={0}, to_apply=%region_1.2 | reduce | flops 262144 | bytes 3145732 | tf_op jit(solution)/shard_map/reduce_sum | solution.py:75
  82.3 30.5 %all_to_all.75 = f32[16,256,64]{1,2,0:T(8,128)S(1)} all-to-all(f32[16,256,64]{1,2,0:T(8,128)} %reduce_sum.121), channel_id=1, replica_groups=mesh['cache_0'=2,'cache_1'=8,'cache_2'=2,'dp_0'=8,'dp_1'=2] {'cache_0','..., dimensions={0} | all-to-all | bytes 2097152 | tf_op jit(solution)/shard_map/all_to_all | solution.py:76
  113.1 18.5 %all_to_all.76 = f32[32,1,1024]{2,1,0:T(1,128)} all-to-all(f32[32,1,1024]{2,1,0:T(1,128)S(1)} %broadcast_in_dim.79), channel_id=1, replica_groups=mesh['cache_0'=2,'cache_1'=8,'cache_2'=2,'dp_0'=8,'dp_1'=2] {'cache_0','..., dimensions={0} | all-to-all | bytes 262144 | tf_op jit(solution)/shard_map/all_to_all | solution.py:31
  133.2 16.8 %all_to_all.77 = bf16[16,256,64]{1,2,0:T(8,128)(2,1)S(1)} all-to-all(bf16[16,256,64]{1,2,0:T(8,128)(2,1)S(1)} %broadcast_in_dim.80), channel_id=1, replica_groups=mesh['cache_0'=2,'cache_1'=8,'cache_2'=2,'dp_0'=8,'dp_1'=2] {'cache_0','..., dimensions={0} | all-to-all | bytes 1048576 | tf_op jit(solution)/shard_map/all_to_all | solution.py:60
  150.1 7.7 %all_to_all.78 = bf16[2,16,256,64]{2,3,1,0:T(8,128)(2,1)S(1)} all-to-all(bf16[2,16,256,64]{2,3,1,0:T(8,128)(2,1)S(1)} %broadcast_in_dim.81), channel_id=1, replica_groups=mesh['cache_0'=2,'cache_1'=8,'cache_2'=2,'dp_0'=8,'dp_1'=2] {'cache_2'}, dimensions={0} | all-to-all | bytes 2097152 | tf_op jit(solution)/shard_map/all_to_all | solution.py:64
  158.9 10.5 %fusion.7 = bf16[16,128,256]{2,1,0:T(8,128)(2,1)} fusion(f32[16,256,520]{1,2,0:T(8,128)} %copy-done.1, pred[256,520]{0,1:T(8,128)(4,1)S(1)} %copy-done.8, bf16[256,16,128]{0,2,1:T(8,128)(2,1)} %bitcast.84, bf16[8,16,128]{2,0,1:T(8,128)(2,1)} %bitcast.87, bf16[512,16,128]{2,0,1:T(8,128)(2,1)S(1)} %fusion.2, bf16[8,16,128]{2,0,1:T(8,128)(2,1)} %bitcast.91, ...), kind=kOutput, calls=%fused_computation.14 | convolution fusion | flops 1125122048 | bytes 15009792 | tf_op jit(solution)/shard_map/hqk,khd->qhd/dot_general | solution.py:112
  169.4 1.3 copy.84
  170.8 4.6 %all_to_all.79 = bf16[2,16,256,64]{2,3,1,0:T(8,128)(2,1)S(1)} all-to-all(bf16[2,16,256,64]{2,3,1,0:T(8,128)(2,1)S(1)} %copy.84), channel_id=1, replica_groups=mesh['cache_0'=2,'cache_1'=8,'cache_2'=2,'dp_0'=8,'dp_1'=2] {'cache_2'}, dimensions={0} | all-to-all | bytes 2097152 | tf_op jit(solution)/shard_map/all_to_all | solution.py:83
  175.8 19.8 %all_to_all.80 = bf16[16,256,64]{1,2,0:T(8,128)(2,1)S(1)} all-to-all(bf16[16,256,64]{1,2,0:T(8,128)(2,1)S(1)} %reduce_sum.128), channel_id=1, replica_groups=mesh['cache_0'=2,'cache_1'=8,'cache_2'=2,'dp_0'=8,'dp_1'=2] {'cache_0','..., dimensions={0} | all-to-all | bytes 1048576 | tf_op jit(solution)/shard_map/all_to_all | solution.py:85
  196.1 16.4 %all_to_all.81 = bf16[16,128,64]{1,2,0:T(8,128)(2,1)S(1)} all-to-all(bf16[16,128,64]{1,2,0:T(8,128)(2,1)S(1)} %bitcast.86), channel_id=1, replica_groups=mesh['cache_0'=2,'cache_1'=8,'cache_2'=2,'dp_0'=8,'dp_1'=2] {'dp_0','dp_1'}, dimensions={0} | all-to-all | bytes 524288 | tf_op jit(solution)/shard_map/all_to_all | solution.py:96
  213.9 30.3 %all_to_all.82 = f32[512,1,1]{2,1,0:T(1,128)S(1)} all-to-all(f32[512,1,1]{2,1,0:T(1,128)S(1)} %broadcast_in_dim.82), channel_id=1, replica_groups=mesh['cache_0'=2,'cache_1'=8,'cache_2'=2,'dp_0'=8,'dp_1'=2] {'cache_0','..., dimensions={0} | all-to-all | bytes 4096 | tf_op jit(solution)/shard_map/all_to_all | solution.py:31
  246.9 12.4 %all_to_all.83 = bf16[16,128,64]{1,2,0:T(8,128)(2,1)S(1)} all-to-all(bf16[16,128,64]{1,2,0:T(8,128)(2,1)S(1)} %broadcast_in_dim.83), channel_id=1, replica_groups=mesh['cache_0'=2,'cache_1'=8,'cache_2'=2,'dp_0'=8,'dp_1'=2] {'dp_0','dp_1'}, dimensions={0} | all-to-all | bytes 524288 | tf_op jit(solution)/shard_map/all_to_all | solution.py:31
  (88 shorter events, 20.5 us)
Async XLA Ops:
  0.6 37.8 %copy-start = (bf16[2048,64]{0,1:T(8,128)(2,1)S(1)}, bf16[2048,64]{0,1:T(8,128)(2,1)}, u32[]{:S(2)}) copy-start(bf16[2048,64]{0,1:T(8,128)(2,1)} %param.18) | copy-start | bytes 786436
  2.3 28.7 %all-to-all-start = ((bf16[16,256,64]{1,2,0:T(8,128)(2,1)}), bf16[16,256,64]{1,2,0:T(8,128)(2,1)S(1)}, u32[]{:S(2)}, u32[]{:S(2)}) async-start(bf16[16,256,64]{1,2,0:T(8,128)(2,1)} %broadcast_in_dim.74), calls=%async_computation | async-start | bytes 1048576 | tf_op jit(solution)/shard_map/all_to_all | solution.py:60
  18.8 25.8 %copy-start.20 = (s32[1,256]{1,0:T(1,128)S(1)}, s32[1,256]{1,0:T(1,128)}, u32[]{:S(2)}) copy-start(s32[1,256]{1,0:T(1,128)} %param.29) | copy-start | bytes 3076
  18.8 26.5 %copy-start.18 = (f32[2,8,16]{2,1,0:T(8,128)S(1)}, f32[2,8,16]{2,1,0:T(8,128)}, u32[]{:S(2)}) copy-start(f32[2,8,16]{2,1,0:T(8,128)} %param.24) | copy-start | bytes 3076
  18.8 26.5 %copy-start.19 = (f32[2,8,16]{2,1,0:T(8,128)S(1)}, f32[2,8,16]{2,1,0:T(8,128)}, u32[]{:S(2)}) copy-start(f32[2,8,16]{2,1,0:T(8,128)} %param.25) | copy-start | bytes 3076
  31.1 17.3 %copy-start.2 = (bf16[2,256,2048]{2,1,0:T(8,128)(2,1)S(1)}, bf16[2,256,2048]{2,1,0:T(8,128)(2,1)}, u32[]{:S(2)}) copy-start(bf16[2,256,2048]{2,1,0:T(8,128)(2,1)} %param.22) | copy-start | bytes 6291460
  40.2 19.5 %all-to-all-start.2 = ((bf16[16,256,64]{1,2,0:T(8,128)(2,1)}), bf16[16,256,64]{1,2,0:T(8,128)(2,1)}, u32[]{:S(2)}, u32[]{:S(2)}) async-start(bf16[16,256,64]{1,2,0:T(8,128)(2,1)} %broadcast_in_dim.76), calls=%async_computation.2 | async-start | bytes 1048576 | tf_op jit(solution)/shard_map/all_to_all | solution.py:60
  48.4 1.6 copy-start.3
  49.0 1.6 copy-start.5
  49.0 1.6 copy-start.17
  49.0 1.6 copy-start.10
  50.6 1.8 copy-start.9
  50.6 18.7 %copy-start.7 = (pred[256,520]{0,1:T(8,128)(4,1)}, pred[256,520]{0,1:T(8,128)(4,1)S(1)}, u32[]{:S(2)}) copy-start(pred[256,520]{0,1:T(8,128)(4,1)S(1)} %pad_add_fusion) | copy-start | bytes 399364
  59.7 8.3 %copy-start.13 = (bf16[8,2048]{1,0:T(8,128)(2,1)S(1)}, bf16[8,2048]{1,0:T(8,128)(2,1)}, u32[]{:S(2)}) copy-start(bf16[8,2048]{1,0:T(8,128)(2,1)} %param.26) | copy-start | bytes 98308
  68.0 1.6 copy-start.4
  68.0 1.6 copy-start.21
  69.3 3.6 %copy-start.1 = (f32[16,256,520]{1,2,0:T(8,128)}, f32[16,256,520]{1,2,0:T(8,128)S(1)}, u32[]{:S(2)}) copy-start(f32[16,256,520]{1,2,0:T(8,128)S(1)} %fusion.8) | copy-start | bytes 25559044
  73.0 39.9 %copy-start.11 = (bf16[256,64]{0,1:T(8,128)(2,1)S(1)}, bf16[256,64]{0,1:T(8,128)(2,1)}, u32[]{:S(2)}) copy-start(bf16[256,64]{0,1:T(8,128)(2,1)} %param.16) | copy-start | bytes 98308
  73.0 39.9 %copy-start.12 = (bf16[256,64]{0,1:T(8,128)(2,1)S(1)}, bf16[256,64]{0,1:T(8,128)(2,1)}, u32[]{:S(2)}) copy-start(bf16[256,64]{0,1:T(8,128)(2,1)} %param.17) | copy-start | bytes 98308
  133.2 25.7 %copy-start.8 = (pred[256,520]{0,1:T(8,128)(4,1)S(1)}, pred[256,520]{0,1:T(8,128)(4,1)}, u32[]{:S(2)}) copy-start(pred[256,520]{0,1:T(8,128)(4,1)} %copy-done.7) | copy-start | bytes 399364
  169.4 26.2 %copy-start.6 = (f32[256,64]{0,1:T(8,128)S(1)}, f32[256,64]{0,1:T(8,128)}, u32[]{:S(2)}) copy-start(f32[256,64]{0,1:T(8,128)} %get-tuple-element.21) | copy-start | bytes 196612
  170.8 75.4 %copy-start.14 = (f32[128,64]{0,1:T(8,128)S(1)}, f32[128,64]{0,1:T(8,128)}, u32[]{:S(2)}) copy-start(f32[128,64]{0,1:T(8,128)} %param.19) | copy-start | bytes 98308
  170.8 75.4 %copy-start.15 = (f32[128,64]{0,1:T(8,128)S(1)}, f32[128,64]{0,1:T(8,128)}, u32[]{:S(2)}) copy-start(f32[128,64]{0,1:T(8,128)} %param.20) | copy-start | bytes 98308
  170.8 75.4 %copy-start.16 = (f32[128,64]{0,1:T(8,128)S(1)}, f32[128,64]{0,1:T(8,128)}, u32[]{:S(2)}) copy-start(f32[128,64]{0,1:T(8,128)} %param.21) | copy-start | bytes 98308

commit v4 on v3

--- a/solution.py
+++ b/solution.py
@@ -84,6 +84,73 @@
     pair_sum = jnp.sum(on_chip.astype(jnp.float32), axis=0).astype(jnp.bfloat16)
     arrived = lax.all_to_all(pair_sum, CHIPS, 0, 0, tiled=True)
     return jnp.sum(arrived.astype(jnp.float32), axis=0)
+
+
+def tokens_and_rows(tokens, gate_values, output_grad):
+    chips, cores = (lax.axis_size(CHIPS), lax.axis_size(CORE))
+    peers = chips * cores
+    rows, cols = tokens.shape
+    row_block = rows // peers
+    flat = rows * cols
+    pair = jnp.stack([gate_values, output_grad])
+    by_chip = pair.reshape(2, chips, cores * row_block, cols).transpose(1, 0, 2, 3)
+    outgoing = jnp.concatenate(
+        [jnp.broadcast_to(tokens.reshape(1, flat), (chips, flat)), by_chip.reshape(chips, -1)], axis=1
+    )
+    across = lax.all_to_all(outgoing, CHIPS, 0, 0, tiled=True)
+    token_tiles = across[:, :flat]
+    row_tiles = across[:, flat:].reshape(chips, 2, cores, row_block, cols)
+    outgoing = jnp.concatenate(
+        [
+            jnp.broadcast_to(token_tiles[None], (cores, chips, flat)),
+            row_tiles.transpose(2, 0, 1, 3, 4).reshape(cores, chips, 2 * row_block * cols),
+        ],
+        axis=2,
+    )
+    arrived = jnp.swapaxes(lax.all_to_all(outgoing, CORE, 0, 0, tiled=True), 0, 1)
+    arrived = arrived.reshape(peers, -1)
+    features = in_order(arrived[:, :flat].reshape(peers, rows, cols), 1)
+    own_rows = arrived[:, flat:].reshape(peers, 2, row_block, cols).transpose(1, 2, 0, 3)
+    own_rows = own_rows.reshape(2, row_block, peers * cols)
+    return features, own_rows[0], own_rows[1]
+
+
+def rows_summed_over_cache(array):
+    chips, cores = (lax.axis_size(CHIPS), lax.axis_size(CORE))
+    tiles = array.reshape(chips, cores, array.shape[0] // (chips * cores), array.shape[1])
+    on_chip = lax.all_to_all(jnp.swapaxes(tiles, 0, 1), CORE, 0, 0, tiled=True).sum(axis=0)
+    return lax.all_to_all(on_chip, CHIPS, 0, 0, tiled=True).sum(axis=0)
+
+
+def rows_to_everyone(grad_rows, layer_rows):
+    chips, cores = (lax.axis_size(CHIPS), lax.axis_size(CORE))
+    peers = chips * cores
+    row_block, width = grad_rows.shape
+    cols = width // peers
+    flat = row_block * width
+    layer_by_chip = layer_rows.reshape(row_block, chips, cores * cols).transpose(1, 0, 2)
+    outgoing = jnp.concatenate(
+        [
+            jnp.broadcast_to(grad_rows.reshape(1, flat), (chips, flat)),
+            layer_by_chip.reshape(chips, -1),
+        ],
+        axis=1,
+    )
+    across = lax.all_to_all(outgoing, CHIPS, 0, 0, tiled=True)
+    grad_tiles = across[:, :flat]
+    layer_tiles = across[:, flat:].reshape(chips, row_block, cores, cols)
+    outgoing = jnp.concatenate(
+        [
+            jnp.broadcast_to(grad_tiles[None], (cores, chips, flat)),
+            layer_tiles.transpose(2, 0, 1, 3).reshape(cores, chips, row_block * cols),
+        ],
+        axis=2,
+    )
+    arrived = jnp.swapaxes(lax.all_to_all(outgoing, CORE, 0, 0, tiled=True), 0, 1)
+    arrived = arrived.reshape(peers, -1)
+    mixed_grad = arrived[:, :flat].reshape(peers * row_block, width)
+    layer_block = arrived[:, flat:].reshape(peers * row_block, cols)
+    return mixed_grad, layer_block
 
 
 def collect(array, axis, dim):
@@ -186,7 +253,7 @@
 ):
     model_width = query_weight.shape[0]
     shard_index = lax.axis_index(CACHE)
-    features = collect_cache(tokens, 1)
+    features, gate_rows, grad_rows_in = tokens_and_rows(tokens, gate_values, output_grad)
     query_pre = jnp.dot(features, query_weight, preferred_element_type=jnp.float32) / math.sqrt(
         model_width
     )
@@ -199,28 +266,21 @@
     values_all = jnp.concatenate([dequantize(value_codes, value_scales), span_values], axis=0)
     mask = key_mask(user_ids, lengths, shard_index, hist_rows, span_rows)
     mixed_part, weighted_slope = forward_part(queries, keys, values_all, mask, HEADS)
-    gate_float = gate_values.astype(jnp.float32)
-    mixed_block = summed_over_cache(mixed_part, 1)
-    back = output_grad.astype(jnp.float32) * gate_float
-    row_sum, row_square, back_sum, back_mixed = packed_total(
-        (
-            jnp.sum(mixed_block, axis=1),
-            jnp.sum(mixed_block * mixed_block, axis=1),
-            jnp.sum(back, axis=1),
-            jnp.sum(back * mixed_block, axis=1),
-        ),
-        CACHE,
-    )
-    row_mean = (row_sum / model_width)[:, None]
-    row_var = (row_square / model_width)[:, None] - row_mean * row_mean
+    mixed_rows = rows_summed_over_cache(mixed_part)
+    row_mean = jnp.mean(mixed_rows, axis=1, keepdims=True)
+    centered = mixed_rows - row_mean
+    row_var = jnp.mean(centered * centered, axis=1, keepdims=True)
     inverse = 1.0 / jnp.sqrt(row_var + 1e-05)
-    normed = (mixed_block - row_mean) * inverse
-    layer_block = (gate_float * normed).astype(jnp.bfloat16)
-    back_cross = inverse[:, 0] * (back_mixed - row_mean[:, 0] * back_sum)
-    grad_block = inverse * (
-        back - (back_sum / model_width)[:, None] - normed * (back_cross / model_width)[:, None]
-    )
-    mixed_grad = collect_cache(grad_block.astype(jnp.bfloat16), 1)
+    normed = centered * inverse
+    gate_float = gate_rows.astype(jnp.float32)
+    layer_rows = (gate_float * normed).astype(jnp.bfloat16)
+    back = grad_rows_in.astype(jnp.float32) * gate_float
+    grad_rows = inverse * (
+        back
+        - jnp.mean(back, axis=1, keepdims=True)
+        - normed * jnp.mean(back * normed, axis=1, keepdims=True)
+    )
+    mixed_grad, layer_block = rows_to_everyone(grad_rows.astype(jnp.bfloat16), layer_rows)
     query_part = backward_part(keys, values_all, weighted_slope, mixed_grad, HEADS)
     query_grad = rounded_sum_over_cache(query_part, 1)
     pre_grad = (query_grad * silu_slope(query_pre)).astype(jnp.bfloat16)

time: 262 us -> 303 us (1.16)
  blocking collectives: 178 us -> 121 us
  local copies, waits for them, and re-layouts: 14.7 us -> 55.9 us
  waiting for transfers between devices: 16.6 us -> 57.8 us
  starting transfers between devices: 17.8 us -> 26.1 us
  other arithmetic: 15.3 us -> 20.8 us
    all_to_all x0 -> x3, waiting for transfers between devices: none -> 50.9 us  [the longest x1 26.8 us: rows_summed_over_cache(): return lax.all_to_all(on_chip, CHIPS, 0, 0, tiled=True).sum(axis=0)]
    all_to_all x3 -> x1, blocking collectives: 61.2 us -> 29.6 us  [sent_to_all(): return lax.all_to_all(copies, axis, split_axis=0, concat_axis=0, tiled=True)]
    all_to_all x0 -> x3, starting transfers between devices: none -> 21.5 us  [the longest x1 13.4 us: tokens_and_rows(): across = lax.all_to_all(outgoing, CHIPS, 0, 0, tiled=True)]
    unnamed x48 -> x63, local copies, waits for them, and re-layouts: 3.29 us -> 21.4 us
    all_to_all x3 -> x1, blocking collectives: 22 us -> 7.06 us  [collect_cache(): lax.all_to_all(jnp.broadcast_to(across, (cores, *across.shape)), CORE, 0,...]
    all_to_all x2 -> x1, starting transfers between devices: 17.8 us -> 4.53 us  [collect_cache(): lax.all_to_all(jnp.broadcast_to(array, (chips, *array.shape)), CHIPS, 0,...]
    all_to_all x2 -> x1, waiting for transfers between devices: 16.6 us -> 6.9 us  [collect_cache(): lax.all_to_all(jnp.broadcast_to(array, (chips, *array.shape)), CHIPS, 0,...]
    transpose x1 -> x8, local copies, waits for them, and re-layouts: 0.14 us -> 8.93 us  [the longest x1 3.06 us: product(): return jnp.einsum(form, left, right, preferred_element_type=jnp.float32)]
  transfers between devices with their start and end apart: 2 -> 4, of which waited for: 2 -> 4; matrix products, arithmetic and copies ran while one was open for 5% -> 3% of each run, Pallas kernels for 0% -> 0%
where the time goes in v4:
time: 303 us; the launch traced here: 300 us
  blocking collectives  121 us (40%)
  waiting for transfers between devices  57.8 us (19%)
  local copies, waits for them, and re-layouts  55.9 us (18%)
  starting transfers between devices  26.1 us (9%)
  other arithmetic  20.8 us (7%)
  matrix products  16.2 us (5%)
    all_to_all x1, blocking collectives, sent_to_all(): return lax.all_to_all(copies, axis, split_axis=0, concat_axis=0, tiled=True)  29.6 us
    all_to_all x1, waiting for transfers between devices, rows_summed_over_cache(): return lax.all_to_all(on_chip, CHIPS, 0, 0, tiled=True).sum(axis=0)  26.8 us
    all_to_all x1, blocking collectives, rows_to_everyone(): across = lax.all_to_all(outgoing, CHIPS, 0, 0, tiled=True)  24.7 us
    unnamed x63, local copies, waits for them, and re-layouts  21.4 us
    all_to_all x1, blocking collectives, rounded_sum_over_cache(): arrived = lax.all_to_all(pair_sum, CHIPS, 0, 0, tiled=True)  18.6 us
    all_to_all x1, blocking collectives, sent_and_summed(): tiles = lax.all_to_all(split_up(array, dim, peers), axis, 0, 0, tiled=True)  16.4 us
    all_to_all x1, waiting for transfers between devices, tokens_and_rows(): across = lax.all_to_all(outgoing, CHIPS, 0, 0, tiled=True)  15.1 us
    dot_general x3, matrix products, product(): return jnp.einsum(form, left, right, preferred_element_type=jnp.float32)  14.9 us
  transfers between devices with their start and end apart: 4, of which 4 were waited for; matrix products, arithmetic and copies ran while one was open for 3% of the time, Pallas kernels for 0%

profile of v4, /device:TPU:1, one launch (start us, length us, event | category | flops | bytes accessed | tf_op | source)
XLA Modules:
  0.0 300.1 jit_solution(9067518957967891755)
XLA Ops:
  6.6 13.4 %all-to-all-start = ((bf16[16,2,9216]{2,1,0:T(2,128)(2,1)}), bf16[16,2,9216]{2,1,0:T(2,128)(2,1)S(1)}, u32[]{:S(2)}, u32[]{:S(2)}) async-start(bf16[16,2,9216]{2,1,0:T(2,128)(2,1)} %reshape.314), calls=%async_computation | async-start | bytes 1179648 | tf_op jit(solution)/shard_map/all_to_all | solution.py:100
  21.4 15.1 %all-to-all-done = bf16[16,2,9216]{2,1,0:T(2,128)(2,1)S(1)} async-done(((bf16[16,2,9216]{2,1,0:T(2,128)(2,1)}), bf16[16,2,9216]{2,1,0:T(2,128)(2,1)S(1)}, u32[]{:S(2)}, u32[]{:S(2)}) %all-to-all-start) | async-done | bytes 589856 | tf_op jit(solution)/shard_map/all_to_all | solution.py:100
  38.0 7.0 %all_to_all.80 = bf16[2,16,17408]{2,1,0:T(8,128)(2,1)S(1)} all-to-all(bf16[2,16,17408]{2,1,0:T(8,128)(2,1)S(1)} %pad_maximum_fusion.7), channel_id=1, replica_groups=mesh['cache_0'=2,'cache_1'=8,'cache_2'=2,'dp_0'=8,'dp_1'=2] {'cache_2'}, dimensions={0} | all-to-all | bytes 2228224 | tf_op jit(solution)/shard_map/all_to_all | solution.py:110
  48.7 3.0 %reshape.293 = bf16[32,256,64]{2,1,0:T(8,128)(2,1)S(1)} reshape(bf16[32,16384]{1,0:T(8,128)(2,1)} %slice.44) | data formatting | bytes 2097152 | tf_op jit(solution)/shard_map/reshape | solution.py:112
  54.4 4.5 %all-to-all-start.2 = ((bf16[16,256,64]{1,2,0:T(8,128)(2,1)}), bf16[16,256,64]{1,2,0:T(8,128)(2,1)}, u32[]{:S(2)}, u32[]{:S(2)}) async-start(bf16[16,256,64]{1,2,0:T(8,128)(2,1)} %broadcast_in_dim.86), calls=%async_computation.2 | async-start | bytes 1048576 | tf_op jit(solution)/shard_map/all_to_all | solution.py:60
  64.3 2.9 fusion.3
  67.2 6.9 %all-to-all-done.2 = bf16[16,256,64]{1,2,0:T(8,128)(2,1)} async-done(((bf16[16,256,64]{1,2,0:T(8,128)(2,1)}), bf16[16,256,64]{1,2,0:T(8,128)(2,1)}, u32[]{:S(2)}, u32[]{:S(2)}) %all-to-all-start.2) | async-done | bytes 524320 | tf_op jit(solution)/shard_map/all_to_all | solution.py:60
  75.3 7.1 %all_to_all.81 = bf16[2,16,256,64]{2,3,1,0:T(8,128)(2,1)S(1)} all-to-all(bf16[2,16,256,64]{2,3,1,0:T(8,128)(2,1)S(1)} %broadcast_in_dim.87), channel_id=1, replica_groups=mesh['cache_0'=2,'cache_1'=8,'cache_2'=2,'dp_0'=8,'dp_1'=2] {'cache_2'}, dimensions={0} | all-to-all | bytes 2097152 | tf_op jit(solution)/shard_map/all_to_all | solution.py:64
  83.8 3.3 %copy-done.2 = f32[16,256,520]{1,2,0:T(8,128)} copy-done((f32[16,256,520]{1,2,0:T(8,128)}, f32[16,256,520]{1,2,0:T(8,128)S(1)}, u32[]{:S(2)}) %copy-start.2) | copy-done | bytes 8519704
  87.0 4.4 %fusion.7 = f32[256,16,128]{0,2,1:T(8,128)} fusion(f32[16,256,520]{1,2,0:T(8,128)S(1)} %fusion.9, pred[256,520]{0,1:T(8,128)(4,1)S(1)} %pad_add_fusion, bf16[8,16,128]{2,0,1:T(8,128)(2,1)S(1)} %bitcast.138, bf16[512,16,128]{2,0,1:T(8,128)(2,1)S(1)} %copy-done.6), kind=kOutput, calls=%fused_computation.14 | convolution fusion | flops 564428800 | bytes 12879872 | tf_op jit(solution)/shard_map/hqk,khd->qhd/dot_general | solution.py:179
  91.5 3.1 %copy.167 = f32[256,16,128]{2,1,0:T(8,128)} copy(f32[256,16,128]{0,2,1:T(8,128)} %fusion.7) | data formatting | bytes 4194304 | tf_op jit(solution)/shard_map/hqk,khd->qhd/transpose | solution.py:179
  99.0 6.2 %all_to_all.82 = f32[2,16,8,2048]{3,2,1,0:T(8,128)} all-to-all(f32[2,16,8,2048]{3,2,1,0:T(8,128)S(1)} %copy.168), channel_id=1, replica_groups=mesh['cache_0'=2,'cache_1'=8,'cache_2'=2,'dp_0'=8,'dp_1'=2] {'cache_2'}, dimensions={0} | all-to-all | bytes 4194304 | tf_op jit(solution)/shard_map/all_to_all | solution.py:121
  108.1 4.6 %all-to-all-start.5 = ((f32[16,8,2048]{2,1,0:T(8,128)}), f32[16,8,2048]{2,1,0:T(8,128)}, u32[]{:S(2)}, u32[]{:S(2)}) async-start(f32[16,8,2048]{2,1,0:T(8,128)} %reduce_sum.116), calls=%async_computation.5 | async-start | bytes 2097152 | tf_op jit(solution)/shard_map/all_to_all | solution.py:122
  113.0 26.8 %all-to-all-done.5 = f32[16,8,2048]{2,1,0:T(8,128)} async-done(((f32[16,8,2048]{2,1,0:T(8,128)}), f32[16,8,2048]{2,1,0:T(8,128)}, u32[]{:S(2)}, u32[]{:S(2)}) %all-to-all-start.5) | async-done | bytes 1048608 | tf_op jit(solution)/shard_map/all_to_all | solution.py:122
  152.6 24.7 %all_to_all.83 = bf16[16,2,8704]{2,1,0:T(2,128)(2,1)} all-to-all(bf16[16,2,8704]{2,1,0:T(2,128)(2,1)} %reshape.316), channel_id=1, replica_groups=mesh['cache_0'=2,'cache_1'=8,'cache_2'=2,'dp_0'=8,'dp_1'=2] {'cache_0','..., dimensions={0} | all-to-all | bytes 1114112 | tf_op jit(solution)/shard_map/all_to_all | solution.py:139
  177.3 3.5 %reshape.317 = bf16[16,1,17408]{2,1,0:T(2,128)(2,1)} reshape(bf16[16,2,8704]{2,1,0:T(2,128)(2,1)} %all_to_all.83) | data formatting | bytes 1114112
  184.5 6.9 %all_to_all.84 = bf16[2,16,16896]{2,1,0:T(8,128)(2,1)S(1)} all-to-all(bf16[2,16,16896]{2,1,0:T(8,128)(2,1)S(1)} %pad_maximum_fusion.8), channel_id=1, replica_groups=mesh['cache_0'=2,'cache_1'=8,'cache_2'=2,'dp_0'=8,'dp_1'=2] {'cache_2'}, dimensions={0} | all-to-all | bytes 2162688 | tf_op jit(solution)/shard_map/all_to_all | solution.py:149
  200.5 9.2 %fusion.8 = bf16[16,128,256]{2,1,0:T(8,128)(2,1)} fusion(f32[16,256,520]{1,2,0:T(8,128)} %copy-done.2, pred[256,520]{0,1:T(8,128)(4,1)S(1)} %copy-done.9, bf16[8,16,128]{2,0,1:T(8,128)(2,1)S(1)} %bitcast.135, bf16[512,16,128]{2,0,1:T(8,128)(2,1)S(1)} %fusion.2, bf16[8,16,128]{2,0,1:T(8,128)(2,1)S(1)} %bitcast.139, bf16[512,16,128]{2,0,1:T(8,128)(2,1)} %fusion.3, ...), kind=kOutput, calls=%fused_computation.15 | convolution fusion | flops 1125122048 | bytes 15009792 | tf_op jit(solution)/shard_map/hqk,khd->qhd/dot_general | solution.py:179
  211.0 4.8 %all_to_all.85 = bf16[2,16,256,64]{2,3,1,0:T(8,128)(2,1)S(1)} all-to-all(bf16[2,16,256,64]{2,3,1,0:T(8,128)(2,1)S(1)} %copy.176), channel_id=1, replica_groups=mesh['cache_0'=2,'cache_1'=8,'cache_2'=2,'dp_0'=8,'dp_1'=2] {'cache_2'}, dimensions={0} | all-to-all | bytes 2097152 | tf_op jit(solution)/shard_map/all_to_all | solution.py:83
  216.1 18.6 %all_to_all.86 = bf16[16,256,64]{1,2,0:T(8,128)(2,1)S(1)} all-to-all(bf16[16,256,64]{1,2,0:T(8,128)(2,1)S(1)} %reduce_sum.124), channel_id=1, replica_groups=mesh['cache_0'=2,'cache_1'=8,'cache_2'=2,'dp_0'=8,'dp_1'=2] {'cache_0','..., dimensions={0} | all-to-all | bytes 1048576 | tf_op jit(solution)/shard_map/all_to_all | solution.py:85
  235.3 16.4 %all_to_all.87 = bf16[16,128,64]{1,2,0:T(8,128)(2,1)S(1)} all-to-all(bf16[16,128,64]{1,2,0:T(8,128)(2,1)S(1)} %bitcast.123), channel_id=1, replica_groups=mesh['cache_0'=2,'cache_1'=8,'cache_2'=2,'dp_0'=8,'dp_1'=2] {'dp_0','dp_1'}, dimensions={0} | all-to-all | bytes 524288 | tf_op jit(solution)/shard_map/all_to_all | solution.py:163
  253.1 29.6 %all_to_all.88 = f32[512,1,1]{2,1,0:T(1,128)S(1)} all-to-all(f32[512,1,1]{2,1,0:T(1,128)S(1)} %broadcast_in_dim.91), channel_id=1, replica_groups=mesh['cache_0'=2,'cache_1'=8,'cache_2'=2,'dp_0'=8,'dp_1'=2] {'cache_0','..., dimensions={0} | all-to-all | bytes 4096 | tf_op jit(solution)/shard_map/all_to_all | solution.py:31
  286.0 3.5 %all-to-all-start.12 = ((bf16[16,128,64]{1,2,0:T(8,128)(2,1)}), bf16[16,128,64]{1,2,0:T(8,128)(2,1)S(1)}, u32[]{:S(2)}, u32[]{:S(2)}) async-start(bf16[16,128,64]{1,2,0:T(8,128)(2,1)} %broadcast_in_dim.92), calls=%async_computation.12 | async-start | bytes 524288 | tf_op jit(solution)/shard_map/all_to_all | solution.py:31
  290.4 8.9 %all-to-all-done.12 = bf16[16,128,64]{1,2,0:T(8,128)(2,1)S(1)} async-done(((bf16[16,128,64]{1,2,0:T(8,128)(2,1)}), bf16[16,128,64]{1,2,0:T(8,128)(2,1)S(1)}, u32[]{:S(2)}, u32[]{:S(2)}) %all-to-all-start.12) | async-done | bytes 262176 | tf_op jit(solution)/shard_map/all_to_all | solution.py:31
  (146 shorter events, 63.7 us)
Async XLA Ops:
  0.6 52.0 %copy-start = (bf16[2048,64]{0,1:T(8,128)(2,1)S(1)}, bf16[2048,64]{0,1:T(8,128)(2,1)}, u32[]{:S(2)}) copy-start(bf16[2048,64]{0,1:T(8,128)(2,1)} %param.18) | copy-start | bytes 786436
  3.7 16.9 %copy-start.17 = (s32[1,256]{1,0:T(1,128)S(1)}, s32[1,256]{1,0:T(1,128)}, u32[]{:S(2)}) copy-start(s32[1,256]{1,0:T(1,128)} %param.29) | copy-start | bytes 3076
  3.7 17.5 %copy-start.18 = (s32[2]{0:T(128)S(1)}, s32[2]{0:T(128)}, u32[]{:S(2)}) copy-start(s32[2]{0:T(128)} %param.28) | copy-start | bytes 28
  6.6 30.0 %all-to-all-start = ((bf16[16,2,9216]{2,1,0:T(2,128)(2,1)}), bf16[16,2,9216]{2,1,0:T(2,128)(2,1)S(1)}, u32[]{:S(2)}, u32[]{:S(2)}) async-start(bf16[16,2,9216]{2,1,0:T(2,128)(2,1)} %reshape.314), calls=%async_computation | async-start | bytes 1179648 | tf_op jit(solution)/shard_map/all_to_all | solution.py:100
  52.6 7.1 %copy-start.15 = (f32[2,8,16]{2,1,0:T(8,128)S(1)}, f32[2,8,16]{2,1,0:T(8,128)}, u32[]{:S(2)}) copy-start(f32[2,8,16]{2,1,0:T(8,128)} %param.24) | copy-start | bytes 3076
  52.6 7.2 %copy-start.16 = (f32[2,8,16]{2,1,0:T(8,128)S(1)}, f32[2,8,16]{2,1,0:T(8,128)}, u32[]{:S(2)}) copy-start(f32[2,8,16]{2,1,0:T(8,128)} %param.25) | copy-start | bytes 3076
  52.6 7.7 %copy-start.4 = (bf16[2,256,2048]{2,1,0:T(8,128)(2,1)S(1)}, bf16[2,256,2048]{2,1,0:T(8,128)(2,1)}, u32[]{:S(2)}) copy-start(bf16[2,256,2048]{2,1,0:T(8,128)(2,1)} %param.22) | copy-start | bytes 6291460
  54.4 19.7 %all-to-all-start.2 = ((bf16[16,256,64]{1,2,0:T(8,128)(2,1)}), bf16[16,256,64]{1,2,0:T(8,128)(2,1)}, u32[]{:S(2)}, u32[]{:S(2)}) async-start(bf16[16,256,64]{1,2,0:T(8,128)(2,1)} %broadcast_in_dim.86), calls=%async_computation.2 | async-start | bytes 1048576 | tf_op jit(solution)/shard_map/all_to_all | solution.py:60
  62.5 21.2 %copy-start.8 = (pred[256,520]{0,1:T(8,128)(4,1)}, pred[256,520]{0,1:T(8,128)(4,1)S(1)}, u32[]{:S(2)}) copy-start(pred[256,520]{0,1:T(8,128)(4,1)S(1)} %pad_add_fusion) | copy-start | bytes 399364
  75.3 7.2 %copy-start.10 = (bf16[8,2048]{1,0:T(8,128)(2,1)S(1)}, bf16[8,2048]{1,0:T(8,128)(2,1)}, u32[]{:S(2)}) copy-start(bf16[8,2048]{1,0:T(8,128)(2,1)} %param.26) | copy-start | bytes 98308
  82.5 4.6 %copy-start.6 = (bf16[512,16,128]{2,0,1:T(8,128)(2,1)S(1)}, bf16[512,16,128]{2,0,1:T(8,128)(2,1)}, u32[]{:S(2)}) copy-start(bf16[512,16,128]{2,0,1:T(8,128)(2,1)} %fusion.3) | copy-start | bytes 6291460
  82.5 4.6 %copy-start.19 = (bf16[8,2048]{1,0:T(8,128)(2,1)S(1)}, bf16[8,2048]{1,0:T(8,128)(2,1)}, u32[]{:S(2)}) copy-start(bf16[8,2048]{1,0:T(8,128)(2,1)} %param.27) | copy-start | bytes 98308
  105.2 7.5 %slice-start = ((bf16[32,17408]{1,0:T(8,128)(2,1)}), bf16[32,1024]{1,0:T(8,128)(2,1)S(1)}, s32[]{:S(2)}) async-start(bf16[32,17408]{1,0:T(8,128)(2,1)} %copy-done.3), calls=%async_computation.13 | async-start | bytes 131072 | tf_op jit(solution)/shard_map/slice | solution.py:113
  108.1 31.7 %all-to-all-start.5 = ((f32[16,8,2048]{2,1,0:T(8,128)}), f32[16,8,2048]{2,1,0:T(8,128)}, u32[]{:S(2)}, u32[]{:S(2)}) async-start(f32[16,8,2048]{2,1,0:T(8,128)} %reduce_sum.116), calls=%async_computation.5 | async-start | bytes 2097152 | tf_op jit(solution)/shard_map/all_to_all | solution.py:122
  195.8 4.7 %copy-start.9 = (pred[256,520]{0,1:T(8,128)(4,1)S(1)}, pred[256,520]{0,1:T(8,128)(4,1)}, u32[]{:S(2)}) copy-start(pred[256,520]{0,1:T(8,128)(4,1)} %copy-done.8) | copy-start | bytes 399364
  195.8 4.7 %copy-start.11 = (bf16[8,2048]{1,0:T(8,128)(2,1)S(1)}, bf16[8,2048]{1,0:T(8,128)(2,1)}, u32[]{:S(2)}) copy-start(bf16[8,2048]{1,0:T(8,128)(2,1)} %param.26) | copy-start | bytes 98308
  195.8 4.7 %copy-start.20 = (bf16[8,2048]{1,0:T(8,128)(2,1)S(1)}, bf16[8,2048]{1,0:T(8,128)(2,1)}, u32[]{:S(2)}) copy-start(bf16[8,2048]{1,0:T(8,128)(2,1)} %param.27) | copy-start | bytes 98308
  211.0 23.8 %copy-start.7 = (f32[256,64]{0,1:T(8,128)S(1)}, f32[256,64]{0,1:T(8,128)}, u32[]{:S(2)}) copy-start(f32[256,64]{0,1:T(8,128)} %get-tuple-element.52) | copy-start | bytes 196612
  234.7 49.9 %copy-start.12 = (f32[128,64]{0,1:T(8,128)S(1)}, f32[128,64]{0,1:T(8,128)}, u32[]{:S(2)}) copy-start(f32[128,64]{0,1:T(8,128)} %param.19) | copy-start | bytes 98308
  234.7 49.9 %copy-start.13 = (f32[128,64]{0,1:T(8,128)S(1)}, f32[128,64]{0,1:T(8,128)}, u32[]{:S(2)}) copy-start(f32[128,64]{0,1:T(8,128)} %param.20) | copy-start | bytes 98308
  234.7 49.9 %copy-start.14 = (f32[128,64]{0,1:T(8,128)S(1)}, f32[128,64]{0,1:T(8,128)}, u32[]{:S(2)}) copy-start(f32[128,64]{0,1:T(8,128)} %param.21) | copy-start | bytes 98308
  234.8 54.7 %slice-start.1 = ((bf16[32,16896]{1,0:T(8,128)(2,1)}), bf16[32,512]{1,0:T(8,128)(2,1)S(1)}, s32[]{:S(2)}) async-start(bf16[32,16896]{1,0:T(8,128)(2,1)} %reshape.302), calls=%async_computation.14 | async-start | bytes 65536 | tf_op jit(solution)/shard_map/slice | solution.py:152
  234.8 65.2 %copy-start.1 = (bf16[2048,64]{0,1:T(8,128)(2,1)S(1)}, bf16[2048,64]{0,1:T(8,128)(2,1)}, u32[]{:S(2)}) copy-start(bf16[2048,64]{0,1:T(8,128)(2,1)} %param.18) | copy-start | bytes 786436
  286.0 13.3 %all-to-all-start.12 = ((bf16[16,128,64]{1,2,0:T(8,128)(2,1)}), bf16[16,128,64]{1,2,0:T(8,128)(2,1)S(1)}, u32[]{:S(2)}, u32[]{:S(2)}) async-start(bf16[16,128,64]{1,2,0:T(8,128)(2,1)} %broadcast_in_dim.92), calls=%async_computation.12 | async-start | bytes 524288 | tf_op jit(solution)/shard_map/all_to_all | solution.py:31
  (3 other events, 5.9 us)

commit v5 on v3

--- a/solution.py
+++ b/solution.py
@@ -84,6 +84,29 @@
     pair_sum = jnp.sum(on_chip.astype(jnp.float32), axis=0).astype(jnp.bfloat16)
     arrived = lax.all_to_all(pair_sum, CHIPS, 0, 0, tiled=True)
     return jnp.sum(arrived.astype(jnp.float32), axis=0)
+
+
+def rows_summed_over_cache(array):
+    chips, cores = (lax.axis_size(CHIPS), lax.axis_size(CORE))
+    tiles = array.reshape(chips, cores, array.shape[0] // (chips * cores), array.shape[1])
+    on_chip = lax.all_to_all(jnp.swapaxes(tiles, 0, 1), CORE, 0, 0, tiled=True).sum(axis=0)
+    return lax.all_to_all(on_chip, CHIPS, 0, 0, tiled=True).sum(axis=0)
+
+
+def columns_to_rows(array):
+    peers = lax.axis_size(CACHE)
+    lead, rows, cols = array.shape
+    tiles = array.reshape(lead, peers, rows // peers, cols).transpose(1, 0, 2, 3)
+    arrived = lax.all_to_all(tiles, CACHE, 0, 0, tiled=True)
+    return arrived.transpose(1, 2, 0, 3).reshape(lead, rows // peers, peers * cols)
+
+
+def rows_to_columns(array):
+    peers = lax.axis_size(CACHE)
+    rows, width = array.shape
+    tiles = array.reshape(rows, peers, width // peers).transpose(1, 0, 2)
+    arrived = lax.all_to_all(tiles, CACHE, 0, 0, tiled=True)
+    return arrived.reshape(peers * rows, width // peers)
 
 
 def collect(array, axis, dim):
@@ -187,10 +210,14 @@
     model_width = query_weight.shape[0]
     shard_index = lax.axis_index(CACHE)
     features = collect_cache(tokens, 1)
+    gate_rows, grad_rows_in = columns_to_rows(jnp.stack([gate_values, output_grad]))
     query_pre = jnp.dot(features, query_weight, preferred_element_type=jnp.float32) / math.sqrt(
         model_width
     )
     query_block = jax.nn.silu(query_pre).astype(jnp.bfloat16)
+    query_block, gate_rows, grad_rows_in = lax.optimization_barrier(
+        (query_block, gate_rows, grad_rows_in)
+    )
     queries = collect_cache(query_block, 1)
     user_ids = segments[0]
     hist_rows = key_codes.shape[1]
@@ -199,28 +226,21 @@
     values_all = jnp.concatenate([dequantize(value_codes, value_scales), span_values], axis=0)
     mask = key_mask(user_ids, lengths, shard_index, hist_rows, span_rows)
     mixed_part, weighted_slope = forward_part(queries, keys, values_all, mask, HEADS)
-    gate_float = gate_values.astype(jnp.float32)
-    mixed_block = summed_over_cache(mixed_part, 1)
-    back = output_grad.astype(jnp.float32) * gate_float
-    row_sum, row_square, back_sum, back_mixed = packed_total(
-        (
-            jnp.sum(mixed_block, axis=1),
-            jnp.sum(mixed_block * mixed_block, axis=1),
-            jnp.sum(back, axis=1),
-            jnp.sum(back * mixed_block, axis=1),
-        ),
-        CACHE,
-    )
-    row_mean = (row_sum / model_width)[:, None]
-    row_var = (row_square / model_width)[:, None] - row_mean * row_mean
+    mixed_rows = rows_summed_over_cache(mixed_part)
+    row_mean = jnp.mean(mixed_rows, axis=1, keepdims=True)
+    centered = mixed_rows - row_mean
+    row_var = jnp.mean(centered * centered, axis=1, keepdims=True)
     inverse = 1.0 / jnp.sqrt(row_var + 1e-05)
-    normed = (mixed_block - row_mean) * inverse
-    layer_block = (gate_float * normed).astype(jnp.bfloat16)
-    back_cross = inverse[:, 0] * (back_mixed - row_mean[:, 0] * back_sum)
-    grad_block = inverse * (
-        back - (back_sum / model_width)[:, None] - normed * (back_cross / model_width)[:, None]
-    )
-    mixed_grad = collect_cache(grad_block.astype(jnp.bfloat16), 1)
+    normed = centered * inverse
+    gate_float = gate_rows.astype(jnp.float32)
+    layer_block = rows_to_columns((gate_float * normed).astype(jnp.bfloat16))
+    back = grad_rows_in.astype(jnp.float32) * gate_float
+    grad_rows = inverse * (
+        back
+        - jnp.mean(back, axis=1, keepdims=True)
+        - normed * jnp.mean(back * normed, axis=1, keepdims=True)
+    )
+    mixed_grad = collect_cache(grad_rows.astype(jnp.bfloat16), 0)
     query_part = backward_part(keys, values_all, weighted_slope, mixed_grad, HEADS)
     query_grad = rounded_sum_over_cache(query_part, 1)
     pre_grad = (query_grad * silu_slope(query_pre)).astype(jnp.bfloat16)

time: 262 us -> 291 us (1.11)
  blocking collectives: 178 us -> 121 us
  waiting for transfers between devices: 16.6 us -> 55.3 us
  starting transfers between devices: 17.8 us -> 45.7 us
  local copies, waits for them, and re-layouts: 14.7 us -> 32.5 us
    all_to_all x5 -> x2, blocking collectives: 98 us -> 36.8 us  [the longest x1 30.5 us: rows_summed_over_cache(): return lax.all_to_all(on_chip, CHIPS, 0, 0, tiled=True).sum(axis=0)]
    all_to_all x0 -> x4, waiting for transfers between devices: none -> 41.5 us  [the longest x2 25.1 us: sent_to_all(): return lax.all_to_all(copies, axis, split_axis=0, concat_axis=0, tiled=True)]
    all_to_all x0 -> x4, starting transfers between devices: none -> 37.6 us  [the longest x2 17.7 us: sent_to_all(): return lax.all_to_all(copies, axis, split_axis=0, concat_axis=0, tiled=True)]
    all_to_all x2, starting transfers between devices: 17.8 us -> 8.12 us  [collect_cache(): lax.all_to_all(jnp.broadcast_to(array, (chips, *array.shape)), CHIPS, 0,...]
    unnamed x48 -> x58, local copies, waits for them, and re-layouts: 3.29 us -> 11.7 us
    all_to_all x1, blocking collectives: 16.8 us -> 22.1 us  [collect_cache(): lax.all_to_all(jnp.broadcast_to(array, (chips, *array.shape)), CHIPS, 0,...]
    transpose x1 -> x5, local copies, waits for them, and re-layouts: 0.14 us -> 4.94 us  [the longest x1 3.06 us: product(): return jnp.einsum(form, left, right, preferred_element_type=jnp.float32)]
    another operation x0 -> x6, local copies, waits for them, and re-layouts: none -> 4.22 us  [the longest x1 2.71 us: rows_summed_over_cache(): array.reshape(chips, cores, array.shape[0] // (chips * cores), array.shap...]
  transfers between devices with their start and end apart: 2 -> 6, of which waited for: 2 -> 6; matrix products, arithmetic and copies ran while one was open for 5% -> 6% of each run, Pallas kernels for 0% -> 0%
where the time goes in v5:
time: 291 us; the launch traced here: 289 us
  blocking collectives  121 us (42%)
  waiting for transfers between devices  55.3 us (19%)
  starting transfers between devices  45.7 us (16%)
  local copies, waits for them, and re-layouts  32.5 us (11%)
  matrix products  17.8 us (6%)
  other arithmetic  14.9 us (5%)
    all_to_all x1, blocking collectives, rows_summed_over_cache(): return lax.all_to_all(on_chip, CHIPS, 0, 0, tiled=True).sum(axis=0)  30.5 us
    all_to_all x2, waiting for transfers between devices, sent_to_all(): return lax.all_to_all(copies, axis, split_axis=0, concat_axis=0, tiled=True)  25.1 us
    all_to_all x3, blocking collectives, collect_cache(): lax.all_to_all(jnp.broadcast_to(across, (cores, *across.shape)), CORE, 0,...  22.1 us
    all_to_all x1, blocking collectives, collect_cache(): lax.all_to_all(jnp.broadcast_to(array, (chips, *array.shape)), CHIPS, 0,...  22.1 us
    all_to_all x1, blocking collectives, rounded_sum_over_cache(): arrived = lax.all_to_all(pair_sum, CHIPS, 0, 0, tiled=True)  19.3 us
    all_to_all x2, starting transfers between devices, sent_to_all(): return lax.all_to_all(copies, axis, split_axis=0, concat_axis=0, tiled=True)  17.7 us
    dot_general x3, matrix products, product(): return jnp.einsum(form, left, right, preferred_element_type=jnp.float32)  16.4 us
    all_to_all x1, blocking collectives, sent_and_summed(): tiles = lax.all_to_all(split_up(array, dim, peers), axis, 0, 0, tiled=True)  16.4 us
  transfers between devices with their start and end apart: 6, of which 6 were waited for; matrix products, arithmetic and copies ran while one was open for 6% of the time, Pallas kernels for 0%

profile of v5, /device:TPU:1, one launch (start us, length us, event | category | flops | bytes accessed | tf_op | source)
XLA Modules:
  0.0 289.3 jit_solution(2470901701927357154)
XLA Ops:
  3.3 14.4 %all-to-all-start.2 = ((bf16[32,2,512]{2,1,0:T(2,128)(2,1)}), bf16[32,2,512]{2,1,0:T(2,128)(2,1)S(1)}, u32[]{:S(2)}, u32[]{:S(2)}) async-start(bf16[32,2,512]{2,1,0:T(2,128)(2,1)} %reshape.172), calls=%async_computation.2 | async-start | bytes 131072 | tf_op jit(solution)/shard_map/all_to_all | solution.py:100
  17.7 9.6 %all-to-all-done.2 = bf16[32,2,512]{2,1,0:T(2,128)(2,1)S(1)} async-done(((bf16[32,2,512]{2,1,0:T(2,128)(2,1)}), bf16[32,2,512]{2,1,0:T(2,128)(2,1)S(1)}, u32[]{:S(2)}, u32[]{:S(2)}) %all-to-all-start.2) | async-done | bytes 65568 | tf_op jit(solution)/shard_map/all_to_all | solution.py:100
  28.9 3.6 %all-to-all-start = ((bf16[16,256,64]{1,2,0:T(8,128)(2,1)}), bf16[16,256,64]{1,2,0:T(8,128)(2,1)S(1)}, u32[]{:S(2)}, u32[]{:S(2)}) async-start(bf16[16,256,64]{1,2,0:T(8,128)(2,1)} %broadcast_in_dim.68), calls=%async_computation | async-start | bytes 1048576 | tf_op jit(solution)/shard_map/all_to_all | solution.py:60
  37.2 9.5 %all-to-all-done = bf16[16,256,64]{1,2,0:T(8,128)(2,1)S(1)} async-done(((bf16[16,256,64]{1,2,0:T(8,128)(2,1)}), bf16[16,256,64]{1,2,0:T(8,128)(2,1)S(1)}, u32[]{:S(2)}, u32[]{:S(2)}) %all-to-all-start) | async-done | bytes 524320 | tf_op jit(solution)/shard_map/all_to_all | solution.py:60
  46.8 8.0 %all_to_all.76 = bf16[2,16,256,64]{2,3,1,0:T(8,128)(2,1)S(1)} all-to-all(bf16[2,16,256,64]{2,3,1,0:T(8,128)(2,1)S(1)} %broadcast_in_dim.69), channel_id=1, replica_groups=mesh['cache_0'=2,'cache_1'=8,'cache_2'=2,'dp_0'=8,'dp_1'=2] {'cache_2'}, dimensions={0} | all-to-all | bytes 2097152 | tf_op jit(solution)/shard_map/all_to_all | solution.py:64
  56.7 4.5 %all-to-all-start.3 = ((bf16[16,256,64]{1,2,0:T(8,128)(2,1)}), bf16[16,256,64]{1,2,0:T(8,128)(2,1)}, u32[]{:S(2)}, u32[]{:S(2)}) async-start(bf16[16,256,64]{1,2,0:T(8,128)(2,1)} %broadcast_in_dim.73), calls=%async_computation.3 | async-start | bytes 1048576 | tf_op jit(solution)/shard_map/all_to_all | solution.py:60
  72.1 4.4 %all-to-all-done.3 = bf16[16,256,64]{1,2,0:T(8,128)(2,1)} async-done(((bf16[16,256,64]{1,2,0:T(8,128)(2,1)}), bf16[16,256,64]{1,2,0:T(8,128)(2,1)}, u32[]{:S(2)}, u32[]{:S(2)}) %all-to-all-start.3) | async-done | bytes 524320 | tf_op jit(solution)/shard_map/all_to_all | solution.py:60
  77.6 7.0 %all_to_all.77 = bf16[2,16,256,64]{2,3,1,0:T(8,128)(2,1)S(1)} all-to-all(bf16[2,16,256,64]{2,3,1,0:T(8,128)(2,1)S(1)} %broadcast_in_dim.74), channel_id=1, replica_groups=mesh['cache_0'=2,'cache_1'=8,'cache_2'=2,'dp_0'=8,'dp_1'=2] {'cache_2'}, dimensions={0} | all-to-all | bytes 2097152 | tf_op jit(solution)/shard_map/all_to_all | solution.py:64
  86.1 3.2 %copy-done.1 = f32[16,256,520]{1,2,0:T(8,128)} copy-done((f32[16,256,520]{1,2,0:T(8,128)}, f32[16,256,520]{1,2,0:T(8,128)S(1)}, u32[]{:S(2)}) %copy-start.1) | copy-done | bytes 8519704
  89.3 4.4 %fusion.7 = f32[256,16,128]{0,2,1:T(8,128)} fusion(f32[16,256,520]{1,2,0:T(8,128)S(1)} %fusion.9, pred[256,520]{0,1:T(8,128)(4,1)S(1)} %pad_add_fusion, bf16[8,16,128]{2,0,1:T(8,128)(2,1)S(1)} %bitcast.101, bf16[512,16,128]{2,0,1:T(8,128)(2,1)S(1)} %copy-done.4), kind=kOutput, calls=%fused_computation.14 | convolution fusion | flops 564428800 | bytes 12879872 | tf_op jit(solution)/shard_map/hqk,khd->qhd/dot_general | solution.py:135
  101.2 6.3 %all_to_all.78 = f32[2,16,8,2048]{3,2,1,0:T(8,128)} all-to-all(f32[2,16,8,2048]{3,2,1,0:T(8,128)S(1)} %copy.113), channel_id=1, replica_groups=mesh['cache_0'=2,'cache_1'=8,'cache_2'=2,'dp_0'=8,'dp_1'=2] {'cache_2'}, dimensions={0} | all-to-all | bytes 4194304 | tf_op jit(solution)/shard_map/all_to_all | solution.py:92
  110.4 30.5 %all_to_all.79 = f32[16,8,2048]{2,1,0:T(8,128)S(1)} all-to-all(f32[16,8,2048]{2,1,0:T(8,128)} %reduce_sum.112), channel_id=1, replica_groups=mesh['cache_0'=2,'cache_1'=8,'cache_2'=2,'dp_0'=8,'dp_1'=2] {'cache_0','..., dimensions={0} | all-to-all | bytes 2097152 | tf_op jit(solution)/shard_map/all_to_all | solution.py:93
  142.5 22.1 %all_to_all.80 = bf16[16,8,2048]{2,1,0:T(8,128)(2,1)S(1)} all-to-all(bf16[16,8,2048]{2,1,0:T(8,128)(2,1)S(1)} %broadcast_in_dim.76), channel_id=1, replica_groups=mesh['cache_0'=2,'cache_1'=8,'cache_2'=2,'dp_0'=8,'dp_1'=2] {'cache_0','..., dimensions={0} | all-to-all | bytes 1048576 | tf_op jit(solution)/shard_map/all_to_all | solution.py:60
  164.7 7.1 %all_to_all.81 = bf16[2,16,8,2048]{3,2,1,0:T(8,128)(2,1)S(1)} all-to-all(bf16[2,16,8,2048]{3,2,1,0:T(8,128)(2,1)S(1)} %broadcast_in_dim.77), channel_id=1, replica_groups=mesh['cache_0'=2,'cache_1'=8,'cache_2'=2,'dp_0'=8,'dp_1'=2] {'cache_2'}, dimensions={0} | all-to-all | bytes 2097152 | tf_op jit(solution)/shard_map/all_to_all | solution.py:64
  173.1 10.8 %fusion.8 = bf16[16,128,256]{2,1,0:T(8,128)(2,1)} fusion(f32[16,256,520]{1,2,0:T(8,128)} %copy-done.1, pred[256,520]{0,1:T(8,128)(4,1)S(1)} %copy-done.10, bf16[8,16,128]{2,0,1:T(8,128)(2,1)} %bitcast.96, bf16[512,16,128]{2,0,1:T(8,128)(2,1)S(1)} %fusion.2, bf16[8,16,128]{2,0,1:T(8,128)(2,1)} %bitcast.100, bf16[512,16,128]{2,0,1:T(8,128)(2,1)} %fusion.3, ...), kind=kOutput, calls=%fused_computation.15 | convolution fusion | flops 1125122048 | bytes 15009792 | tf_op jit(solution)/shard_map/hqk,khd->qhd/dot_general | solution.py:135
  185.3 4.5 %all_to_all.82 = bf16[2,16,256,64]{2,3,1,0:T(8,128)(2,1)S(1)} all-to-all(bf16[2,16,256,64]{2,3,1,0:T(8,128)(2,1)S(1)} %copy.117), channel_id=1, replica_groups=mesh['cache_0'=2,'cache_1'=8,'cache_2'=2,'dp_0'=8,'dp_1'=2] {'cache_2'}, dimensions={0} | all-to-all | bytes 2097152 | tf_op jit(solution)/shard_map/all_to_all | solution.py:83
  190.1 19.3 %all_to_all.83 = bf16[16,256,64]{1,2,0:T(8,128)(2,1)S(1)} all-to-all(bf16[16,256,64]{1,2,0:T(8,128)(2,1)S(1)} %reduce_sum.118), channel_id=1, replica_groups=mesh['cache_0'=2,'cache_1'=8,'cache_2'=2,'dp_0'=8,'dp_1'=2] {'cache_0','..., dimensions={0} | all-to-all | bytes 1048576 | tf_op jit(solution)/shard_map/all_to_all | solution.py:85
  210.0 16.4 %all_to_all.84 = bf16[16,128,64]{1,2,0:T(8,128)(2,1)S(1)} all-to-all(bf16[16,128,64]{1,2,0:T(8,128)(2,1)S(1)} %bitcast.90), channel_id=1, replica_groups=mesh['cache_0'=2,'cache_1'=8,'cache_2'=2,'dp_0'=8,'dp_1'=2] {'dp_0','dp_1'}, dimensions={0} | all-to-all | bytes 524288 | tf_op jit(solution)/shard_map/all_to_all | solution.py:119
  228.5 14.1 %all-to-all-start.13 = ((f32[512,1,1]{2,1,0:T(1,128)}), f32[512,1,1]{2,1,0:T(1,128)S(1)}, u32[]{:S(2)}, u32[]{:S(2)}) async-start(f32[512,1,1]{2,1,0:T(1,128)} %broadcast_in_dim.78), calls=%async_computation.13 | async-start | bytes 524288 | tf_op jit(solution)/shard_map/all_to_all | solution.py:31
  243.5 15.4 %all-to-all-done.13 = f32[512,1,1]{2,1,0:T(1,128)S(1)} async-done(((f32[512,1,1]{2,1,0:T(1,128)}), f32[512,1,1]{2,1,0:T(1,128)S(1)}, u32[]{:S(2)}, u32[]{:S(2)}) %all-to-all-start.13) | async-done | bytes 2080 | tf_op jit(solution)/shard_map/all_to_all | solution.py:31
  258.9 5.5 %all-to-all-start.7 = ((bf16[32,2,256]{2,1,0:T(2,128)(2,1)}), bf16[32,2,256]{2,1,0:T(2,128)(2,1)S(1)}, u32[]{:S(2)}, u32[]{:S(2)}) async-start(bf16[32,2,256]{2,1,0:T(2,128)(2,1)} %reshape.174), calls=%async_computation.7 | async-start | bytes 65536 | tf_op jit(solution)/shard_map/all_to_all | solution.py:108
  266.9 6.9 %all-to-all-done.7 = bf16[32,2,256]{2,1,0:T(2,128)(2,1)S(1)} async-done(((bf16[32,2,256]{2,1,0:T(2,128)(2,1)}), bf16[32,2,256]{2,1,0:T(2,128)(2,1)S(1)}, u32[]{:S(2)}, u32[]{:S(2)}) %all-to-all-start.7) | async-done | bytes 32800 | tf_op jit(solution)/shard_map/all_to_all | solution.py:108
  274.6 3.5 %all-to-all-start.14 = ((bf16[16,128,64]{1,2,0:T(8,128)(2,1)}), bf16[16,128,64]{1,2,0:T(8,128)(2,1)S(1)}, u32[]{:S(2)}, u32[]{:S(2)}) async-start(bf16[16,128,64]{1,2,0:T(8,128)(2,1)} %broadcast_in_dim.79), calls=%async_computation.14 | async-start | bytes 524288 | tf_op jit(solution)/shard_map/all_to_all | solution.py:31
  278.9 9.7 %all-to-all-done.14 = bf16[16,128,64]{1,2,0:T(8,128)(2,1)S(1)} async-done(((bf16[16,128,64]{1,2,0:T(8,128)(2,1)}), bf16[16,128,64]{1,2,0:T(8,128)(2,1)S(1)}, u32[]{:S(2)}, u32[]{:S(2)}) %all-to-all-start.14) | async-done | bytes 262176 | tf_op jit(solution)/shard_map/all_to_all | solution.py:31
  (114 shorter events, 46.9 us)
Async XLA Ops:
  0.6 54.3 %copy-start = (bf16[2048,64]{0,1:T(8,128)(2,1)S(1)}, bf16[2048,64]{0,1:T(8,128)(2,1)}, u32[]{:S(2)}) copy-start(bf16[2048,64]{0,1:T(8,128)(2,1)} %param.18) | copy-start | bytes 786436
  3.3 24.0 %all-to-all-start.2 = ((bf16[32,2,512]{2,1,0:T(2,128)(2,1)}), bf16[32,2,512]{2,1,0:T(2,128)(2,1)S(1)}, u32[]{:S(2)}, u32[]{:S(2)}) async-start(bf16[32,2,512]{2,1,0:T(2,128)(2,1)} %reshape.172), calls=%async_computation.2 | async-start | bytes 131072 | tf_op jit(solution)/shard_map/all_to_all | solution.py:100
  28.9 17.8 %all-to-all-start = ((bf16[16,256,64]{1,2,0:T(8,128)(2,1)}), bf16[16,256,64]{1,2,0:T(8,128)(2,1)S(1)}, u32[]{:S(2)}, u32[]{:S(2)}) async-start(bf16[16,256,64]{1,2,0:T(8,128)(2,1)} %broadcast_in_dim.68), calls=%async_computation | async-start | bytes 1048576 | tf_op jit(solution)/shard_map/all_to_all | solution.py:60
  37.2 24.1 %copy-start.21 = (s32[1,256]{1,0:T(1,128)S(1)}, s32[1,256]{1,0:T(1,128)}, u32[]{:S(2)}) copy-start(s32[1,256]{1,0:T(1,128)} %param.29) | copy-start | bytes 3076
  37.2 24.8 %copy-start.19 = (f32[2,8,16]{2,1,0:T(8,128)S(1)}, f32[2,8,16]{2,1,0:T(8,128)}, u32[]{:S(2)}) copy-start(f32[2,8,16]{2,1,0:T(8,128)} %param.24) | copy-start | bytes 3076
  37.2 24.9 %copy-start.20 = (f32[2,8,16]{2,1,0:T(8,128)S(1)}, f32[2,8,16]{2,1,0:T(8,128)}, u32[]{:S(2)}) copy-start(f32[2,8,16]{2,1,0:T(8,128)} %param.25) | copy-start | bytes 3076
  46.8 18.3 %copy-start.2 = (bf16[2,256,2048]{2,1,0:T(8,128)(2,1)S(1)}, bf16[2,256,2048]{2,1,0:T(8,128)(2,1)}, u32[]{:S(2)}) copy-start(bf16[2,256,2048]{2,1,0:T(8,128)(2,1)} %param.22) | copy-start | bytes 6291460
  56.7 19.7 %all-to-all-start.3 = ((bf16[16,256,64]{1,2,0:T(8,128)(2,1)}), bf16[16,256,64]{1,2,0:T(8,128)(2,1)}, u32[]{:S(2)}, u32[]{:S(2)}) async-start(bf16[16,256,64]{1,2,0:T(8,128)(2,1)} %broadcast_in_dim.73), calls=%async_computation.3 | async-start | bytes 1048576 | tf_op jit(solution)/shard_map/all_to_all | solution.py:60
  67.3 18.7 %copy-start.9 = (pred[256,520]{0,1:T(8,128)(4,1)}, pred[256,520]{0,1:T(8,128)(4,1)S(1)}, u32[]{:S(2)}) copy-start(pred[256,520]{0,1:T(8,128)(4,1)S(1)} %pad_add_fusion) | copy-start | bytes 399364
  76.5 8.3 %copy-start.14 = (bf16[8,2048]{1,0:T(8,128)(2,1)S(1)}, bf16[8,2048]{1,0:T(8,128)(2,1)}, u32[]{:S(2)}) copy-start(bf16[8,2048]{1,0:T(8,128)(2,1)} %param.26) | copy-start | bytes 98308
  84.8 4.6 %copy-start.4 = (bf16[512,16,128]{2,0,1:T(8,128)(2,1)S(1)}, bf16[512,16,128]{2,0,1:T(8,128)(2,1)}, u32[]{:S(2)}) copy-start(bf16[512,16,128]{2,0,1:T(8,128)(2,1)} %fusion.3) | copy-start | bytes 6291460
  84.8 4.5 %copy-start.22 = (bf16[8,2048]{1,0:T(8,128)(2,1)S(1)}, bf16[8,2048]{1,0:T(8,128)(2,1)}, u32[]{:S(2)}) copy-start(bf16[8,2048]{1,0:T(8,128)(2,1)} %param.27) | copy-start | bytes 98308
  86.0 3.3 %copy-start.1 = (f32[16,256,520]{1,2,0:T(8,128)}, f32[16,256,520]{1,2,0:T(8,128)S(1)}, u32[]{:S(2)}) copy-start(f32[16,256,520]{1,2,0:T(8,128)S(1)} %fusion.9) | copy-start | bytes 25559044
  107.5 34.0 %copy-start.6 = (bf16[8,2048]{1,0:T(8,128)(2,1)S(1)}, bf16[8,2048]{1,0:T(8,128)(2,1)}, u32[]{:S(2)}) copy-start(bf16[8,2048]{1,0:T(8,128)(2,1)} %unstack.15) | copy-start | bytes 98308
  107.5 34.0 %copy-start.7 = (bf16[8,2048]{1,0:T(8,128)(2,1)S(1)}, bf16[8,2048]{1,0:T(8,128)(2,1)}, u32[]{:S(2)}) copy-start(bf16[8,2048]{1,0:T(8,128)(2,1)} %unstack.13) | copy-start | bytes 98308
  164.6 8.5 %copy-start.10 = (pred[256,520]{0,1:T(8,128)(4,1)S(1)}, pred[256,520]{0,1:T(8,128)(4,1)}, u32[]{:S(2)}) copy-start(pred[256,520]{0,1:T(8,128)(4,1)} %copy-done.9) | copy-start | bytes 399364
  183.9 25.5 %copy-start.8 = (f32[256,64]{0,1:T(8,128)S(1)}, f32[256,64]{0,1:T(8,128)}, u32[]{:S(2)}) copy-start(f32[256,64]{0,1:T(8,128)} %get-tuple-element.49) | copy-start | bytes 196612
  185.2 57.4 %copy-start.13 = (bf16[8,2048]{1,0:T(8,128)(2,1)S(1)}, bf16[8,2048]{1,0:T(8,128)(2,1)}, u32[]{:S(2)}) copy-start(bf16[8,2048]{1,0:T(8,128)(2,1)} %get-tuple-element.47) | copy-start | bytes 98308
  189.8 76.5 %copy-start.15 = (f32[128,64]{0,1:T(8,128)S(1)}, f32[128,64]{0,1:T(8,128)}, u32[]{:S(2)}) copy-start(f32[128,64]{0,1:T(8,128)} %param.19) | copy-start | bytes 98308
  189.8 76.5 %copy-start.16 = (f32[128,64]{0,1:T(8,128)S(1)}, f32[128,64]{0,1:T(8,128)}, u32[]{:S(2)}) copy-start(f32[128,64]{0,1:T(8,128)} %param.20) | copy-start | bytes 98308
  189.8 76.5 %copy-start.17 = (f32[128,64]{0,1:T(8,128)S(1)}, f32[128,64]{0,1:T(8,128)}, u32[]{:S(2)}) copy-start(f32[128,64]{0,1:T(8,128)} %param.21) | copy-start | bytes 98308
  228.5 30.4 %all-to-all-start.13 = ((f32[512,1,1]{2,1,0:T(1,128)}), f32[512,1,1]{2,1,0:T(1,128)S(1)}, u32[]{:S(2)}, u32[]{:S(2)}) async-start(f32[512,1,1]{2,1,0:T(1,128)} %broadcast_in_dim.78), calls=%async_computation.13 | async-start | bytes 524288 | tf_op jit(solution)/shard_map/all_to_all | solution.py:31
  258.9 14.9 %all-to-all-start.7 = ((bf16[32,2,256]{2,1,0:T(2,128)(2,1)}), bf16[32,2,256]{2,1,0:T(2,128)(2,1)S(1)}, u32[]{:S(2)}, u32[]{:S(2)}) async-start(bf16[32,2,256]{2,1,0:T(2,128)(2,1)} %reshape.174), calls=%async_computation.7 | async-start | bytes 65536 | tf_op jit(solution)/shard_map/all_to_all | solution.py:108
  274.6 14.0 %all-to-all-start.14 = ((bf16[16,128,64]{1,2,0:T(8,128)(2,1)}), bf16[16,128,64]{1,2,0:T(8,128)(2,1)S(1)}, u32[]{:S(2)}, u32[]{:S(2)}) async-start(bf16[16,128,64]{1,2,0:T(8,128)(2,1)} %broadcast_in_dim.79), calls=%async_computation.14 | async-start | bytes 524288 | tf_op jit(solution)/shard_map/all_to_all | solution.py:31
  (5 other events, 8.2 us)

commit v6 on v3

--- a/solution.py
+++ b/solution.py
@@ -55,16 +55,24 @@
 CORE = "cache_2"
 
 
+def partner(array):
+    return lax.ppermute(array, CORE, [(0, 1), (1, 0)])
+
+
+def by_core(tiles):
+    first = lax.axis_index(CORE) == 0
+    return (jnp.where(first, tiles[0], tiles[1]), jnp.where(first, tiles[1], tiles[0]))
+
+
 def collect_cache(array, dim):
     chips = lax.axis_size(CHIPS)
     across = lax.all_to_all(
         jnp.broadcast_to(array, (chips, *array.shape)), CHIPS, 0, 0, tiled=True
     )
-    cores = lax.axis_size(CORE)
-    pairs = lax.all_to_all(
-        jnp.broadcast_to(across, (cores, *across.shape)), CORE, 0, 0, tiled=True
-    )
-    tiles = jnp.swapaxes(pairs, 0, 1).reshape(chips * cores, *array.shape)
+    other = partner(across)
+    first = lax.axis_index(CORE) == 0
+    pairs = jnp.stack([jnp.where(first, across, other), jnp.where(first, other, across)])
+    tiles = jnp.swapaxes(pairs, 0, 1).reshape(2 * chips, *array.shape)
     return in_order(tiles, dim)
 
 
@@ -72,7 +80,8 @@
     chips, cores = (lax.axis_size(CHIPS), lax.axis_size(CORE))
     tiles = split_up(array, dim, chips * cores)
     tiles = jnp.swapaxes(tiles.reshape(chips, cores, *tiles.shape[1:]), 0, 1)
-    on_chip = lax.all_to_all(tiles, CORE, 0, 0, tiled=True).sum(axis=0)
+    kept, sent = by_core(tiles)
+    on_chip = kept + partner(sent)
     return lax.all_to_all(on_chip, CHIPS, 0, 0, tiled=True).sum(axis=0)
 
 
@@ -80,9 +89,9 @@
     chips, cores = (lax.axis_size(CHIPS), lax.axis_size(CORE))
     tiles = split_up(array.astype(jnp.bfloat16), dim, chips * cores)
     tiles = jnp.swapaxes(tiles.reshape(chips, cores, *tiles.shape[1:]), 0, 1)
-    on_chip = lax.all_to_all(tiles, CORE, 0, 0, tiled=True)
-    pair_sum = jnp.sum(on_chip.astype(jnp.float32), axis=0).astype(jnp.bfloat16)
-    arrived = lax.all_to_all(pair_sum, CHIPS, 0, 0, tiled=True)
+    kept, sent = by_core(tiles)
+    pair_sum = kept.astype(jnp.float32) + partner(sent).astype(jnp.float32)
+    arrived = lax.all_to_all(pair_sum.astype(jnp.bfloat16), CHIPS, 0, 0, tiled=True)
     return jnp.sum(arrived.astype(jnp.float32), axis=0)
 
 

time: 262 us -> 266 us (1.015)
  blocking collectives: 178 us -> 173 us
  starting transfers between devices: 17.8 us -> 22.7 us
  waiting for transfers between devices: 16.6 us -> 20.3 us
  local copies, waits for them, and re-layouts: 14.7 us -> 17.4 us
    all_to_all x6 -> x1, blocking collectives: 52.7 us -> 19.8 us  [rounded_sum_over_cache(): lax.all_to_all(pair_sum.astype(jnp.bfloat16), CHIPS, 0, 0, tiled=True)]
    all_to_all x1 -> x2, blocking collectives: 16.8 us -> 45.2 us  [collect_cache(): lax.all_to_all(jnp.broadcast_to(array, (chips, *array.shape)), CHIPS, 0,...]
    ppermute x0 -> x5, starting transfers between devices: none -> 18.4 us  [partner(): return lax.ppermute(array, CORE, [(0, 1), (1, 0)])]
    all_to_all x2 -> x1, starting transfers between devices: 17.8 us -> 4.31 us  [collect_cache(): lax.all_to_all(jnp.broadcast_to(array, (chips, *array.shape)), CHIPS, 0,...]
    unnamed x48 -> x40, local copies, waits for them, and re-layouts: 3.29 us -> 8.94 us
    ppermute x0 -> x5, waiting for transfers between devices: none -> 5.48 us  [partner(): return lax.ppermute(array, CORE, [(0, 1), (1, 0)])]
    reduce_sum x2 -> x0, other arithmetic: 3.19 us -> none  [the longest x1 2.89 us: summed_over_cache(): on_chip = lax.all_to_all(tiles, CORE, 0, 0, tiled=True).sum(axis=0)]
    all_to_all x2 -> x1, waiting for transfers between devices: 16.6 us -> 14.9 us  [collect_cache(): lax.all_to_all(jnp.broadcast_to(array, (chips, *array.shape)), CHIPS, 0,...]
  transfers between devices with their start and end apart: 2 -> 6, of which waited for: 2 -> 4; matrix products, arithmetic and copies ran while one was open for 5% -> 7% of each run, Pallas kernels for 0% -> 0%
where the time goes in v6:
time: 266 us; the launch traced here: 264 us
  blocking collectives  173 us (65%)
  starting transfers between devices  22.7 us (9%)
  waiting for transfers between devices  20.3 us (8%)
  local copies, waits for them, and re-layouts  17.4 us (7%)
  other arithmetic  14.7 us (6%)
  matrix products  14.1 us (5%)
    all_to_all x3, blocking collectives, sent_to_all(): return lax.all_to_all(copies, axis, split_axis=0, concat_axis=0, tiled=True)  60.6 us
    all_to_all x2, blocking collectives, collect_cache(): lax.all_to_all(jnp.broadcast_to(array, (chips, *array.shape)), CHIPS, 0,...  45.2 us
    all_to_all x1, blocking collectives, summed_over_cache(): return lax.all_to_all(on_chip, CHIPS, 0, 0, tiled=True).sum(axis=0)  30.9 us
    all_to_all x1, blocking collectives, rounded_sum_over_cache(): lax.all_to_all(pair_sum.astype(jnp.bfloat16), CHIPS, 0, 0, tiled=True)  19.8 us
    ppermute x5, starting transfers between devices, partner(): return lax.ppermute(array, CORE, [(0, 1), (1, 0)])  18.4 us
    all_to_all x1, blocking collectives, sent_and_summed(): tiles = lax.all_to_all(split_up(array, dim, peers), axis, 0, 0, tiled=True)  16.4 us
    all_to_all x1, waiting for transfers between devices, collect_cache(): lax.all_to_all(jnp.broadcast_to(array, (chips, *array.shape)), CHIPS, 0,...  14.9 us
    dot_general x3, matrix products, product(): return jnp.einsum(form, left, right, preferred_element_type=jnp.float32)  13.4 us
  transfers between devices with their start and end apart: 6, of which 4 were waited for; matrix products, arithmetic and copies ran while one was open for 7% of the time, Pallas kernels for 0%

profile of v6, /device:TPU:1, one launch (start us, length us, event | category | flops | bytes accessed | tf_op | source)
XLA Modules:
  0.0 264.0 jit_solution(6122838706488555316)
XLA Ops:
  1.6 28.5 %all_to_all.47 = bf16[16,256,64]{1,2,0:T(8,128)(2,1)S(1)} all-to-all(bf16[16,256,64]{1,2,0:T(8,128)(2,1)S(1)} %broadcast_in_dim.65), channel_id=1, replica_groups=mesh['cache_0'=2,'cache_1'=8,'cache_2'=2,'dp_0'=8,'dp_1'=2] {'cache_0','..., dimensions={0} | all-to-all | bytes 1048576 | tf_op jit(solution)/shard_map/all_to_all | solution.py:69
  30.1 4.8 %collective-permute-start = (bf16[16,256,64]{1,2,0:T(8,128)(2,1)S(1)}, bf16[16,256,64]{1,2,0:T(8,128)(2,1)S(1)}, u32[]{:S(2)}, u32[]{:S(2)}) collective-permute-start(bf16[16,256,64]{1,2,0:T(8,128)(2,1)S(1)} %all_to_all.47), channel_id=1, source_target_pairs={{0,16},{16,0},{1,17},{17,1},{2,18},{18,2},{3,19},{19,3},{4,20},{20... | collective-permute-start | bytes 1572872 | tf_op jit(solution)/shard_map/ppermute | solution.py:59
  39.4 4.1 %copy.120 = f32[64,8,16,128]{3,2,1,0:T(8,128)} copy(bf16[64,8,16,128]{3,1,2,0:T(8,128)(2,1)} %bitcast.122) | data formatting | bytes 6291456
  43.6 2.6 copy.119
  47.6 4.3 %all-to-all-start.1 = ((bf16[16,256,64]{1,2,0:T(8,128)(2,1)}), bf16[16,256,64]{1,2,0:T(8,128)(2,1)}, u32[]{:S(2)}, u32[]{:S(2)}) async-start(bf16[16,256,64]{1,2,0:T(8,128)(2,1)} %broadcast_in_dim.66), calls=%async_computation.1 | async-start | bytes 1048576 | tf_op jit(solution)/shard_map/all_to_all | solution.py:69
  53.1 14.9 %all-to-all-done.1 = bf16[16,256,64]{1,2,0:T(8,128)(2,1)} async-done(((bf16[16,256,64]{1,2,0:T(8,128)(2,1)}), bf16[16,256,64]{1,2,0:T(8,128)(2,1)}, u32[]{:S(2)}, u32[]{:S(2)}) %all-to-all-start.1) | async-done | bytes 524320 | tf_op jit(solution)/shard_map/all_to_all | solution.py:69
  67.9 3.8 %collective-permute-start.1 = (bf16[16,256,64]{1,2,0:T(8,128)(2,1)}, bf16[16,256,64]{1,2,0:T(8,128)(2,1)S(1)}, u32[]{:S(2)}, u32[]{:S(2)}) collective-permute-start(bf16[16,256,64]{1,2,0:T(8,128)(2,1)} %all-to-all-done.1), channel_id=1, source_target_pairs={{0,16},{16,0},{1,17},{17,1},{2,18},{18,2},{3,19},{19,3},{4,20},{20... | collective-permute-start | bytes 1572872 | tf_op jit(solution)/shard_map/ppermute | solution.py:59
  71.8 5.9 %fusion.2 = (bf16[512,16,128]{2,0,1:T(8,128)(2,1)S(1)}, bf16[512,16,128]{2,0,1:T(8,128)(2,1)S(1)}) fusion(f32[512,16,128]{2,1,0:T(8,128)} %bitcast.113, f32[512,16]{0,1:T(8,128)S(1)} %copy-done.6, f32[512,16]{0,1:T(8,128)S(1)} %copy-done.5, f32[512,16,128]{2,1,0:T(8,128)} %bitcast.114), kind=kLoop, calls=%fused_computation.6 | loop fusion | flops 4194304 | bytes 12648448 | tf_op jit(solution)/shard_map/convert_element_type | solution.py:131
  77.7 1.5 select_bitcast_fusion.5
  80.8 3.2 %fusion = f32[16,128,256]{2,1,0:T(8,128)S(1)} fusion(f32[16,256,520]{1,2,0:T(8,128)S(1)} %fusion.8, pred[256,520]{0,1:T(8,128)(4,1)S(1)} %copy-done.4, bf16[8,16,128]{2,0,1:T(8,128)(2,1)S(1)} %bitcast.131, bf16[512,16,128]{2,0,1:T(8,128)(2,1)S(1)} %get-tuple-element.29), kind=kOutput, calls=%fused_computation.3 | convolution fusion | flops 564428800 | bytes 12879872 | tf_op jit(solution)/shard_map/hqk,khd->qhd/dot_general | solution.py:121
  84.2 1.9 collective-permute-start.2
  86.1 2.6 collective-permute-done.2
  89.0 30.9 %all_to_all.48 = f32[16,256,64]{1,2,0:T(8,128)S(1)} all-to-all(f32[16,256,64]{1,2,0:T(8,128)S(1)} %fusion.11), channel_id=1, replica_groups=mesh['cache_0'=2,'cache_1'=8,'cache_2'=2,'dp_0'=8,'dp_1'=2] {'cache_0','..., dimensions={0} | all-to-all | bytes 2097152 | tf_op jit(solution)/shard_map/all_to_all | solution.py:85
  120.2 17.9 %all_to_all.49 = f32[32,1,1024]{2,1,0:T(1,128)} all-to-all(f32[32,1,1024]{2,1,0:T(1,128)S(1)} %broadcast_in_dim.68), channel_id=1, replica_groups=mesh['cache_0'=2,'cache_1'=8,'cache_2'=2,'dp_0'=8,'dp_1'=2] {'cache_0','..., dimensions={0} | all-to-all | bytes 262144 | tf_op jit(solution)/shard_map/all_to_all | solution.py:31
  139.1 1.4 multiply_convert_fusion.5
  140.6 16.8 %all_to_all.50 = bf16[16,256,64]{1,2,0:T(8,128)(2,1)S(1)} all-to-all(bf16[16,256,64]{1,2,0:T(8,128)(2,1)S(1)} %broadcast_in_dim.69), channel_id=1, replica_groups=mesh['cache_0'=2,'cache_1'=8,'cache_2'=2,'dp_0'=8,'dp_1'=2] {'cache_0','..., dimensions={0} | all-to-all | bytes 1048576 | tf_op jit(solution)/shard_map/all_to_all | solution.py:69
  157.3 5.5 %collective-permute-start.3 = (bf16[16,256,64]{1,2,0:T(8,128)(2,1)S(1)}, bf16[16,256,64]{1,2,0:T(8,128)(2,1)S(1)}, u32[]{:S(2)}, u32[]{:S(2)}) collective-permute-start(bf16[16,256,64]{1,2,0:T(8,128)(2,1)S(1)} %all_to_all.50), channel_id=1, source_target_pairs={{0,16},{16,0},{1,17},{17,1},{2,18},{18,2},{3,19},{19,3},{4,20},{20... | collective-permute-start | bytes 1572872 | tf_op jit(solution)/shard_map/ppermute | solution.py:59
  165.5 8.9 %fusion.7 = bf16[16,128,256]{2,1,0:T(8,128)(2,1)} fusion(f32[16,256,520]{1,2,0:T(8,128)} %copy-done.1, pred[256,520]{0,1:T(8,128)(4,1)} %pad_add_fusion, bf16[256,16,128]{0,2,1:T(8,128)(2,1)} %bitcast.124, bf16[8,16,128]{2,0,1:T(8,128)(2,1)S(1)} %bitcast.128, bf16[512,16,128]{2,0,1:T(8,128)(2,1)S(1)} %get-tuple-element.28, ...), kind=kOutput, calls=%fused_computation.14 | convolution fusion | flops 1125122048 | bytes 15009792 | tf_op jit(solution)/shard_map/hqk,khd->qhd/dot_general | solution.py:121
  175.7 2.3 collective-permute-start.4
  178.0 1.5 collective-permute-done.4
  179.8 19.8 %all_to_all.51 = bf16[16,256,64]{1,2,0:T(8,128)(2,1)S(1)} all-to-all(bf16[16,256,64]{1,2,0:T(8,128)(2,1)S(1)} %fusion.12), channel_id=1, replica_groups=mesh['cache_0'=2,'cache_1'=8,'cache_2'=2,'dp_0'=8,'dp_1'=2] {'cache_0','..., dimensions={0} | all-to-all | bytes 1048576 | tf_op jit(solution)/shard_map/all_to_all | solution.py:94
  200.1 16.4 %all_to_all.52 = bf16[16,128,64]{1,2,0:T(8,128)(2,1)S(1)} all-to-all(bf16[16,128,64]{1,2,0:T(8,128)(2,1)S(1)} %bitcast.126), channel_id=1, replica_groups=mesh['cache_0'=2,'cache_1'=8,'cache_2'=2,'dp_0'=8,'dp_1'=2] {'dp_0','dp_1'}, dimensions={0} | all-to-all | bytes 524288 | tf_op jit(solution)/shard_map/all_to_all | solution.py:105
  217.9 30.3 %all_to_all.53 = f32[512,1,1]{2,1,0:T(1,128)S(1)} all-to-all(f32[512,1,1]{2,1,0:T(1,128)S(1)} %broadcast_in_dim.70), channel_id=1, replica_groups=mesh['cache_0'=2,'cache_1'=8,'cache_2'=2,'dp_0'=8,'dp_1'=2] {'cache_0','..., dimensions={0} | all-to-all | bytes 4096 | tf_op jit(solution)/shard_map/all_to_all | solution.py:31
  250.9 12.4 %all_to_all.54 = bf16[16,128,64]{1,2,0:T(8,128)(2,1)S(1)} all-to-all(bf16[16,128,64]{1,2,0:T(8,128)(2,1)S(1)} %broadcast_in_dim.71), channel_id=1, replica_groups=mesh['cache_0'=2,'cache_1'=8,'cache_2'=2,'dp_0'=8,'dp_1'=2] {'dp_0','dp_1'}, dimensions={0} | all-to-all | bytes 524288 | tf_op jit(solution)/shard_map/all_to_all | solution.py:31
  (86 shorter events, 20.0 us)
Async XLA Ops:
  0.6 45.7 %copy-start = (bf16[2048,64]{0,1:T(8,128)(2,1)S(1)}, bf16[2048,64]{0,1:T(8,128)(2,1)}, u32[]{:S(2)}) copy-start(bf16[2048,64]{0,1:T(8,128)(2,1)} %param.18) | copy-start | bytes 786436
  0.6 42.9 %copy-start.2 = (bf16[2,256,2048]{2,1,0:T(8,128)(2,1)S(1)}, bf16[2,256,2048]{2,1,0:T(8,128)(2,1)}, u32[]{:S(2)}) copy-start(bf16[2,256,2048]{2,1,0:T(8,128)(2,1)} %param.23) | copy-start | bytes 6291460
  30.1 16.1 %collective-permute-start = (bf16[16,256,64]{1,2,0:T(8,128)(2,1)S(1)}, bf16[16,256,64]{1,2,0:T(8,128)(2,1)S(1)}, u32[]{:S(2)}, u32[]{:S(2)}) collective-permute-start(bf16[16,256,64]{1,2,0:T(8,128)(2,1)S(1)} %all_to_all.47), channel_id=1, source_target_pairs={{0,16},{16,0},{1,17},{17,1},{2,18},{18,2},{3,19},{19,3},{4,20},{20... | collective-permute-start | bytes 1572872 | tf_op jit(solution)/shard_map/ppermute | solution.py:59
  46.1 5.8 %copy-start.14 = (s32[1,256]{1,0:T(1,128)S(1)}, s32[1,256]{1,0:T(1,128)}, u32[]{:S(2)}) copy-start(s32[1,256]{1,0:T(1,128)} %param.29) | copy-start | bytes 3076
  46.1 5.9 %copy-start.15 = (s32[2]{0:T(128)S(1)}, s32[2]{0:T(128)}, u32[]{:S(2)}) copy-start(s32[2]{0:T(128)} %param.28) | copy-start | bytes 28
  46.1 25.6 %copy-start.5 = (f32[512,16]{0,1:T(8,128)S(1)}, f32[512,16]{0,1:T(8,128)}, u32[]{:S(2)}) copy-start(f32[512,16]{0,1:T(8,128)} %mul.153) | copy-start | bytes 98308
  46.1 25.6 %copy-start.6 = (f32[512,16]{0,1:T(8,128)S(1)}, f32[512,16]{0,1:T(8,128)}, u32[]{:S(2)}) copy-start(f32[512,16]{0,1:T(8,128)} %mul.162) | copy-start | bytes 98308
  47.6 20.3 %all-to-all-start.1 = ((bf16[16,256,64]{1,2,0:T(8,128)(2,1)}), bf16[16,256,64]{1,2,0:T(8,128)(2,1)}, u32[]{:S(2)}, u32[]{:S(2)}) async-start(bf16[16,256,64]{1,2,0:T(8,128)(2,1)} %broadcast_in_dim.66), calls=%async_computation.1 | async-start | bytes 1048576 | tf_op jit(solution)/shard_map/all_to_all | solution.py:69
  67.9 9.8 %collective-permute-start.1 = (bf16[16,256,64]{1,2,0:T(8,128)(2,1)}, bf16[16,256,64]{1,2,0:T(8,128)(2,1)S(1)}, u32[]{:S(2)}, u32[]{:S(2)}) collective-permute-start(bf16[16,256,64]{1,2,0:T(8,128)(2,1)} %all-to-all-done.1), channel_id=1, source_target_pairs={{0,16},{16,0},{1,17},{17,1},{2,18},{18,2},{3,19},{19,3},{4,20},{20... | collective-permute-start | bytes 1572872 | tf_op jit(solution)/shard_map/ppermute | solution.py:59
  77.6 3.1 %copy-start.3 = (bf16[512,16,128]{2,0,1:T(8,128)(2,1)}, bf16[512,16,128]{2,0,1:T(8,128)(2,1)S(1)}, u32[]{:S(2)}) copy-start(bf16[512,16,128]{2,0,1:T(8,128)(2,1)S(1)} %get-tuple-element.29) | copy-start | bytes 6291460
  77.7 1.8 copy-start.9
  79.4 1.3 copy-start.4
  79.5 1.3 copy-start.16
  80.7 3.3 %copy-start.1 = (f32[16,256,520]{1,2,0:T(8,128)}, f32[16,256,520]{1,2,0:T(8,128)S(1)}, u32[]{:S(2)}) copy-start(f32[16,256,520]{1,2,0:T(8,128)S(1)} %fusion.8) | copy-start | bytes 25559044
  84.2 35.9 %copy-start.7 = (bf16[256,64]{0,1:T(8,128)(2,1)S(1)}, bf16[256,64]{0,1:T(8,128)(2,1)}, u32[]{:S(2)}) copy-start(bf16[256,64]{0,1:T(8,128)(2,1)} %param.16) | copy-start | bytes 98308
  84.2 35.9 %copy-start.8 = (bf16[256,64]{0,1:T(8,128)(2,1)S(1)}, bf16[256,64]{0,1:T(8,128)(2,1)}, u32[]{:S(2)}) copy-start(bf16[256,64]{0,1:T(8,128)(2,1)} %param.17) | copy-start | bytes 98308
  84.2 4.6 %collective-permute-start.2 = (f32[16,256,64]{1,2,0:T(8,128)S(1)}, f32[16,256,64]{1,2,0:T(8,128)S(1)}, u32[]{:S(2)}, u32[]{:S(2)}) collective-permute-start(f32[16,256,64]{1,2,0:T(8,128)S(1)} %select_bitcast_fusion), channel_id=1, source_target_pairs={{0,16},{16,0},{1,17},{17,1},{2,18},{18,2},{3,19},{19,3},{4,20},{20... | collective-permute-start | bytes 3145736 | tf_op jit(solution)/shard_map/ppermute | solution.py:59
  140.5 24.9 %copy-start.10 = (bf16[8,2048]{1,0:T(8,128)(2,1)S(1)}, bf16[8,2048]{1,0:T(8,128)(2,1)}, u32[]{:S(2)}) copy-start(bf16[8,2048]{1,0:T(8,128)(2,1)} %param.26) | copy-start | bytes 98308
  140.5 24.9 %copy-start.17 = (bf16[8,2048]{1,0:T(8,128)(2,1)S(1)}, bf16[8,2048]{1,0:T(8,128)(2,1)}, u32[]{:S(2)}) copy-start(bf16[8,2048]{1,0:T(8,128)(2,1)} %param.27) | copy-start | bytes 98308
  157.3 6.9 %collective-permute-start.3 = (bf16[16,256,64]{1,2,0:T(8,128)(2,1)S(1)}, bf16[16,256,64]{1,2,0:T(8,128)(2,1)S(1)}, u32[]{:S(2)}, u32[]{:S(2)}) collective-permute-start(bf16[16,256,64]{1,2,0:T(8,128)(2,1)S(1)} %all_to_all.50), channel_id=1, source_target_pairs={{0,16},{16,0},{1,17},{17,1},{2,18},{18,2},{3,19},{19,3},{4,20},{20... | collective-permute-start | bytes 1572872 | tf_op jit(solution)/shard_map/ppermute | solution.py:59
  175.6 74.5 %copy-start.11 = (f32[128,64]{0,1:T(8,128)S(1)}, f32[128,64]{0,1:T(8,128)}, u32[]{:S(2)}) copy-start(f32[128,64]{0,1:T(8,128)} %param.19) | copy-start | bytes 98308
  175.6 74.5 %copy-start.12 = (f32[128,64]{0,1:T(8,128)S(1)}, f32[128,64]{0,1:T(8,128)}, u32[]{:S(2)}) copy-start(f32[128,64]{0,1:T(8,128)} %param.20) | copy-start | bytes 98308
  175.6 74.5 %copy-start.13 = (f32[128,64]{0,1:T(8,128)S(1)}, f32[128,64]{0,1:T(8,128)}, u32[]{:S(2)}) copy-start(f32[128,64]{0,1:T(8,128)} %param.21) | copy-start | bytes 98308
  175.7 3.8 %collective-permute-start.4 = (bf16[16,256,64]{1,2,0:T(8,128)(2,1)S(1)}, bf16[16,256,64]{1,2,0:T(8,128)(2,1)S(1)}, u32[]{:S(2)}, u32[]{:S(2)}) collective-permute-start(bf16[16,256,64]{1,2,0:T(8,128)(2,1)S(1)} %select_bitcast_fusion.1), channel_id=1, source_target_pairs={{0,16},{16,0},{1,17},{17,1},{2,18},{18,2},{3,19},{19,3},{4,20},{20... | collective-permute-start | bytes 1572872 | tf_op jit(solution)/shard_map/ppermute | solution.py:59

commit v7 on v6

--- a/solution.py
+++ b/solution.py
@@ -62,6 +62,19 @@
 def by_core(tiles):
     first = lax.axis_index(CORE) == 0
     return (jnp.where(first, tiles[0], tiles[1]), jnp.where(first, tiles[1], tiles[0]))
+
+
+def collect_cache_early(array, dim):
+    chips = lax.axis_size(CHIPS)
+    across = lax.all_to_all(
+        jnp.broadcast_to(array, (chips, *array.shape)), CHIPS, 0, 0, tiled=True
+    )
+    cores = lax.axis_size(CORE)
+    pairs = lax.all_to_all(
+        jnp.broadcast_to(across, (cores, *across.shape)), CORE, 0, 0, tiled=True
+    )
+    tiles = jnp.swapaxes(pairs, 0, 1).reshape(chips * cores, *array.shape)
+    return in_order(tiles, dim)
 
 
 def collect_cache(array, dim):
@@ -195,12 +208,12 @@
 ):
     model_width = query_weight.shape[0]
     shard_index = lax.axis_index(CACHE)
-    features = collect_cache(tokens, 1)
+    features = collect_cache_early(tokens, 1)
     query_pre = jnp.dot(features, query_weight, preferred_element_type=jnp.float32) / math.sqrt(
         model_width
     )
     query_block = jax.nn.silu(query_pre).astype(jnp.bfloat16)
-    queries = collect_cache(query_block, 1)
+    queries = collect_cache_early(query_block, 1)
     user_ids = segments[0]
     hist_rows = key_codes.shape[1]
     span_rows = span_keys.shape[0]

time: 266 us -> 256 us (0.962)
  blocking collectives: 173 us -> 159 us
  starting transfers between devices: 22.7 us -> 27.8 us
  local copies, waits for them, and re-layouts: 17.4 us -> 13.4 us
    all_to_all x2 -> x1, blocking collectives: 45.2 us -> 16.8 us  [collect_cache(): lax.all_to_all(jnp.broadcast_to(array, (chips, *array.shape)), CHIPS, 0,...]
    all_to_all x0 -> x2, blocking collectives: none -> 14.3 us  [collect_cache_early(): lax.all_to_all(jnp.broadcast_to(across, (cores, *across.shape)), CORE, 0,...]
    all_to_all x1 -> x2, starting transfers between devices: 4.31 us -> 17.7 us  [collect_cache_early(): lax.all_to_all(jnp.broadcast_to(array, (chips, *array.shape)), CHIPS, 0,...]
    ppermute x5 -> x3, starting transfers between devices: 18.4 us -> 10.1 us  [partner(): return lax.ppermute(array, CORE, [(0, 1), (1, 0)])]
    unnamed x40 -> x48, local copies, waits for them, and re-layouts: 8.94 us -> 3.3 us
    broadcast_in_dim x0 -> x4, local copies, waits for them, and re-layouts: none -> 3.76 us  [the longest x2 2.47 us: collect_cache_early(): jnp.broadcast_to(array, (chips, *array.shape))]
    all_to_all x1 -> x2, waiting for transfers between devices: 14.9 us -> 16.6 us  [collect_cache_early(): lax.all_to_all(jnp.broadcast_to(array, (chips, *array.shape)), CHIPS, 0,...]
    convert_element_type x1 -> x2, other arithmetic: 5.85 us -> 4.7 us  [dequantize(): scaled.astype(jnp.bfloat16).reshape(user_count * row_count, model_width)]
  transfers between devices with their start and end apart: 6 -> 5, of which waited for: 4 -> 5; matrix products, arithmetic and copies ran while one was open for 7% -> 5% of each run, Pallas kernels for 0% -> 0%
where the time goes in v7:
time: 256 us; the launch traced here: 254 us
  blocking collectives  159 us (62%)
  starting transfers between devices  27.8 us (11%)
  waiting for transfers between devices  21.7 us (8%)
  matrix products  16.4 us (6%)
  other arithmetic  13.9 us (5%)
  local copies, waits for them, and re-layouts  13.4 us (5%)
    all_to_all x3, blocking collectives, sent_to_all(): return lax.all_to_all(copies, axis, split_axis=0, concat_axis=0, tiled=True)  60.9 us
    all_to_all x1, blocking collectives, summed_over_cache(): return lax.all_to_all(on_chip, CHIPS, 0, 0, tiled=True).sum(axis=0)  30.6 us
    all_to_all x1, blocking collectives, rounded_sum_over_cache(): lax.all_to_all(pair_sum.astype(jnp.bfloat16), CHIPS, 0, 0, tiled=True)  19.8 us
    all_to_all x2, starting transfers between devices, collect_cache_early(): lax.all_to_all(jnp.broadcast_to(array, (chips, *array.shape)), CHIPS, 0,...  17.7 us
    all_to_all x1, blocking collectives, collect_cache(): lax.all_to_all(jnp.broadcast_to(array, (chips, *array.shape)), CHIPS, 0,...  16.8 us
    all_to_all x2, waiting for transfers between devices, collect_cache_early(): lax.all_to_all(jnp.broadcast_to(array, (chips, *array.shape)), CHIPS, 0,...  16.6 us
    all_to_all x1, blocking collectives, sent_and_summed(): tiles = lax.all_to_all(split_up(array, dim, peers), axis, 0, 0, tiled=True)  16.4 us
    dot_general x3, matrix products, product(): return jnp.einsum(form, left, right, preferred_element_type=jnp.float32)  15 us
  transfers between devices with their start and end apart: 5, of which 5 were waited for; matrix products, arithmetic and copies ran while one was open for 5% of the time, Pallas kernels for 0%

profile of v7, /device:TPU:1, one launch (start us, length us, event | category | flops | bytes accessed | tf_op | source)
XLA Modules:
  0.0 253.6 jit_solution(8753201808401096022)
XLA Ops:
  0.6 1.6 broadcast_in_dim.71
  2.3 13.4 %all-to-all-start = ((bf16[16,256,64]{1,2,0:T(8,128)(2,1)}), bf16[16,256,64]{1,2,0:T(8,128)(2,1)S(1)}, u32[]{:S(2)}, u32[]{:S(2)}) async-start(bf16[16,256,64]{1,2,0:T(8,128)(2,1)} %broadcast_in_dim.71), calls=%async_computation | async-start | bytes 1048576 | tf_op jit(solution)/shard_map/all_to_all | solution.py:69
  17.2 1.5 compare_and_fusion
  18.8 12.2 %all-to-all-done = bf16[16,256,64]{1,2,0:T(8,128)(2,1)S(1)} async-done(((bf16[16,256,64]{1,2,0:T(8,128)(2,1)}), bf16[16,256,64]{1,2,0:T(8,128)(2,1)S(1)}, u32[]{:S(2)}, u32[]{:S(2)}) %all-to-all-start) | async-done | bytes 524320 | tf_op jit(solution)/shard_map/all_to_all | solution.py:69
  31.1 7.2 %all_to_all.57 = bf16[2,16,256,64]{2,3,1,0:T(8,128)(2,1)S(1)} all-to-all(bf16[2,16,256,64]{2,3,1,0:T(8,128)(2,1)S(1)} %broadcast_in_dim.72), channel_id=1, replica_groups=mesh['cache_0'=2,'cache_1'=8,'cache_2'=2,'dp_0'=8,'dp_1'=2] {'cache_2'}, dimensions={0} | all-to-all | bytes 2097152 | tf_op jit(solution)/shard_map/all_to_all | solution.py:73
  40.2 4.3 %all-to-all-start.2 = ((bf16[16,256,64]{1,2,0:T(8,128)(2,1)}), bf16[16,256,64]{1,2,0:T(8,128)(2,1)}, u32[]{:S(2)}, u32[]{:S(2)}) async-start(bf16[16,256,64]{1,2,0:T(8,128)(2,1)} %broadcast_in_dim.73), calls=%async_computation.2 | async-start | bytes 1048576 | tf_op jit(solution)/shard_map/all_to_all | solution.py:69
  50.6 1.8 fusion.2
  52.4 2.9 %fusion.3 = bf16[512,16,128]{2,0,1:T(8,128)(2,1)} fusion(f32[512,16,128]{2,1,0:T(8,128)S(1)} %bitcast.106, f32[512,16]{0,1:T(8,128)S(1)} %copy-done.9), kind=kLoop, calls=%fused_computation.8 | loop fusion | flops 2097152 | bytes 6324224 | tf_op jit(solution)/shard_map/convert_element_type | solution.py:144
  55.3 4.4 %all-to-all-done.2 = bf16[16,256,64]{1,2,0:T(8,128)(2,1)} async-done(((bf16[16,256,64]{1,2,0:T(8,128)(2,1)}), bf16[16,256,64]{1,2,0:T(8,128)(2,1)}, u32[]{:S(2)}, u32[]{:S(2)}) %all-to-all-start.2) | async-done | bytes 524320 | tf_op jit(solution)/shard_map/all_to_all | solution.py:69
  60.8 7.0 %all_to_all.58 = bf16[2,16,256,64]{2,3,1,0:T(8,128)(2,1)S(1)} all-to-all(bf16[2,16,256,64]{2,3,1,0:T(8,128)(2,1)S(1)} %broadcast_in_dim.74), channel_id=1, replica_groups=mesh['cache_0'=2,'cache_1'=8,'cache_2'=2,'dp_0'=8,'dp_1'=2] {'cache_2'}, dimensions={0} | all-to-all | bytes 2097152 | tf_op jit(solution)/shard_map/all_to_all | solution.py:73
  69.6 3.2 %fusion = f32[16,128,256]{2,1,0:T(8,128)S(1)} fusion(f32[16,256,520]{1,2,0:T(8,128)S(1)} %fusion.8, pred[256,520]{0,1:T(8,128)(4,1)S(1)} %pad_add_fusion, bf16[8,16,128]{2,0,1:T(8,128)(2,1)S(1)} %bitcast.125, bf16[512,16,128]{2,0,1:T(8,128)(2,1)S(1)} %copy-done.4), kind=kOutput, calls=%fused_computation.3 | convolution fusion | flops 564428800 | bytes 12879872 | tf_op jit(solution)/shard_map/hqk,khd->qhd/dot_general | solution.py:134
  73.0 2.3 collective-permute-start
  75.3 2.3 collective-permute-done
  77.8 30.6 %all_to_all.59 = f32[16,256,64]{1,2,0:T(8,128)S(1)} all-to-all(f32[16,256,64]{1,2,0:T(8,128)S(1)} %fusion.11), channel_id=1, replica_groups=mesh['cache_0'=2,'cache_1'=8,'cache_2'=2,'dp_0'=8,'dp_1'=2] {'cache_0','..., dimensions={0} | all-to-all | bytes 2097152 | tf_op jit(solution)/shard_map/all_to_all | solution.py:98
  108.7 18.2 %all_to_all.60 = f32[32,1,1024]{2,1,0:T(1,128)} all-to-all(f32[32,1,1024]{2,1,0:T(1,128)S(1)} %broadcast_in_dim.76), channel_id=1, replica_groups=mesh['cache_0'=2,'cache_1'=8,'cache_2'=2,'dp_0'=8,'dp_1'=2] {'cache_0','..., dimensions={0} | all-to-all | bytes 262144 | tf_op jit(solution)/shard_map/all_to_all | solution.py:31
  128.6 16.8 %all_to_all.61 = bf16[16,256,64]{1,2,0:T(8,128)(2,1)S(1)} all-to-all(bf16[16,256,64]{1,2,0:T(8,128)(2,1)S(1)} %broadcast_in_dim.77), channel_id=1, replica_groups=mesh['cache_0'=2,'cache_1'=8,'cache_2'=2,'dp_0'=8,'dp_1'=2] {'cache_0','..., dimensions={0} | all-to-all | bytes 1048576 | tf_op jit(solution)/shard_map/all_to_all | solution.py:82
  145.3 5.5 %collective-permute-start.1 = (bf16[16,256,64]{1,2,0:T(8,128)(2,1)S(1)}, bf16[16,256,64]{1,2,0:T(8,128)(2,1)S(1)}, u32[]{:S(2)}, u32[]{:S(2)}) collective-permute-start(bf16[16,256,64]{1,2,0:T(8,128)(2,1)S(1)} %all_to_all.61), channel_id=1, source_target_pairs={{0,16},{16,0},{1,17},{17,1},{2,18},{18,2},{3,19},{19,3},{4,20},{20... | collective-permute-start | bytes 1572872 | tf_op jit(solution)/shard_map/ppermute | solution.py:59
  153.4 10.5 %fusion.7 = bf16[16,128,256]{2,1,0:T(8,128)(2,1)} fusion(f32[16,256,520]{1,2,0:T(8,128)} %copy-done.1, pred[256,520]{0,1:T(8,128)(4,1)S(1)} %copy-done.8, bf16[256,16,128]{0,2,1:T(8,128)(2,1)} %bitcast.117, bf16[8,16,128]{2,0,1:T(8,128)(2,1)} %bitcast.120, bf16[512,16,128]{2,0,1:T(8,128)(2,1)S(1)} %fusion.2, bf16[8,16,128]{2,0,1:T(8,128)(2,1)} %bitcast.124, ...), kind=kOutput, calls=%fused_computation.14 | convolution fusion | flops 1125122048 | bytes 15009792 | tf_op jit(solution)/shard_map/hqk,khd->qhd/dot_general | solution.py:134
  165.3 2.3 collective-permute-start.2
  167.6 1.5 collective-permute-done.2
  169.4 19.8 %all_to_all.62 = bf16[16,256,64]{1,2,0:T(8,128)(2,1)S(1)} all-to-all(bf16[16,256,64]{1,2,0:T(8,128)(2,1)S(1)} %fusion.12), channel_id=1, replica_groups=mesh['cache_0'=2,'cache_1'=8,'cache_2'=2,'dp_0'=8,'dp_1'=2] {'cache_0','..., dimensions={0} | all-to-all | bytes 1048576 | tf_op jit(solution)/shard_map/all_to_all | solution.py:107
  189.7 16.4 %all_to_all.63 = bf16[16,128,64]{1,2,0:T(8,128)(2,1)S(1)} all-to-all(bf16[16,128,64]{1,2,0:T(8,128)(2,1)S(1)} %bitcast.119), channel_id=1, replica_groups=mesh['cache_0'=2,'cache_1'=8,'cache_2'=2,'dp_0'=8,'dp_1'=2] {'dp_0','dp_1'}, dimensions={0} | all-to-all | bytes 524288 | tf_op jit(solution)/shard_map/all_to_all | solution.py:118
  207.5 30.3 %all_to_all.64 = f32[512,1,1]{2,1,0:T(1,128)S(1)} all-to-all(f32[512,1,1]{2,1,0:T(1,128)S(1)} %broadcast_in_dim.78), channel_id=1, replica_groups=mesh['cache_0'=2,'cache_1'=8,'cache_2'=2,'dp_0'=8,'dp_1'=2] {'cache_0','..., dimensions={0} | all-to-all | bytes 4096 | tf_op jit(solution)/shard_map/all_to_all | solution.py:31
  240.5 12.4 %all_to_all.65 = bf16[16,128,64]{1,2,0:T(8,128)(2,1)S(1)} all-to-all(bf16[16,128,64]{1,2,0:T(8,128)(2,1)S(1)} %broadcast_in_dim.79), channel_id=1, replica_groups=mesh['cache_0'=2,'cache_1'=8,'cache_2'=2,'dp_0'=8,'dp_1'=2] {'dp_0','dp_1'}, dimensions={0} | all-to-all | bytes 524288 | tf_op jit(solution)/shard_map/all_to_all | solution.py:31
  (92 shorter events, 23.3 us)
Async XLA Ops:
  0.6 37.8 %copy-start = (bf16[2048,64]{0,1:T(8,128)(2,1)S(1)}, bf16[2048,64]{0,1:T(8,128)(2,1)}, u32[]{:S(2)}) copy-start(bf16[2048,64]{0,1:T(8,128)(2,1)} %param.18) | copy-start | bytes 786436
  2.3 28.7 %all-to-all-start = ((bf16[16,256,64]{1,2,0:T(8,128)(2,1)}), bf16[16,256,64]{1,2,0:T(8,128)(2,1)S(1)}, u32[]{:S(2)}, u32[]{:S(2)}) async-start(bf16[16,256,64]{1,2,0:T(8,128)(2,1)} %broadcast_in_dim.71), calls=%async_computation | async-start | bytes 1048576 | tf_op jit(solution)/shard_map/all_to_all | solution.py:69
  18.8 25.7 %copy-start.20 = (s32[1,256]{1,0:T(1,128)S(1)}, s32[1,256]{1,0:T(1,128)}, u32[]{:S(2)}) copy-start(s32[1,256]{1,0:T(1,128)} %param.29) | copy-start | bytes 3076
  18.8 26.4 %copy-start.18 = (f32[2,8,16]{2,1,0:T(8,128)S(1)}, f32[2,8,16]{2,1,0:T(8,128)}, u32[]{:S(2)}) copy-start(f32[2,8,16]{2,1,0:T(8,128)} %param.24) | copy-start | bytes 3076
  18.8 26.5 %copy-start.19 = (f32[2,8,16]{2,1,0:T(8,128)S(1)}, f32[2,8,16]{2,1,0:T(8,128)}, u32[]{:S(2)}) copy-start(f32[2,8,16]{2,1,0:T(8,128)} %param.25) | copy-start | bytes 3076
  31.1 17.2 %copy-start.2 = (bf16[2,256,2048]{2,1,0:T(8,128)(2,1)S(1)}, bf16[2,256,2048]{2,1,0:T(8,128)(2,1)}, u32[]{:S(2)}) copy-start(bf16[2,256,2048]{2,1,0:T(8,128)(2,1)} %param.22) | copy-start | bytes 6291460
  40.2 19.4 %all-to-all-start.2 = ((bf16[16,256,64]{1,2,0:T(8,128)(2,1)}), bf16[16,256,64]{1,2,0:T(8,128)(2,1)}, u32[]{:S(2)}, u32[]{:S(2)}) async-start(bf16[16,256,64]{1,2,0:T(8,128)(2,1)} %broadcast_in_dim.73), calls=%async_computation.2 | async-start | bytes 1048576 | tf_op jit(solution)/shard_map/all_to_all | solution.py:69
  48.3 1.6 copy-start.3
  48.9 1.6 copy-start.10
  50.5 1.8 copy-start.9
  50.5 18.7 %copy-start.7 = (pred[256,520]{0,1:T(8,128)(4,1)}, pred[256,520]{0,1:T(8,128)(4,1)S(1)}, u32[]{:S(2)}) copy-start(pred[256,520]{0,1:T(8,128)(4,1)S(1)} %pad_add_fusion) | copy-start | bytes 399364
  59.6 8.3 %copy-start.13 = (bf16[8,2048]{1,0:T(8,128)(2,1)S(1)}, bf16[8,2048]{1,0:T(8,128)(2,1)}, u32[]{:S(2)}) copy-start(bf16[8,2048]{1,0:T(8,128)(2,1)} %param.26) | copy-start | bytes 98308
  68.0 1.6 copy-start.4
  69.3 3.6 %copy-start.1 = (f32[16,256,520]{1,2,0:T(8,128)}, f32[16,256,520]{1,2,0:T(8,128)S(1)}, u32[]{:S(2)}) copy-start(f32[16,256,520]{1,2,0:T(8,128)S(1)} %fusion.8) | copy-start | bytes 25559044
  73.0 35.6 %copy-start.11 = (bf16[256,64]{0,1:T(8,128)(2,1)S(1)}, bf16[256,64]{0,1:T(8,128)(2,1)}, u32[]{:S(2)}) copy-start(bf16[256,64]{0,1:T(8,128)(2,1)} %param.16) | copy-start | bytes 98308
  73.0 35.5 %copy-start.12 = (bf16[256,64]{0,1:T(8,128)(2,1)S(1)}, bf16[256,64]{0,1:T(8,128)(2,1)}, u32[]{:S(2)}) copy-start(bf16[256,64]{0,1:T(8,128)(2,1)} %param.17) | copy-start | bytes 98308
  73.0 4.6 %collective-permute-start = (f32[16,256,64]{1,2,0:T(8,128)S(1)}, f32[16,256,64]{1,2,0:T(8,128)S(1)}, u32[]{:S(2)}, u32[]{:S(2)}) collective-permute-start(f32[16,256,64]{1,2,0:T(8,128)S(1)} %select_bitcast_fusion), channel_id=1, source_target_pairs={{0,16},{16,0},{1,17},{17,1},{2,18},{18,2},{3,19},{19,3},{4,20},{20... | collective-permute-start | bytes 3145736 | tf_op jit(solution)/shard_map/ppermute | solution.py:59
  128.5 24.8 %copy-start.8 = (pred[256,520]{0,1:T(8,128)(4,1)S(1)}, pred[256,520]{0,1:T(8,128)(4,1)}, u32[]{:S(2)}) copy-start(pred[256,520]{0,1:T(8,128)(4,1)} %copy-done.7) | copy-start | bytes 399364
  145.3 6.9 %collective-permute-start.1 = (bf16[16,256,64]{1,2,0:T(8,128)(2,1)S(1)}, bf16[16,256,64]{1,2,0:T(8,128)(2,1)S(1)}, u32[]{:S(2)}, u32[]{:S(2)}) collective-permute-start(bf16[16,256,64]{1,2,0:T(8,128)(2,1)S(1)} %all_to_all.61), channel_id=1, source_target_pairs={{0,16},{16,0},{1,17},{17,1},{2,18},{18,2},{3,19},{19,3},{4,20},{20... | collective-permute-start | bytes 1572872 | tf_op jit(solution)/shard_map/ppermute | solution.py:59
  163.9 25.3 %copy-start.6 = (f32[256,64]{0,1:T(8,128)S(1)}, f32[256,64]{0,1:T(8,128)}, u32[]{:S(2)}) copy-start(f32[256,64]{0,1:T(8,128)} %get-tuple-element.23) | copy-start | bytes 196612
  165.2 74.5 %copy-start.14 = (f32[128,64]{0,1:T(8,128)S(1)}, f32[128,64]{0,1:T(8,128)}, u32[]{:S(2)}) copy-start(f32[128,64]{0,1:T(8,128)} %param.19) | copy-start | bytes 98308
  165.2 74.5 %copy-start.15 = (f32[128,64]{0,1:T(8,128)S(1)}, f32[128,64]{0,1:T(8,128)}, u32[]{:S(2)}) copy-start(f32[128,64]{0,1:T(8,128)} %param.20) | copy-start | bytes 98308
  165.2 74.5 %copy-start.16 = (f32[128,64]{0,1:T(8,128)S(1)}, f32[128,64]{0,1:T(8,128)}, u32[]{:S(2)}) copy-start(f32[128,64]{0,1:T(8,128)} %param.21) | copy-start | bytes 98308
  165.3 3.8 %collective-permute-start.2 = (bf16[16,256,64]{1,2,0:T(8,128)(2,1)S(1)}, bf16[16,256,64]{1,2,0:T(8,128)(2,1)S(1)}, u32[]{:S(2)}, u32[]{:S(2)}) collective-permute-start(bf16[16,256,64]{1,2,0:T(8,128)(2,1)S(1)} %select_bitcast_fusion.1), channel_id=1, source_target_pairs={{0,16},{16,0},{1,17},{17,1},{2,18},{18,2},{3,19},{19,3},{4,20},{20... | collective-permute-start | bytes 1572872 | tf_op jit(solution)/shard_map/ppermute | solution.py:59
  (3 other events, 4.7 us)

commit v8 on v7

--- a/solution.py
+++ b/solution.py
@@ -213,7 +213,7 @@
         model_width
     )
     query_block = jax.nn.silu(query_pre).astype(jnp.bfloat16)
-    queries = collect_cache_early(query_block, 1)
+    queries = collect_cache(query_block, 1)
     user_ids = segments[0]
     hist_rows = key_codes.shape[1]
     span_rows = span_keys.shape[0]

time: 256 us -> 258 us (level)
  blocking collectives: 159 us -> 152 us
  starting transfers between devices: 27.8 us -> 32.2 us
  waiting for transfers between devices: 21.7 us -> 26 us
    all_to_all x0 -> x1, waiting for transfers between devices: none -> 14 us  [collect_cache(): lax.all_to_all(jnp.broadcast_to(array, (chips, *array.shape)), CHIPS, 0,...]
    all_to_all x2 -> x1, waiting for transfers between devices: 16.6 us -> 6.56 us  [collect_cache_early(): lax.all_to_all(jnp.broadcast_to(array, (chips, *array.shape)), CHIPS, 0,...]
    all_to_all x2 -> x1, blocking collectives: 14.3 us -> 7.11 us  [collect_cache_early(): lax.all_to_all(jnp.broadcast_to(across, (cores, *across.shape)), CORE, 0,...]
    unnamed x48 -> x36, local copies, waits for them, and re-layouts: 3.3 us -> 8.33 us
    ppermute x3 -> x4, starting transfers between devices: 10.1 us -> 14.5 us  [partner(): return lax.ppermute(array, CORE, [(0, 1), (1, 0)])]
    all_to_all x0 -> x1, starting transfers between devices: none -> 4.33 us  [collect_cache(): lax.all_to_all(jnp.broadcast_to(array, (chips, *array.shape)), CHIPS, 0,...]
    all_to_all x2 -> x1, starting transfers between devices: 17.7 us -> 13.4 us  [collect_cache_early(): lax.all_to_all(jnp.broadcast_to(array, (chips, *array.shape)), CHIPS, 0,...]
    convert_element_type x2 -> x1, other arithmetic: 4.7 us -> 5.85 us  [dequantize(): scaled.astype(jnp.bfloat16).reshape(user_count * row_count, model_width)]
  transfers between devices with their start and end apart: 5 -> 6, of which waited for: 5 -> 5; matrix products, arithmetic and copies ran while one was open for 5% -> 6% of each run, Pallas kernels for 0% -> 0%
where the time goes in v8:
time: 258 us; the launch traced here: 256 us
  blocking collectives  152 us (59%)
  starting transfers between devices  32.2 us (12%)
  waiting for transfers between devices  26 us (10%)
  local copies, waits for them, and re-layouts  15.8 us (6%)
  other arithmetic  14.5 us (6%)
  matrix products  14.1 us (5%)
    all_to_all x3, blocking collectives, sent_to_all(): return lax.all_to_all(copies, axis, split_axis=0, concat_axis=0, tiled=True)  60.6 us
    all_to_all x1, blocking collectives, summed_over_cache(): return lax.all_to_all(on_chip, CHIPS, 0, 0, tiled=True).sum(axis=0)  30.9 us
    all_to_all x1, blocking collectives, rounded_sum_over_cache(): lax.all_to_all(pair_sum.astype(jnp.bfloat16), CHIPS, 0, 0, tiled=True)  19.8 us
    all_to_all x1, blocking collectives, collect_cache(): lax.all_to_all(jnp.broadcast_to(array, (chips, *array.shape)), CHIPS, 0,...  16.8 us
    all_to_all x1, blocking collectives, sent_and_summed(): tiles = lax.all_to_all(split_up(array, dim, peers), axis, 0, 0, tiled=True)  16.4 us
    ppermute x4, starting transfers between devices, partner(): return lax.ppermute(array, CORE, [(0, 1), (1, 0)])  14.5 us
    all_to_all x1, waiting for transfers between devices, collect_cache(): lax.all_to_all(jnp.broadcast_to(array, (chips, *array.shape)), CHIPS, 0,...  14 us
    all_to_all x1, starting transfers between devices, collect_cache_early(): lax.all_to_all(jnp.broadcast_to(array, (chips, *array.shape)), CHIPS, 0,...  13.4 us
  transfers between devices with their start and end apart: 6, of which 5 were waited for; matrix products, arithmetic and copies ran while one was open for 6% of the time, Pallas kernels for 0%

profile of v8, /device:TPU:1, one launch (start us, length us, event | category | flops | bytes accessed | tf_op | source)
XLA Modules:
  0.0 256.0 jit_solution(366740422302553247)
XLA Ops:
  0.7 1.8 broadcast_in_dim.68
  2.5 13.4 %all-to-all-start = ((bf16[16,256,64]{1,2,0:T(8,128)(2,1)}), bf16[16,256,64]{1,2,0:T(8,128)(2,1)S(1)}, u32[]{:S(2)}, u32[]{:S(2)}) async-start(bf16[16,256,64]{1,2,0:T(8,128)(2,1)} %broadcast_in_dim.68), calls=%async_computation | async-start | bytes 1048576 | tf_op jit(solution)/shard_map/all_to_all | solution.py:69
  17.9 4.1 %copy.119 = f32[64,8,16,128]{3,2,1,0:T(8,128)} copy(bf16[64,8,16,128]{3,1,2,0:T(8,128)(2,1)} %bitcast.119) | data formatting | bytes 6291456
  22.0 2.6 copy.118
  24.6 6.6 %all-to-all-done = bf16[16,256,64]{1,2,0:T(8,128)(2,1)S(1)} async-done(((bf16[16,256,64]{1,2,0:T(8,128)(2,1)}), bf16[16,256,64]{1,2,0:T(8,128)(2,1)S(1)}, u32[]{:S(2)}, u32[]{:S(2)}) %all-to-all-start) | async-done | bytes 524320 | tf_op jit(solution)/shard_map/all_to_all | solution.py:69
  31.3 7.1 %all_to_all.52 = bf16[2,16,256,64]{2,3,1,0:T(8,128)(2,1)S(1)} all-to-all(bf16[2,16,256,64]{2,3,1,0:T(8,128)(2,1)S(1)} %broadcast_in_dim.69), channel_id=1, replica_groups=mesh['cache_0'=2,'cache_1'=8,'cache_2'=2,'dp_0'=8,'dp_1'=2] {'cache_2'}, dimensions={0} | all-to-all | bytes 2097152 | tf_op jit(solution)/shard_map/all_to_all | solution.py:73
  39.7 4.3 %all-to-all-start.2 = ((bf16[16,256,64]{1,2,0:T(8,128)(2,1)}), bf16[16,256,64]{1,2,0:T(8,128)(2,1)}, u32[]{:S(2)}, u32[]{:S(2)}) async-start(bf16[16,256,64]{1,2,0:T(8,128)(2,1)} %broadcast_in_dim.70), calls=%async_computation.2 | async-start | bytes 1048576 | tf_op jit(solution)/shard_map/all_to_all | solution.py:82
  45.2 14.0 %all-to-all-done.2 = bf16[16,256,64]{1,2,0:T(8,128)(2,1)} async-done(((bf16[16,256,64]{1,2,0:T(8,128)(2,1)}), bf16[16,256,64]{1,2,0:T(8,128)(2,1)}, u32[]{:S(2)}, u32[]{:S(2)}) %all-to-all-start.2) | async-done | bytes 524320 | tf_op jit(solution)/shard_map/all_to_all | solution.py:82
  59.2 4.7 %collective-permute-start = (bf16[16,256,64]{1,2,0:T(8,128)(2,1)}, bf16[16,256,64]{1,2,0:T(8,128)(2,1)S(1)}, u32[]{:S(2)}, u32[]{:S(2)}) collective-permute-start(bf16[16,256,64]{1,2,0:T(8,128)(2,1)} %all-to-all-done.2), channel_id=1, source_target_pairs={{0,16},{16,0},{1,17},{17,1},{2,18},{18,2},{3,19},{19,3},{4,20},{20... | collective-permute-start | bytes 1572872 | tf_op jit(solution)/shard_map/ppermute | solution.py:59
  63.9 5.9 %fusion.2 = (bf16[512,16,128]{2,0,1:T(8,128)(2,1)S(1)}, bf16[512,16,128]{2,0,1:T(8,128)(2,1)S(1)}) fusion(f32[512,16,128]{2,1,0:T(8,128)} %bitcast.110, f32[512,16]{0,1:T(8,128)S(1)} %mul.162, f32[512,16]{0,1:T(8,128)S(1)} %mul.153, f32[512,16,128]{2,1,0:T(8,128)} %bitcast.111), kind=kLoop, calls=%fused_computation.6 | loop fusion | flops 4194304 | bytes 12648448 | tf_op jit(solution)/shard_map/convert_element_type | solution.py:144
  69.8 1.5 select_bitcast_fusion.5
  72.8 3.2 %fusion = f32[16,128,256]{2,1,0:T(8,128)S(1)} fusion(f32[16,256,520]{1,2,0:T(8,128)S(1)} %fusion.8, pred[256,520]{0,1:T(8,128)(4,1)S(1)} %copy-done.4, bf16[8,16,128]{2,0,1:T(8,128)(2,1)S(1)} %bitcast.128, bf16[512,16,128]{2,0,1:T(8,128)(2,1)S(1)} %get-tuple-element.27), kind=kOutput, calls=%fused_computation.3 | convolution fusion | flops 564428800 | bytes 12879872 | tf_op jit(solution)/shard_map/hqk,khd->qhd/dot_general | solution.py:134
  76.2 1.9 collective-permute-start.1
  78.1 2.6 %collective-permute-done.1 = f32[16,256,64]{1,2,0:T(8,128)S(1)} collective-permute-done((f32[16,256,64]{1,2,0:T(8,128)S(1)}, f32[16,256,64]{1,2,0:T(8,128)S(1)}, u32[]{:S(2)}, u32[]{:S(2)}) %collective-permute-start.1) | collective-permute-done | bytes 1048608 | tf_op jit(solution)/shard_map/ppermute | solution.py:59
  81.0 30.9 %all_to_all.53 = f32[16,256,64]{1,2,0:T(8,128)S(1)} all-to-all(f32[16,256,64]{1,2,0:T(8,128)S(1)} %fusion.11), channel_id=1, replica_groups=mesh['cache_0'=2,'cache_1'=8,'cache_2'=2,'dp_0'=8,'dp_1'=2] {'cache_0','..., dimensions={0} | all-to-all | bytes 2097152 | tf_op jit(solution)/shard_map/all_to_all | solution.py:98
  112.2 17.9 %all_to_all.54 = f32[32,1,1024]{2,1,0:T(1,128)} all-to-all(f32[32,1,1024]{2,1,0:T(1,128)S(1)} %broadcast_in_dim.72), channel_id=1, replica_groups=mesh['cache_0'=2,'cache_1'=8,'cache_2'=2,'dp_0'=8,'dp_1'=2] {'cache_0','..., dimensions={0} | all-to-all | bytes 262144 | tf_op jit(solution)/shard_map/all_to_all | solution.py:31
  132.5 16.8 %all_to_all.55 = bf16[16,256,64]{1,2,0:T(8,128)(2,1)S(1)} all-to-all(bf16[16,256,64]{1,2,0:T(8,128)(2,1)S(1)} %broadcast_in_dim.73), channel_id=1, replica_groups=mesh['cache_0'=2,'cache_1'=8,'cache_2'=2,'dp_0'=8,'dp_1'=2] {'cache_0','..., dimensions={0} | all-to-all | bytes 1048576 | tf_op jit(solution)/shard_map/all_to_all | solution.py:82
  149.3 5.5 %collective-permute-start.2 = (bf16[16,256,64]{1,2,0:T(8,128)(2,1)S(1)}, bf16[16,256,64]{1,2,0:T(8,128)(2,1)S(1)}, u32[]{:S(2)}, u32[]{:S(2)}) collective-permute-start(bf16[16,256,64]{1,2,0:T(8,128)(2,1)S(1)} %all_to_all.55), channel_id=1, source_target_pairs={{0,16},{16,0},{1,17},{17,1},{2,18},{18,2},{3,19},{19,3},{4,20},{20... | collective-permute-start | bytes 1572872 | tf_op jit(solution)/shard_map/ppermute | solution.py:59
  157.4 8.9 %fusion.7 = bf16[16,128,256]{2,1,0:T(8,128)(2,1)} fusion(f32[16,256,520]{1,2,0:T(8,128)} %copy-done.1, pred[256,520]{0,1:T(8,128)(4,1)} %pad_add_fusion, bf16[256,16,128]{0,2,1:T(8,128)(2,1)} %bitcast.121, bf16[8,16,128]{2,0,1:T(8,128)(2,1)S(1)} %bitcast.125, bf16[512,16,128]{2,0,1:T(8,128)(2,1)S(1)} %get-tuple-element.26, ...), kind=kOutput, calls=%fused_computation.14 | convolution fusion | flops 1125122048 | bytes 15009792 | tf_op jit(solution)/shard_map/hqk,khd->qhd/dot_general | solution.py:134
  167.7 2.3 collective-permute-start.3
  171.7 19.8 %all_to_all.56 = bf16[16,256,64]{1,2,0:T(8,128)(2,1)S(1)} all-to-all(bf16[16,256,64]{1,2,0:T(8,128)(2,1)S(1)} %fusion.12), channel_id=1, replica_groups=mesh['cache_0'=2,'cache_1'=8,'cache_2'=2,'dp_0'=8,'dp_1'=2] {'cache_0','..., dimensions={0} | all-to-all | bytes 1048576 | tf_op jit(solution)/shard_map/all_to_all | solution.py:107
  192.1 16.4 %all_to_all.57 = bf16[16,128,64]{1,2,0:T(8,128)(2,1)S(1)} all-to-all(bf16[16,128,64]{1,2,0:T(8,128)(2,1)S(1)} %bitcast.123), channel_id=1, replica_groups=mesh['cache_0'=2,'cache_1'=8,'cache_2'=2,'dp_0'=8,'dp_1'=2] {'dp_0','dp_1'}, dimensions={0} | all-to-all | bytes 524288 | tf_op jit(solution)/shard_map/all_to_all | solution.py:118
  209.9 30.3 %all_to_all.58 = f32[512,1,1]{2,1,0:T(1,128)S(1)} all-to-all(f32[512,1,1]{2,1,0:T(1,128)S(1)} %broadcast_in_dim.74), channel_id=1, replica_groups=mesh['cache_0'=2,'cache_1'=8,'cache_2'=2,'dp_0'=8,'dp_1'=2] {'cache_0','..., dimensions={0} | all-to-all | bytes 4096 | tf_op jit(solution)/shard_map/all_to_all | solution.py:31
  242.8 12.4 %all_to_all.59 = bf16[16,128,64]{1,2,0:T(8,128)(2,1)S(1)} all-to-all(bf16[16,128,64]{1,2,0:T(8,128)(2,1)S(1)} %broadcast_in_dim.75), channel_id=1, replica_groups=mesh['cache_0'=2,'cache_1'=8,'cache_2'=2,'dp_0'=8,'dp_1'=2] {'dp_0','dp_1'}, dimensions={0} | all-to-all | bytes 524288 | tf_op jit(solution)/shard_map/all_to_all | solution.py:31
  (81 shorter events, 19.3 us)
Async XLA Ops:
  0.6 37.9 %copy-start = (bf16[2048,64]{0,1:T(8,128)(2,1)S(1)}, bf16[2048,64]{0,1:T(8,128)(2,1)}, u32[]{:S(2)}) copy-start(bf16[2048,64]{0,1:T(8,128)(2,1)} %param.18) | copy-start | bytes 786436
  0.6 21.4 %copy-start.2 = (bf16[2,256,2048]{2,1,0:T(8,128)(2,1)S(1)}, bf16[2,256,2048]{2,1,0:T(8,128)(2,1)}, u32[]{:S(2)}) copy-start(bf16[2,256,2048]{2,1,0:T(8,128)(2,1)} %param.23) | copy-start | bytes 6291460
  2.5 28.7 %all-to-all-start = ((bf16[16,256,64]{1,2,0:T(8,128)(2,1)}), bf16[16,256,64]{1,2,0:T(8,128)(2,1)S(1)}, u32[]{:S(2)}, u32[]{:S(2)}) async-start(bf16[16,256,64]{1,2,0:T(8,128)(2,1)} %broadcast_in_dim.68), calls=%async_computation | async-start | bytes 1048576 | tf_op jit(solution)/shard_map/all_to_all | solution.py:69
  24.6 19.5 %copy-start.12 = (s32[1,256]{1,0:T(1,128)S(1)}, s32[1,256]{1,0:T(1,128)}, u32[]{:S(2)}) copy-start(s32[1,256]{1,0:T(1,128)} %param.29) | copy-start | bytes 3076
  24.6 19.6 %copy-start.13 = (s32[2]{0:T(128)S(1)}, s32[2]{0:T(128)}, u32[]{:S(2)}) copy-start(s32[2]{0:T(128)} %param.28) | copy-start | bytes 28
  39.7 19.5 %all-to-all-start.2 = ((bf16[16,256,64]{1,2,0:T(8,128)(2,1)}), bf16[16,256,64]{1,2,0:T(8,128)(2,1)}, u32[]{:S(2)}, u32[]{:S(2)}) async-start(bf16[16,256,64]{1,2,0:T(8,128)(2,1)} %broadcast_in_dim.70), calls=%async_computation.2 | async-start | bytes 1048576 | tf_op jit(solution)/shard_map/all_to_all | solution.py:82
  59.2 10.6 %collective-permute-start = (bf16[16,256,64]{1,2,0:T(8,128)(2,1)}, bf16[16,256,64]{1,2,0:T(8,128)(2,1)S(1)}, u32[]{:S(2)}, u32[]{:S(2)}) collective-permute-start(bf16[16,256,64]{1,2,0:T(8,128)(2,1)} %all-to-all-done.2), channel_id=1, source_target_pairs={{0,16},{16,0},{1,17},{17,1},{2,18},{18,2},{3,19},{19,3},{4,20},{20... | collective-permute-start | bytes 1572872 | tf_op jit(solution)/shard_map/ppermute | solution.py:59
  63.9 7.5 %copy-start.7 = (bf16[8,2048]{1,0:T(8,128)(2,1)S(1)}, bf16[8,2048]{1,0:T(8,128)(2,1)}, u32[]{:S(2)}) copy-start(bf16[8,2048]{1,0:T(8,128)(2,1)} %param.26) | copy-start | bytes 98308
  69.8 3.0 %copy-start.3 = (bf16[512,16,128]{2,0,1:T(8,128)(2,1)}, bf16[512,16,128]{2,0,1:T(8,128)(2,1)S(1)}, u32[]{:S(2)}) copy-start(bf16[512,16,128]{2,0,1:T(8,128)(2,1)S(1)} %get-tuple-element.27) | copy-start | bytes 6291460
  71.5 1.3 copy-start.4
  71.5 1.3 copy-start.14
  72.7 3.3 %copy-start.1 = (f32[16,256,520]{1,2,0:T(8,128)}, f32[16,256,520]{1,2,0:T(8,128)S(1)}, u32[]{:S(2)}) copy-start(f32[16,256,520]{1,2,0:T(8,128)S(1)} %fusion.8) | copy-start | bytes 25559044
  76.2 35.9 %copy-start.5 = (bf16[256,64]{0,1:T(8,128)(2,1)S(1)}, bf16[256,64]{0,1:T(8,128)(2,1)}, u32[]{:S(2)}) copy-start(bf16[256,64]{0,1:T(8,128)(2,1)} %param.16) | copy-start | bytes 98308
  76.2 35.8 %copy-start.6 = (bf16[256,64]{0,1:T(8,128)(2,1)S(1)}, bf16[256,64]{0,1:T(8,128)(2,1)}, u32[]{:S(2)}) copy-start(bf16[256,64]{0,1:T(8,128)(2,1)} %param.17) | copy-start | bytes 98308
  76.2 4.6 %collective-permute-start.1 = (f32[16,256,64]{1,2,0:T(8,128)S(1)}, f32[16,256,64]{1,2,0:T(8,128)S(1)}, u32[]{:S(2)}, u32[]{:S(2)}) collective-permute-start(f32[16,256,64]{1,2,0:T(8,128)S(1)} %select_bitcast_fusion), channel_id=1, source_target_pairs={{0,16},{16,0},{1,17},{17,1},{2,18},{18,2},{3,19},{19,3},{4,20},{20... | collective-permute-start | bytes 3145736 | tf_op jit(solution)/shard_map/ppermute | solution.py:59
  132.5 24.9 %copy-start.8 = (bf16[8,2048]{1,0:T(8,128)(2,1)S(1)}, bf16[8,2048]{1,0:T(8,128)(2,1)}, u32[]{:S(2)}) copy-start(bf16[8,2048]{1,0:T(8,128)(2,1)} %param.26) | copy-start | bytes 98308
  132.5 24.9 %copy-start.15 = (bf16[8,2048]{1,0:T(8,128)(2,1)S(1)}, bf16[8,2048]{1,0:T(8,128)(2,1)}, u32[]{:S(2)}) copy-start(bf16[8,2048]{1,0:T(8,128)(2,1)} %param.27) | copy-start | bytes 98308
  149.3 6.9 %collective-permute-start.2 = (bf16[16,256,64]{1,2,0:T(8,128)(2,1)S(1)}, bf16[16,256,64]{1,2,0:T(8,128)(2,1)S(1)}, u32[]{:S(2)}, u32[]{:S(2)}) collective-permute-start(bf16[16,256,64]{1,2,0:T(8,128)(2,1)S(1)} %all_to_all.55), channel_id=1, source_target_pairs={{0,16},{16,0},{1,17},{17,1},{2,18},{18,2},{3,19},{19,3},{4,20},{20... | collective-permute-start | bytes 1572872 | tf_op jit(solution)/shard_map/ppermute | solution.py:59
  167.6 74.5 %copy-start.9 = (f32[128,64]{0,1:T(8,128)S(1)}, f32[128,64]{0,1:T(8,128)}, u32[]{:S(2)}) copy-start(f32[128,64]{0,1:T(8,128)} %param.19) | copy-start | bytes 98308
  167.6 74.5 %copy-start.10 = (f32[128,64]{0,1:T(8,128)S(1)}, f32[128,64]{0,1:T(8,128)}, u32[]{:S(2)}) copy-start(f32[128,64]{0,1:T(8,128)} %param.20) | copy-start | bytes 98308
  167.6 74.5 %copy-start.11 = (f32[128,64]{0,1:T(8,128)S(1)}, f32[128,64]{0,1:T(8,128)}, u32[]{:S(2)}) copy-start(f32[128,64]{0,1:T(8,128)} %param.21) | copy-start | bytes 98308
  167.7 3.8 %collective-permute-start.3 = (bf16[16,256,64]{1,2,0:T(8,128)(2,1)S(1)}, bf16[16,256,64]{1,2,0:T(8,128)(2,1)S(1)}, u32[]{:S(2)}, u32[]{:S(2)}) collective-permute-start(bf16[16,256,64]{1,2,0:T(8,128)(2,1)S(1)} %select_bitcast_fusion.1), channel_id=1, source_target_pairs={{0,16},{16,0},{1,17},{17,1},{2,18},{18,2},{3,19},{19,3},{4,20},{20... | collective-permute-start | bytes 1572872 | tf_op jit(solution)/shard_map/ppermute | solution.py:59

commit v9 on v7

--- a/solution.py
+++ b/solution.py
@@ -250,7 +250,9 @@
         features, pre_grad, (((0,), (0,)), ((), ())), preferred_element_type=jnp.float32
     ) / math.sqrt(model_width)
     grad_owned = sent_and_summed(weight_part.astype(jnp.bfloat16), DP, 0)
-    square_total = of_everyone(jnp.sum(grad_owned * grad_owned).reshape(1), CACHE_DP)[0]
+    square_pair = jnp.sum(grad_owned * grad_owned).reshape(1)
+    square_pair = square_pair + partner(square_pair)
+    square_total = of_everyone(square_pair, CHIPS + DP)[0]
     grad_level = jnp.sqrt(square_total / (model_width * model_width))
     clip_factor = jnp.minimum(1.0, 0.5 / (grad_level + 1e-06))
     clipped = clip_factor * grad_owned

time: 256 us -> 256 us (level)
  blocking collectives: 159 us -> 152 us
  starting transfers between devices: 27.8 us -> 34 us
    all_to_all x3, blocking collectives: 60.9 us -> 54.3 us  [sent_to_all(): return lax.all_to_all(copies, axis, split_axis=0, concat_axis=0, tiled=True)]
    ppermute x3 -> x4, starting transfers between devices: 10.1 us -> 16.2 us  [partner(): return lax.ppermute(array, CORE, [(0, 1), (1, 0)])]
    ppermute x3 -> x4, waiting for transfers between devices: 5.11 us -> 6.18 us  [partner(): return lax.ppermute(array, CORE, [(0, 1), (1, 0)])]
  transfers between devices with their start and end apart: 5 -> 6, of which waited for: 5 -> 6; matrix products, arithmetic and copies ran while one was open for 5% -> 5% of each run, Pallas kernels for 0% -> 0%
where the time goes in v9:
time: 256 us; the launch traced here: 254 us
  blocking collectives  152 us (59%)
  starting transfers between devices  34 us (13%)
  waiting for transfers between devices  22.7 us (9%)
  matrix products  16.4 us (6%)
  other arithmetic  13.7 us (5%)
  local copies, waits for them, and re-layouts  12.7 us (5%)
  between operations  3.13 us (1%)
    all_to_all x3, blocking collectives, sent_to_all(): return lax.all_to_all(copies, axis, split_axis=0, concat_axis=0, tiled=True)  54.3 us
    all_to_all x1, blocking collectives, summed_over_cache(): return lax.all_to_all(on_chip, CHIPS, 0, 0, tiled=True).sum(axis=0)  30.3 us
    all_to_all x1, blocking collectives, rounded_sum_over_cache(): lax.all_to_all(pair_sum.astype(jnp.bfloat16), CHIPS, 0, 0, tiled=True)  19.8 us
    all_to_all x2, starting transfers between devices, collect_cache_early(): lax.all_to_all(jnp.broadcast_to(array, (chips, *array.shape)), CHIPS, 0,...  17.8 us
    all_to_all x1, blocking collectives, collect_cache(): lax.all_to_all(jnp.broadcast_to(array, (chips, *array.shape)), CHIPS, 0,...  16.8 us
    all_to_all x2, waiting for transfers between devices, collect_cache_early(): lax.all_to_all(jnp.broadcast_to(array, (chips, *array.shape)), CHIPS, 0,...  16.5 us
    all_to_all x1, blocking collectives, sent_and_summed(): tiles = lax.all_to_all(split_up(array, dim, peers), axis, 0, 0, tiled=True)  16.4 us
    ppermute x4, starting transfers between devices, partner(): return lax.ppermute(array, CORE, [(0, 1), (1, 0)])  16.2 us
  transfers between devices with their start and end apart: 6, of which 6 were waited for; matrix products, arithmetic and copies ran while one was open for 5% of the time, Pallas kernels for 0%

profile of v9, /device:TPU:1, one launch (start us, length us, event | category | flops | bytes accessed | tf_op | source)
XLA Modules:
  0.0 254.3 jit_solution(2505219942190801847)
XLA Ops:
  0.6 1.6 broadcast_in_dim.71
  2.3 13.4 %all-to-all-start = ((bf16[16,256,64]{1,2,0:T(8,128)(2,1)}), bf16[16,256,64]{1,2,0:T(8,128)(2,1)S(1)}, u32[]{:S(2)}, u32[]{:S(2)}) async-start(bf16[16,256,64]{1,2,0:T(8,128)(2,1)} %broadcast_in_dim.71), calls=%async_computation | async-start | bytes 1048576 | tf_op jit(solution)/shard_map/all_to_all | solution.py:69
  17.2 1.5 compare_and_fusion
  18.8 12.2 %all-to-all-done = bf16[16,256,64]{1,2,0:T(8,128)(2,1)S(1)} async-done(((bf16[16,256,64]{1,2,0:T(8,128)(2,1)}), bf16[16,256,64]{1,2,0:T(8,128)(2,1)S(1)}, u32[]{:S(2)}, u32[]{:S(2)}) %all-to-all-start) | async-done | bytes 524320 | tf_op jit(solution)/shard_map/all_to_all | solution.py:69
  31.1 7.2 %all_to_all.57 = bf16[2,16,256,64]{2,3,1,0:T(8,128)(2,1)S(1)} all-to-all(bf16[2,16,256,64]{2,3,1,0:T(8,128)(2,1)S(1)} %broadcast_in_dim.72), channel_id=1, replica_groups=mesh['cache_0'=2,'cache_1'=8,'cache_2'=2,'dp_0'=8,'dp_1'=2] {'cache_2'}, dimensions={0} | all-to-all | bytes 2097152 | tf_op jit(solution)/shard_map/all_to_all | solution.py:73
  40.2 4.3 %all-to-all-start.2 = ((bf16[16,256,64]{1,2,0:T(8,128)(2,1)}), bf16[16,256,64]{1,2,0:T(8,128)(2,1)}, u32[]{:S(2)}, u32[]{:S(2)}) async-start(bf16[16,256,64]{1,2,0:T(8,128)(2,1)} %broadcast_in_dim.73), calls=%async_computation.2 | async-start | bytes 1048576 | tf_op jit(solution)/shard_map/all_to_all | solution.py:69
  50.6 1.8 fusion.2
  52.4 3.0 %fusion.3 = bf16[512,16,128]{2,0,1:T(8,128)(2,1)} fusion(f32[512,16,128]{2,1,0:T(8,128)S(1)} %bitcast.108, f32[512,16]{0,1:T(8,128)S(1)} %copy-done.9), kind=kLoop, calls=%fused_computation.8 | loop fusion | flops 2097152 | bytes 6324224 | tf_op jit(solution)/shard_map/convert_element_type | solution.py:144
  55.4 4.3 %all-to-all-done.2 = bf16[16,256,64]{1,2,0:T(8,128)(2,1)} async-done(((bf16[16,256,64]{1,2,0:T(8,128)(2,1)}), bf16[16,256,64]{1,2,0:T(8,128)(2,1)}, u32[]{:S(2)}, u32[]{:S(2)}) %all-to-all-start.2) | async-done | bytes 524320 | tf_op jit(solution)/shard_map/all_to_all | solution.py:69
  60.9 7.0 %all_to_all.58 = bf16[2,16,256,64]{2,3,1,0:T(8,128)(2,1)S(1)} all-to-all(bf16[2,16,256,64]{2,3,1,0:T(8,128)(2,1)S(1)} %broadcast_in_dim.74), channel_id=1, replica_groups=mesh['cache_0'=2,'cache_1'=8,'cache_2'=2,'dp_0'=8,'dp_1'=2] {'cache_2'}, dimensions={0} | all-to-all | bytes 2097152 | tf_op jit(solution)/shard_map/all_to_all | solution.py:73
  69.6 3.2 %fusion = f32[16,128,256]{2,1,0:T(8,128)S(1)} fusion(f32[16,256,520]{1,2,0:T(8,128)S(1)} %fusion.8, pred[256,520]{0,1:T(8,128)(4,1)S(1)} %pad_add_fusion, bf16[8,16,128]{2,0,1:T(8,128)(2,1)S(1)} %bitcast.127, bf16[512,16,128]{2,0,1:T(8,128)(2,1)S(1)} %copy-done.4), kind=kOutput, calls=%fused_computation.3 | convolution fusion | flops 564428800 | bytes 12879872 | tf_op jit(solution)/shard_map/hqk,khd->qhd/dot_general | solution.py:134
  73.1 2.3 collective-permute-start
  75.4 2.3 collective-permute-done
  77.8 30.3 %all_to_all.59 = f32[16,256,64]{1,2,0:T(8,128)S(1)} all-to-all(f32[16,256,64]{1,2,0:T(8,128)S(1)} %fusion.11), channel_id=1, replica_groups=mesh['cache_0'=2,'cache_1'=8,'cache_2'=2,'dp_0'=8,'dp_1'=2] {'cache_0','..., dimensions={0} | all-to-all | bytes 2097152 | tf_op jit(solution)/shard_map/all_to_all | solution.py:98
  108.5 18.5 %all_to_all.60 = f32[32,1,1024]{2,1,0:T(1,128)} all-to-all(f32[32,1,1024]{2,1,0:T(1,128)S(1)} %broadcast_in_dim.76), channel_id=1, replica_groups=mesh['cache_0'=2,'cache_1'=8,'cache_2'=2,'dp_0'=8,'dp_1'=2] {'cache_0','..., dimensions={0} | all-to-all | bytes 262144 | tf_op jit(solution)/shard_map/all_to_all | solution.py:31
  128.6 16.8 %all_to_all.61 = bf16[16,256,64]{1,2,0:T(8,128)(2,1)S(1)} all-to-all(bf16[16,256,64]{1,2,0:T(8,128)(2,1)S(1)} %broadcast_in_dim.77), channel_id=1, replica_groups=mesh['cache_0'=2,'cache_1'=8,'cache_2'=2,'dp_0'=8,'dp_1'=2] {'cache_0','..., dimensions={0} | all-to-all | bytes 1048576 | tf_op jit(solution)/shard_map/all_to_all | solution.py:82
  145.4 5.5 %collective-permute-start.1 = (bf16[16,256,64]{1,2,0:T(8,128)(2,1)S(1)}, bf16[16,256,64]{1,2,0:T(8,128)(2,1)S(1)}, u32[]{:S(2)}, u32[]{:S(2)}) collective-permute-start(bf16[16,256,64]{1,2,0:T(8,128)(2,1)S(1)} %all_to_all.61), channel_id=1, source_target_pairs={{0,16},{16,0},{1,17},{17,1},{2,18},{18,2},{3,19},{19,3},{4,20},{20... | collective-permute-start | bytes 1572872 | tf_op jit(solution)/shard_map/ppermute | solution.py:59
  153.4 10.5 %fusion.7 = bf16[16,128,256]{2,1,0:T(8,128)(2,1)} fusion(f32[16,256,520]{1,2,0:T(8,128)} %copy-done.1, pred[256,520]{0,1:T(8,128)(4,1)S(1)} %copy-done.8, bf16[256,16,128]{0,2,1:T(8,128)(2,1)} %bitcast.119, bf16[8,16,128]{2,0,1:T(8,128)(2,1)} %bitcast.122, bf16[512,16,128]{2,0,1:T(8,128)(2,1)S(1)} %fusion.2, bf16[8,16,128]{2,0,1:T(8,128)(2,1)} %bitcast.126, ...), kind=kOutput, calls=%fused_computation.14 | convolution fusion | flops 1125122048 | bytes 15009792 | tf_op jit(solution)/shard_map/hqk,khd->qhd/dot_general | solution.py:134
  165.4 2.3 collective-permute-start.2
  169.4 19.8 %all_to_all.62 = bf16[16,256,64]{1,2,0:T(8,128)(2,1)S(1)} all-to-all(bf16[16,256,64]{1,2,0:T(8,128)(2,1)S(1)} %fusion.12), channel_id=1, replica_groups=mesh['cache_0'=2,'cache_1'=8,'cache_2'=2,'dp_0'=8,'dp_1'=2] {'cache_0','..., dimensions={0} | all-to-all | bytes 1048576 | tf_op jit(solution)/shard_map/all_to_all | solution.py:107
  189.8 16.4 %all_to_all.63 = bf16[16,128,64]{1,2,0:T(8,128)(2,1)S(1)} all-to-all(bf16[16,128,64]{1,2,0:T(8,128)(2,1)S(1)} %bitcast.121), channel_id=1, replica_groups=mesh['cache_0'=2,'cache_1'=8,'cache_2'=2,'dp_0'=8,'dp_1'=2] {'dp_0','dp_1'}, dimensions={0} | all-to-all | bytes 524288 | tf_op jit(solution)/shard_map/all_to_all | solution.py:118
  206.8 6.1 %collective-permute-start.3 = (f32[1]{0:T(128)}, f32[1]{0:T(128)}, u32[]{:S(2)}, u32[]{:S(2)}) collective-permute-start(f32[1]{0:T(128)} %bitcast.44), channel_id=1, source_target_pairs={{0,16},{16,0},{1,17},{17,1},{2,18},{18,2},{3,19},{19,3},{4,20},{20... | collective-permute-start | bytes 20 | tf_op jit(solution)/shard_map/ppermute | solution.py:59
  215.4 23.6 %all_to_all.64 = f32[256,1,1]{2,1,0:T(1,128)S(1)} all-to-all(f32[256,1,1]{2,1,0:T(1,128)S(1)} %broadcast_in_dim.78), channel_id=1, replica_groups=mesh['cache_0'=2,'cache_1'=8,'cache_2'=2,'dp_0'=8,'dp_1'=2] {'cache_0','..., dimensions={0} | all-to-all | bytes 2048 | tf_op jit(solution)/shard_map/all_to_all | solution.py:31
  241.3 12.3 %all_to_all.65 = bf16[16,128,64]{1,2,0:T(8,128)(2,1)S(1)} all-to-all(bf16[16,128,64]{1,2,0:T(8,128)(2,1)S(1)} %broadcast_in_dim.79), channel_id=1, replica_groups=mesh['cache_0'=2,'cache_1'=8,'cache_2'=2,'dp_0'=8,'dp_1'=2] {'dp_0','dp_1'}, dimensions={0} | all-to-all | bytes 524288 | tf_op jit(solution)/shard_map/all_to_all | solution.py:31
  (94 shorter events, 24.9 us)
Async XLA Ops:
  0.6 37.8 %copy-start = (bf16[2048,64]{0,1:T(8,128)(2,1)S(1)}, bf16[2048,64]{0,1:T(8,128)(2,1)}, u32[]{:S(2)}) copy-start(bf16[2048,64]{0,1:T(8,128)(2,1)} %param.18) | copy-start | bytes 786436
  2.3 28.7 %all-to-all-start = ((bf16[16,256,64]{1,2,0:T(8,128)(2,1)}), bf16[16,256,64]{1,2,0:T(8,128)(2,1)S(1)}, u32[]{:S(2)}, u32[]{:S(2)}) async-start(bf16[16,256,64]{1,2,0:T(8,128)(2,1)} %broadcast_in_dim.71), calls=%async_computation | async-start | bytes 1048576 | tf_op jit(solution)/shard_map/all_to_all | solution.py:69
  18.8 25.8 %copy-start.20 = (s32[1,256]{1,0:T(1,128)S(1)}, s32[1,256]{1,0:T(1,128)}, u32[]{:S(2)}) copy-start(s32[1,256]{1,0:T(1,128)} %param.29) | copy-start | bytes 3076
  18.8 26.5 %copy-start.18 = (f32[2,8,16]{2,1,0:T(8,128)S(1)}, f32[2,8,16]{2,1,0:T(8,128)}, u32[]{:S(2)}) copy-start(f32[2,8,16]{2,1,0:T(8,128)} %param.24) | copy-start | bytes 3076
  18.8 26.5 %copy-start.19 = (f32[2,8,16]{2,1,0:T(8,128)S(1)}, f32[2,8,16]{2,1,0:T(8,128)}, u32[]{:S(2)}) copy-start(f32[2,8,16]{2,1,0:T(8,128)} %param.25) | copy-start | bytes 3076
  31.1 17.3 %copy-start.2 = (bf16[2,256,2048]{2,1,0:T(8,128)(2,1)S(1)}, bf16[2,256,2048]{2,1,0:T(8,128)(2,1)}, u32[]{:S(2)}) copy-start(bf16[2,256,2048]{2,1,0:T(8,128)(2,1)} %param.22) | copy-start | bytes 6291460
  40.2 19.5 %all-to-all-start.2 = ((bf16[16,256,64]{1,2,0:T(8,128)(2,1)}), bf16[16,256,64]{1,2,0:T(8,128)(2,1)}, u32[]{:S(2)}, u32[]{:S(2)}) async-start(bf16[16,256,64]{1,2,0:T(8,128)(2,1)} %broadcast_in_dim.73), calls=%async_computation.2 | async-start | bytes 1048576 | tf_op jit(solution)/shard_map/all_to_all | solution.py:69
  49.0 1.6 copy-start.10
  50.6 1.8 copy-start.9
  50.6 18.7 %copy-start.7 = (pred[256,520]{0,1:T(8,128)(4,1)}, pred[256,520]{0,1:T(8,128)(4,1)S(1)}, u32[]{:S(2)}) copy-start(pred[256,520]{0,1:T(8,128)(4,1)S(1)} %pad_add_fusion) | copy-start | bytes 399364
  59.7 8.3 %copy-start.13 = (bf16[8,2048]{1,0:T(8,128)(2,1)S(1)}, bf16[8,2048]{1,0:T(8,128)(2,1)}, u32[]{:S(2)}) copy-start(bf16[8,2048]{1,0:T(8,128)(2,1)} %param.26) | copy-start | bytes 98308
  68.0 1.6 copy-start.4
  69.3 3.6 %copy-start.1 = (f32[16,256,520]{1,2,0:T(8,128)}, f32[16,256,520]{1,2,0:T(8,128)S(1)}, u32[]{:S(2)}) copy-start(f32[16,256,520]{1,2,0:T(8,128)S(1)} %fusion.8) | copy-start | bytes 25559044
  73.0 35.3 %copy-start.11 = (bf16[256,64]{0,1:T(8,128)(2,1)S(1)}, bf16[256,64]{0,1:T(8,128)(2,1)}, u32[]{:S(2)}) copy-start(bf16[256,64]{0,1:T(8,128)(2,1)} %param.16) | copy-start | bytes 98308
  73.0 35.3 %copy-start.12 = (bf16[256,64]{0,1:T(8,128)(2,1)S(1)}, bf16[256,64]{0,1:T(8,128)(2,1)}, u32[]{:S(2)}) copy-start(bf16[256,64]{0,1:T(8,128)(2,1)} %param.17) | copy-start | bytes 98308
  73.1 4.6 %collective-permute-start = (f32[16,256,64]{1,2,0:T(8,128)S(1)}, f32[16,256,64]{1,2,0:T(8,128)S(1)}, u32[]{:S(2)}, u32[]{:S(2)}) collective-permute-start(f32[16,256,64]{1,2,0:T(8,128)S(1)} %select_bitcast_fusion), channel_id=1, source_target_pairs={{0,16},{16,0},{1,17},{17,1},{2,18},{18,2},{3,19},{19,3},{4,20},{20... | collective-permute-start | bytes 3145736 | tf_op jit(solution)/shard_map/ppermute | solution.py:59
  128.6 24.9 %copy-start.8 = (pred[256,520]{0,1:T(8,128)(4,1)S(1)}, pred[256,520]{0,1:T(8,128)(4,1)}, u32[]{:S(2)}) copy-start(pred[256,520]{0,1:T(8,128)(4,1)} %copy-done.7) | copy-start | bytes 399364
  145.4 6.9 %collective-permute-start.1 = (bf16[16,256,64]{1,2,0:T(8,128)(2,1)S(1)}, bf16[16,256,64]{1,2,0:T(8,128)(2,1)S(1)}, u32[]{:S(2)}, u32[]{:S(2)}) collective-permute-start(bf16[16,256,64]{1,2,0:T(8,128)(2,1)S(1)} %all_to_all.61), channel_id=1, source_target_pairs={{0,16},{16,0},{1,17},{17,1},{2,18},{18,2},{3,19},{19,3},{4,20},{20... | collective-permute-start | bytes 1572872 | tf_op jit(solution)/shard_map/ppermute | solution.py:59
  164.0 25.3 %copy-start.6 = (f32[256,64]{0,1:T(8,128)S(1)}, f32[256,64]{0,1:T(8,128)}, u32[]{:S(2)}) copy-start(f32[256,64]{0,1:T(8,128)} %get-tuple-element.23) | copy-start | bytes 196612
  165.3 75.3 %copy-start.14 = (f32[128,64]{0,1:T(8,128)S(1)}, f32[128,64]{0,1:T(8,128)}, u32[]{:S(2)}) copy-start(f32[128,64]{0,1:T(8,128)} %param.19) | copy-start | bytes 98308
  165.3 75.3 %copy-start.15 = (f32[128,64]{0,1:T(8,128)S(1)}, f32[128,64]{0,1:T(8,128)}, u32[]{:S(2)}) copy-start(f32[128,64]{0,1:T(8,128)} %param.20) | copy-start | bytes 98308
  165.3 75.3 %copy-start.16 = (f32[128,64]{0,1:T(8,128)S(1)}, f32[128,64]{0,1:T(8,128)}, u32[]{:S(2)}) copy-start(f32[128,64]{0,1:T(8,128)} %param.21) | copy-start | bytes 98308
  165.4 3.8 %collective-permute-start.2 = (bf16[16,256,64]{1,2,0:T(8,128)(2,1)S(1)}, bf16[16,256,64]{1,2,0:T(8,128)(2,1)S(1)}, u32[]{:S(2)}, u32[]{:S(2)}) collective-permute-start(bf16[16,256,64]{1,2,0:T(8,128)(2,1)S(1)} %select_bitcast_fusion.1), channel_id=1, source_target_pairs={{0,16},{16,0},{1,17},{17,1},{2,18},{18,2},{3,19},{19,3},{4,20},{20... | collective-permute-start | bytes 1572872 | tf_op jit(solution)/shard_map/ppermute | solution.py:59
  206.8 7.2 %collective-permute-start.3 = (f32[1]{0:T(128)}, f32[1]{0:T(128)}, u32[]{:S(2)}, u32[]{:S(2)}) collective-permute-start(f32[1]{0:T(128)} %bitcast.44), channel_id=1, source_target_pairs={{0,16},{16,0},{1,17},{17,1},{2,18},{18,2},{3,19},{19,3},{4,20},{20... | collective-permute-start | bytes 20 | tf_op jit(solution)/shard_map/ppermute | solution.py:59
  (4 other events, 6.3 us)
